TPU v7x, 512 devices: a whole 4x8x8 slice. The times are simulated.
512 devices in a mesh: dp: 128 (over z, y, core), proto: 4 (over x).
Axes of the slice: x: 4, y: 8, z: 8, core: 2. Of those that a mesh axis runs over, the one named last changes fastest.
Arguments:
- teacher_emb: bfloat16 [32768, 128], P('dp'), may hold values from -64 to 64
- student_emb: bfloat16 [32768, 128], P('dp'), may hold values from -64 to 64
- prototypes: float32 [32768, 128], P(('dp', 'proto')), may hold values from -0.125 to 0.125
Outputs:
- grad_prototypes: float32 [32768, 128], P(('dp', 'proto'))
- grad_student: float32 [32768, 128], P('dp')
All inputs are finite; a program needn't handle non-finite values.
Results may differ from a plain program's by a relative error of at most 0.012.
The roundings to bfloat16 on the way count: a program that leaves them out, or rounds other values in their place, can miss the bound.
Values may be sent and summed in bfloat16 or wider, within the bound.
No kernel may reach another device: no remote copies, remote signals or barrier semaphores. Data moves between devices by JAX's collectives and lax.ppermute only.
A program may use at most 64 MiB of HBM per device.

v0:
```python
import math

import jax
import jax.numpy as jnp
from jax import lax
from jax.sharding import PartitionSpec as P

ITERS = 3


teacher_temp = 0.07
student_temp = 0.1


def joined(array, axis, combine):
    everything = jax.tree.map(lambda part: lax.all_gather(part, axis), array)
    first = jax.tree.map(lambda part: part[0], everything)

    def hop(k, so_far):
        return combine(so_far, jax.tree.map(lambda part: part[k], everything))

    return lax.fori_loop(1, lax.axis_size(axis), hop, first)


def contract_rows(left, right):
    return lax.dot_general(
        left, right, (((1,), (1,)), ((), ())), preferred_element_type=jnp.float32
    )


def combine_stats(first, second):
    teacher_top = jnp.maximum(first[0], second[0])
    student_top = jnp.maximum(first[1], second[1])
    total = first[2] * jnp.exp(first[1] - student_top) + second[2] * jnp.exp(
        second[1] - student_top
    )
    return (teacher_top, student_top, total)


def per_device(teacher_emb, student_emb, prototypes):
    copies = lax.all_gather(prototypes.astype(jnp.bfloat16), "dp", axis=0, tiled=True)
    rows_here = teacher_emb.shape[0]
    width = teacher_emb.shape[1]
    block = math.gcd(rows_here, 128)
    count_blocks = rows_here // block

    def teacher_block(emb):
        logits = contract_rows(emb, copies)
        top = jnp.max(logits, axis=1)
        return (jnp.exp((logits - top[:, None]) / teacher_temp), top)

    base_local, teacher_local = lax.map(
        teacher_block, teacher_emb.reshape(count_blocks, block, width)
    )
    base_local = base_local.reshape(rows_here, -1)
    teacher_local = teacher_local.reshape(rows_here)

    def student_stats(emb):
        logits = contract_rows(emb, copies) / student_temp
        top = jnp.max(logits, axis=1)
        return (top, jnp.sum(jnp.exp(logits - top[:, None]), axis=1))

    student_local, total_local = lax.map(
        student_stats, student_emb.reshape(count_blocks, block, width)
    )
    student_local = student_local.reshape(rows_here)
    total_local = total_local.reshape(rows_here)
    teacher_top, student_top, total = joined(
        (teacher_local, student_local, total_local), "proto", combine_stats
    )
    shift = jnp.exp((teacher_local - teacher_top) / teacher_temp)
    row_scale = jnp.ones((rows_here,), jnp.float32)
    col_scale = jnp.ones((base_local.shape[1],), jnp.float32)
    for step in range(ITERS):
        partial_cols = jnp.dot(row_scale * shift, base_local, precision=lax.Precision.HIGHEST)
        col_scale = 1.0 / lax.psum(partial_cols, "dp")
        partial_rows = shift * jnp.dot(base_local, col_scale, precision=lax.Precision.HIGHEST)
        row_scale = 1.0 / lax.psum(partial_rows, "proto")
    row_factor = row_scale * shift
    student_factor = jnp.exp(student_local - student_top) / total

    def gradient_block(items):
        emb, plan, factor, local_top, soft_factor = items
        logits = contract_rows(emb, copies) / student_temp
        probs = jnp.exp(logits - local_top[:, None]) * soft_factor[:, None]
        targets = factor[:, None] * plan * col_scale[None, :]
        grads = (probs - targets).astype(jnp.bfloat16)
        return (grads, jnp.dot(grads, copies, preferred_element_type=jnp.float32) / student_temp)

    grad_logits, student_terms = lax.map(
        gradient_block,
        (
            student_emb.reshape(count_blocks, block, width),
            base_local.reshape(count_blocks, block, -1),
            row_factor.reshape(count_blocks, block),
            student_local.reshape(count_blocks, block),
            student_factor.reshape(count_blocks, block),
        ),
    )
    grad_logits = grad_logits.reshape(rows_here, -1)
    grad_student = lax.psum(student_terms.reshape(rows_here, width), "proto")
    grad_prototypes = lax.psum_scatter(
        lax.dot_general(
            grad_logits, student_emb, (((0,), (0,)), ((), ())), preferred_element_type=jnp.float32
        )
        / student_temp,
        "dp",
        scatter_dimension=0,
        tiled=True,
    )
    return (grad_prototypes, grad_student)


def solution(mesh):
    in_specs = (P("dp", None), P("dp", None), P(("dp", "proto"), None))
    out_specs = (P(("dp", "proto"), None), P("dp", None))
    return jax.shard_map(
        per_device, mesh=mesh, in_specs=in_specs, out_specs=out_specs, check_vma=False
    )
```

profile of v0, /device:TPU:6, one launch (start us, length us, event | category | flops | bytes accessed | tf_op | source)
XLA Modules:
  0.0 1962.4 jit_solution(7701246373878074425)
XLA Ops:
  7.2 1.4 convert_element_type.6
  8.7 90.5 %all-gather.5.cloned.1.call-done = bf16[8192,128]{1,0:T(8,128)(2,1)} async-done(((bf16[64,128]{1,0:T(8,128)(2,1)}), bf16[8192,128]{1,0:T(8,128)(2,1)}) %all-gather.5.cloned.1.call-update) | async-done | bytes 2097168 | tf_op jit(solution)/shard_map/all_gather | solution.py:41
  99.2 6.5 while.55
  99.2 2.4 fusion.65
  102.4 2.4 fusion.65
  105.7 6.7 all-gather.1
  112.4 10.0 while.56
  112.4 2.4 fusion.67
  114.8 2.6 bitcast_dynamic-update-slice_fusion.4
  117.4 2.4 fusion.67
  119.8 2.6 bitcast_dynamic-update-slice_fusion.4
  122.4 9.2 all-gather
  131.6 7.0 all-gather.2
  138.9 7.4 fusion.29
  146.3 490.9 %psum.49 = f32[8192]{0:T(1024)S(1)} all-reduce(f32[8192]{0:T(1024)S(1)} %bitcast.163), channel_id=1, replica_groups=mesh['dp'=128,'proto'=4] {'dp'}, use_global_device_ids=true, to_apply=%region_9.10 | all-reduce | flops 8192 | bytes 65536 | tf_op jit(solution)/shard_map/psum | solution.py:76
  637.1 8.9 fusion.30
  646.1 9.9 psum.50
  656.0 7.4 fusion.31
  663.4 490.9 %psum.51 = f32[8192]{0:T(1024)S(1)} all-reduce(f32[8192]{0:T(1024)S(1)} %bitcast.160), channel_id=1, replica_groups=mesh['dp'=128,'proto'=4] {'dp'}, use_global_device_ids=true, to_apply=%region_11.12 | all-reduce | flops 8192 | bytes 65536 | tf_op jit(solution)/shard_map/psum | solution.py:76
  1154.3 8.9 fusion.32
  1163.2 7.7 psum.52
  1171.0 7.4 fusion.33
  1178.4 491.1 %psum.53 = f32[8192]{0:T(1024)S(1)} all-reduce(f32[8192]{0:T(1024)S(1)} %bitcast.162), channel_id=1, replica_groups=mesh['dp'=128,'proto'=4] {'dp'}, use_global_device_ids=true, to_apply=%region_13.14 | all-reduce | flops 8192 | bytes 65536 | tf_op jit(solution)/shard_map/psum | solution.py:76
  1669.5 9.0 fusion.34
  1678.5 9.7 psum.54
  1688.3 11.7 while.58
  1688.4 5.1 bitcast_dynamic-update-slice_fusion.5
  1694.2 5.0 bitcast_dynamic-update-slice_fusion.5
  1700.7 5.4 convolution_multiply_fusion.3
  1706.2 39.5 %all-reduce.2.cloned.1.call-done = f32[256,128]{1,0:T(8,128)} async-done(((f32[256,128]{1,0:T(8,128)}), f32[256,128]{1,0:T(8,128)}) %all-reduce.2.cloned.1.call-update) | async-done | bytes 131088 | tf_op jit(solution)/shard_map/psum | solution.py:101
  1745.7 208.7 %reduce-scatter.2.cloned.1.call-done = f32[64,128]{1,0:T(8,128)} async-done(((f32[8192,128]{1,0:T(8,128)}), f32[64,128]{1,0:T(8,128)}) %reduce-scatter.2.cloned.1.call-update) | async-done | bytes 32784 | tf_op jit(solution)/shard_map/reduce_scatter | solution.py:102
  1954.3 1.6 copy.62
  (64 shorter events, 4.6 us)
Async XLA Ops:
  7.2 92.0 %all-gather.5.cloned.1.call-start = ((), (), s32[]{:S(2)}) async-start(), calls=%async_computation.1 | async-start | bytes 2113536 | tf_op jit(solution)/shard_map/all_gather | solution.py:41
  8.6 1737.1 %all-reduce.2.cloned.1.call-start = ((), (), s32[]{:S(2)}) async-start(), calls=%async_computation.3 | async-start | bytes 262144 | tf_op jit(solution)/shard_map/psum | solution.py:101
  99.2 13.2 copy-start.2
  1669.5 18.8 copy-start
  1669.5 18.8 copy-start.1
  1700.0 0.7 copy-start.3
  1700.7 253.7 %reduce-scatter.2.cloned.1.call-start = ((), (), s32[]{:S(2)}) async-start(), calls=%async_computation.2 | async-start | bytes 4227072 | tf_op jit(solution)/shard_map/reduce_scatter | solution.py:102
Sparse Core Ops, SparseCore 0:
  11.7 87.4 all-gather.4
  1700.8 44.8 all-reduce.1
  1751.3 203.0 reduce-scatter.1
where the time goes:
time: 1960 us
  blocking collectives  1520 us (78%)
  waiting for transfers between devices  339 us (17%)
  matrix products  75.6 us (4%)
    psum x3, blocking collectives, per_device(): col_scale = 1.0 / lax.psum(partial_cols, 'dp')  1470 us
    reduce_scatter x1, waiting for transfers between devices, per_device(): lax.psum_scatter(lax.dot_general(grad_logits, student_emb, (((0,), (0,)),...  209 us
    all_gather x1, waiting for transfers between devices, per_device(): lax.all_gather(prototypes.astype(jnp.bfloat16), 'dp', axis=0, tiled=True)  90.5 us
    psum x1, waiting for transfers between devices, per_device(): grad_student = lax.psum(student_terms.reshape(rows_here, width), 'proto')  39.5 us
  transfers between devices with their start and end apart: 3, of which 3 were waited for; matrix products, arithmetic and copies ran while one was open for 0% of the time, Pallas kernels for 0%

commit v1 on v0

--- a/solution.py
+++ b/solution.py
@@ -12,14 +12,46 @@
 student_temp = 0.1
 
 
-def joined(array, axis, combine):
-    everything = jax.tree.map(lambda part: lax.all_gather(part, axis), array)
-    first = jax.tree.map(lambda part: part[0], everything)
+def swap(x, axis, k):
+    n = lax.axis_size(axis)
+    return lax.ppermute(x, axis, [(i, i ^ (1 << k)) for i in range(n)])
 
-    def hop(k, so_far):
-        return combine(so_far, jax.tree.map(lambda part: part[k], everything))
 
-    return lax.fori_loop(1, lax.axis_size(axis), hop, first)
+def bits(axis):
+    return int(math.log2(lax.axis_size(axis)))
+
+
+def tree_butterfly(x, axis, combine):
+    for k in range(bits(axis)):
+        x = combine(x, swap(x, axis, k))
+    return x
+
+
+def sum_over(x, axis):
+    return tree_butterfly(x, axis, lambda a, b: a + b)
+
+
+def gather_blocks(x, axis):
+    me = lax.axis_index(axis)
+    for k in reversed(range(bits(axis))):
+        bit = (me >> k) & 1
+        other = swap(x, axis, k)
+        buf = jnp.zeros((2,) + x.shape, x.dtype)
+        buf = lax.dynamic_update_index_in_dim(buf, x, bit, 0)
+        buf = lax.dynamic_update_index_in_dim(buf, other, 1 - bit, 0)
+        x = buf.reshape((-1,) + x.shape[1:])
+    return x
+
+
+def scatter_blocks(x, axis):
+    me = lax.axis_index(axis)
+    for k in range(bits(axis)):
+        bit = (me >> k) & 1
+        x = x.reshape((2, x.shape[0] // 2) + x.shape[1:])
+        keep = lax.dynamic_index_in_dim(x, bit, 0, keepdims=False)
+        send = lax.dynamic_index_in_dim(x, 1 - bit, 0, keepdims=False)
+        x = keep + swap(send, axis, k)
+    return x
 
 
 def contract_rows(left, right):
@@ -34,11 +66,11 @@
     total = first[2] * jnp.exp(first[1] - student_top) + second[2] * jnp.exp(
         second[1] - student_top
     )
-    return (teacher_top, student_top, total)
+    return jnp.stack([teacher_top, student_top, total])
 
 
 def per_device(teacher_emb, student_emb, prototypes):
-    copies = lax.all_gather(prototypes.astype(jnp.bfloat16), "dp", axis=0, tiled=True)
+    copies = gather_blocks(prototypes.astype(jnp.bfloat16), "dp")
     rows_here = teacher_emb.shape[0]
     width = teacher_emb.shape[1]
     block = math.gcd(rows_here, 128)
@@ -65,17 +97,18 @@
     )
     student_local = student_local.reshape(rows_here)
     total_local = total_local.reshape(rows_here)
-    teacher_top, student_top, total = joined(
-        (teacher_local, student_local, total_local), "proto", combine_stats
+    stats = tree_butterfly(
+        jnp.stack([teacher_local, student_local, total_local]), "proto", combine_stats
     )
+    teacher_top, student_top, total = stats[0], stats[1], stats[2]
     shift = jnp.exp((teacher_local - teacher_top) / teacher_temp)
     row_scale = jnp.ones((rows_here,), jnp.float32)
     col_scale = jnp.ones((base_local.shape[1],), jnp.float32)
     for step in range(ITERS):
         partial_cols = jnp.dot(row_scale * shift, base_local, precision=lax.Precision.HIGHEST)
-        col_scale = 1.0 / lax.psum(partial_cols, "dp")
+        col_scale = 1.0 / sum_over(partial_cols, "dp")
         partial_rows = shift * jnp.dot(base_local, col_scale, precision=lax.Precision.HIGHEST)
-        row_scale = 1.0 / lax.psum(partial_rows, "proto")
+        row_scale = 1.0 / sum_over(partial_rows, "proto")
     row_factor = row_scale * shift
     student_factor = jnp.exp(student_local - student_top) / total
 
@@ -98,15 +131,13 @@
         ),
     )
     grad_logits = grad_logits.reshape(rows_here, -1)
-    grad_student = lax.psum(student_terms.reshape(rows_here, width), "proto")
-    grad_prototypes = lax.psum_scatter(
+    grad_student = sum_over(student_terms.reshape(rows_here, width), "proto")
+    grad_prototypes = scatter_blocks(
         lax.dot_general(
             grad_logits, student_emb, (((0,), (0,)), ((), ())), preferred_element_type=jnp.float32
         )
         / student_temp,
         "dp",
-        scatter_dimension=0,
-        tiled=True,
     )
     return (grad_prototypes, grad_student)
 

time: 1960 us -> 438 us (0.22)
  blocking collectives: 1520 us -> 0 us
  starting transfers between devices: 0.12 us -> 179 us
  waiting for transfers between devices: 339 us -> 185 us
  matrix products: 75.6 us -> 52.5 us
    psum x6 -> x0, blocking collectives: 1500 us -> none  [the longest x3 1470 us: per_device(): col_scale = 1.0 / lax.psum(partial_cols, 'dp')]
    reduce_scatter x1 -> x0, waiting for transfers between devices: 209 us -> none  [per_device(): lax.psum_scatter(lax.dot_general(grad_logits, student_emb, (((0,), (0,)),...]
    ppermute x0 -> x45, waiting for transfers between devices: none -> 185 us  [swap(): return lax.ppermute(x, axis, [(i, i ^ 1 << k) for i in range(n)])]
    ppermute x0 -> x45, starting transfers between devices: none -> 179 us  [swap(): return lax.ppermute(x, axis, [(i, i ^ 1 << k) for i in range(n)])]
    all_gather x1 -> x0, waiting for transfers between devices: 90.5 us -> none  [per_device(): lax.all_gather(prototypes.astype(jnp.bfloat16), 'dp', axis=0, tiled=True)]
    psum x1 -> x0, waiting for transfers between devices: 39.5 us -> none  [per_device(): grad_student = lax.psum(student_terms.reshape(rows_here, width), 'proto')]
    all_gather x3 -> x0, blocking collectives: 22.9 us -> none  [joined(): everything = jax.tree.map(lambda part: lax.all_gather(part, axis), array)]
  transfers between devices with their start and end apart: 3 -> 45, of which waited for: 3 -> 42; matrix products, arithmetic and copies ran while one was open for 0% -> 0% of each run, Pallas kernels for 0% -> 0%
where the time goes in v1:
time: 438 us; the launch traced here: 431 us
  waiting for transfers between devices  185 us (42%)
  starting transfers between devices  179 us (41%)
  matrix products  52.5 us (12%)
  other arithmetic  9.53 us (2%)
    ppermute x45, waiting for transfers between devices, swap(): return lax.ppermute(x, axis, [(i, i ^ 1 << k) for i in range(n)])  185 us
    ppermute x45, starting transfers between devices, swap(): return lax.ppermute(x, axis, [(i, i ^ 1 << k) for i in range(n)])  179 us
    dot_general x3, matrix products, per_device(): jnp.dot(base_local, col_scale, precision=lax.Precision.HIGHEST)  19.7 us
    dot_general x3, matrix products, per_device(): jnp.dot(row_scale * shift, base_local, precision=lax.Precision.HIGHEST)  14.5 us
    dot_general x6, matrix products, contract_rows(): lax.dot_general(left, right, (((1,), (1,)), ((), ())), preferred_element_...  13.3 us
  transfers between devices with their start and end apart: 45, of which 42 were waited for; matrix products, arithmetic and copies ran while one was open for 0% of the time, Pallas kernels for 0%

profile of v1, /device:TPU:6, one launch (start us, length us, event | category | flops | bytes accessed | tf_op | source)
XLA Modules:
  0.0 430.6 jit_solution(929646026211950893)
XLA Ops:
  1.4 10.9 %collective-permute-start = (bf16[64,128]{1,0:T(8,128)(2,1)S(1)}, bf16[64,128]{1,0:T(8,128)(2,1)S(1)}, u32[]{:S(2)}, u32[]{:S(2)}) collective-permute-start(bf16[64,128]{1,0:T(8,128)(2,1)S(1)} %get-tuple-element.160), channel_id=1, source_target_pairs={{0,256},{4,260},{8,264},{12,268},{16,272},{20,276},{24,280},{28,28... | collective-permute-start | bytes 49160 | tf_op jit(solution)/shard_map/ppermute | solution.py:17
  14.1 4.4 %collective-permute-start.1 = (bf16[128,128]{1,0:T(8,128)(2,1)S(1)}, bf16[128,128]{1,0:T(8,128)(2,1)S(1)}, u32[]{:S(2)}, u32[]{:S(2)}) collective-permute-start(bf16[128,128]{1,0:T(8,128)(2,1)S(1)} %bitcast.254), channel_id=1, source_target_pairs={{0,128},{4,132},{8,136},{12,140},{16,144},{20,148},{24,152},{28,15... | collective-permute-start | bytes 98312 | tf_op jit(solution)/shard_map/ppermute | solution.py:17
  26.9 7.7 %collective-permute-start.3 = (bf16[512,128]{1,0:T(8,128)(2,1)S(1)}, bf16[512,128]{1,0:T(8,128)(2,1)S(1)}, u32[]{:S(2)}, u32[]{:S(2)}) collective-permute-start(bf16[512,128]{1,0:T(8,128)(2,1)S(1)} %bitcast.237), channel_id=1, source_target_pairs={{0,32},{4,36},{8,40},{12,44},{16,48},{20,52},{24,56},{28,60},{32,0... | collective-permute-start | bytes 393224 | tf_op jit(solution)/shard_map/ppermute | solution.py:17
  38.6 5.1 %collective-permute-start.4 = (bf16[1024,128]{1,0:T(8,128)(2,1)S(1)}, bf16[1024,128]{1,0:T(8,128)(2,1)S(1)}, u32[]{:S(2)}, u32[]{:S(2)}) collective-permute-start(bf16[1024,128]{1,0:T(8,128)(2,1)S(1)} %bitcast.229), channel_id=1, source_target_pairs={{0,16},{4,20},{8,24},{12,28},{16,0},{20,4},{24,8},{28,12},{32,48},... | collective-permute-start | bytes 786440 | tf_op jit(solution)/shard_map/ppermute | solution.py:17
  43.8 7.3 %collective-permute-done.4 = bf16[1024,128]{1,0:T(8,128)(2,1)S(1)} collective-permute-done((bf16[1024,128]{1,0:T(8,128)(2,1)S(1)}, bf16[1024,128]{1,0:T(8,128)(2,1)S(1)}, u32[]{:S(2)}, u32[]{:S(2)}) %collective-permute-start.4) | collective-permute-done | bytes 262176 | tf_op jit(solution)/shard_map/ppermute | solution.py:17
  53.4 11.1 %collective-permute-done.5 = bf16[2048,128]{1,0:T(8,128)(2,1)S(1)} collective-permute-done((bf16[2048,128]{1,0:T(8,128)(2,1)S(1)}, bf16[2048,128]{1,0:T(8,128)(2,1)S(1)}, u32[]{:S(2)}, u32[]{:S(2)}) %collective-permute-start.5) | collective-permute-done | bytes 524320 | tf_op jit(solution)/shard_map/ppermute | solution.py:17
  70.6 6.9 %while.37 = (s32[]{:T(128)}, f32[2,128,8192]{2,1,0:T(8,128)}, f32[2,128]{1,0:T(2,128)S(1)}, bf16[2,128,128]{2,1,0:T(8,128)(2,1)S(1)}, bf16[8192,128]{1,0:T(8,128)(2,1)S(1)}, /*index=5*/s32[]{:T(128)}, s32[]{:T(128)}) while((s32[]{:T(128)}, f32[2,128,8192]{2,1,0:T(8,128)}, f32[2,128]{1,0:T(2,128)S(1)}, bf16[2,128,128]{2,1,0:T(8,128)(2,1)S(1)}, ...), condition=%wide.region_2.3_spmd, body=%wide.region_0.2_spmd.sunk | while | flops 271581056 | bytes 14715477 | solution.py:84
  93.4 6.5 %fusion.36 = f32[1,8192,1]{1,0,2:T(1,128)S(1)} fusion(f32[2,128,1]{1,2,0:T(1,128)S(1)} %bitcast.274, f32[2,128,8192]{2,1,0:T(8,128)} %get-tuple-element.367), kind=kOutput, calls=%fused_computation.93 | convolution fusion | flops 25165824 | bytes 8422400 | tf_op jit(solution)/shard_map/dot_general | solution.py:108
  110.7 4.9 %collective-permute-done.11 = f32[8192]{0:T(1024)S(1)} collective-permute-done((f32[8192]{0:T(1024)S(1)}, f32[8192]{0:T(1024)S(1)}, u32[]{:S(2)}, u32[]{:S(2)}) %collective-permute-start.11) | collective-permute-done | bytes 32800 | tf_op jit(solution)/shard_map/ppermute | solution.py:17
  115.5 6.7 %collective-permute-start.12 = (f32[8192]{0:T(1024)S(1)}, f32[8192]{0:T(1024)S(1)}, u32[]{:S(2)}, u32[]{:S(2)}) collective-permute-start(f32[8192]{0:T(1024)S(1)} %add.224), channel_id=1, source_target_pairs={{0,32},{4,36},{8,40},{12,44},{16,48},{20,52},{24,56},{28,60},{32,0... | collective-permute-start | bytes 98312 | tf_op jit(solution)/shard_map/ppermute | solution.py:17
  131.3 4.8 %collective-permute-start.14 = (f32[8192]{0:T(1024)S(1)}, f32[8192]{0:T(1024)S(1)}, u32[]{:S(2)}, u32[]{:S(2)}) collective-permute-start(f32[8192]{0:T(1024)S(1)} %add.226), channel_id=1, source_target_pairs={{0,128},{4,132},{8,136},{12,140},{16,144},{20,148},{24,152},{28,15... | collective-permute-start | bytes 98312 | tf_op jit(solution)/shard_map/ppermute | solution.py:17
  138.0 8.1 %collective-permute-start.15 = (f32[8192]{0:T(1024)S(1)}, f32[8192]{0:T(1024)S(1)}, u32[]{:S(2)}, u32[]{:S(2)}) collective-permute-start(f32[8192]{0:T(1024)S(1)} %add.227), channel_id=1, source_target_pairs={{0,256},{4,260},{8,264},{12,268},{16,272},{20,276},{24,280},{28,28... | collective-permute-start | bytes 98312 | tf_op jit(solution)/shard_map/ppermute | solution.py:17
  147.8 6.6 %fusion.37 = f32[1,256]{1,0:T(1,128)S(1)} fusion(f32[256,8192]{1,0:T(8,128)S(1)} %bitcast.211, f32[8192,1]{0,1:T(1,128)S(1)} %bitcast.251), kind=kOutput, calls=%fused_computation.94 | convolution fusion | flops 25165824 | bytes 8422400 | tf_op jit(solution)/shard_map/dot_general | solution.py:110
  181.7 4.8 %collective-permute-done.20 = f32[8192]{0:T(1024)S(1)} collective-permute-done((f32[8192]{0:T(1024)S(1)}, f32[8192]{0:T(1024)S(1)}, u32[]{:S(2)}, u32[]{:S(2)}) %collective-permute-start.20) | collective-permute-done | bytes 32800 | tf_op jit(solution)/shard_map/ppermute | solution.py:17
  186.4 6.4 %collective-permute-start.21 = (f32[8192]{0:T(1024)S(1)}, f32[8192]{0:T(1024)S(1)}, u32[]{:S(2)}, u32[]{:S(2)}) collective-permute-start(f32[8192]{0:T(1024)S(1)} %add.233), channel_id=1, source_target_pairs={{0,32},{4,36},{8,40},{12,44},{16,48},{20,52},{24,56},{28,60},{32,0... | collective-permute-start | bytes 98312 | tf_op jit(solution)/shard_map/ppermute | solution.py:17
  202.0 5.1 %collective-permute-start.23 = (f32[8192]{0:T(1024)S(1)}, f32[8192]{0:T(1024)S(1)}, u32[]{:S(2)}, u32[]{:S(2)}) collective-permute-start(f32[8192]{0:T(1024)S(1)} %add.235), channel_id=1, source_target_pairs={{0,128},{4,132},{8,136},{12,140},{16,144},{20,148},{24,152},{28,15... | collective-permute-start | bytes 98312 | tf_op jit(solution)/shard_map/ppermute | solution.py:17
  209.0 7.9 %collective-permute-start.24 = (f32[8192]{0:T(1024)S(1)}, f32[8192]{0:T(1024)S(1)}, u32[]{:S(2)}, u32[]{:S(2)}) collective-permute-start(f32[8192]{0:T(1024)S(1)} %add.236), channel_id=1, source_target_pairs={{0,256},{4,260},{8,264},{12,268},{16,272},{20,276},{24,280},{28,28... | collective-permute-start | bytes 98312 | tf_op jit(solution)/shard_map/ppermute | solution.py:17
  218.7 6.6 %fusion.39 = f32[1,256]{1,0:T(1,128)S(1)} fusion(f32[256,8192]{1,0:T(8,128)S(1)} %bitcast.213, f32[8192,1]{0,1:T(1,128)S(1)} %bitcast.252), kind=kOutput, calls=%fused_computation.96 | convolution fusion | flops 25165824 | bytes 8422400 | tf_op jit(solution)/shard_map/dot_general | solution.py:110
  252.5 4.8 %collective-permute-done.29 = f32[8192]{0:T(1024)S(1)} collective-permute-done((f32[8192]{0:T(1024)S(1)}, f32[8192]{0:T(1024)S(1)}, u32[]{:S(2)}, u32[]{:S(2)}) %collective-permute-start.29) | collective-permute-done | bytes 32800 | tf_op jit(solution)/shard_map/ppermute | solution.py:17
  257.3 6.2 %collective-permute-start.30 = (f32[8192]{0:T(1024)S(1)}, f32[8192]{0:T(1024)S(1)}, u32[]{:S(2)}, u32[]{:S(2)}) collective-permute-start(f32[8192]{0:T(1024)S(1)} %add.242), channel_id=1, source_target_pairs={{0,32},{4,36},{8,40},{12,44},{16,48},{20,52},{24,56},{28,60},{32,0... | collective-permute-start | bytes 98312 | tf_op jit(solution)/shard_map/ppermute | solution.py:17
  272.9 5.1 %collective-permute-start.32 = (f32[8192]{0:T(1024)S(1)}, f32[8192]{0:T(1024)S(1)}, u32[]{:S(2)}, u32[]{:S(2)}) collective-permute-start(f32[8192]{0:T(1024)S(1)} %add.244), channel_id=1, source_target_pairs={{0,128},{4,132},{8,136},{12,140},{16,144},{20,148},{24,152},{28,15... | collective-permute-start | bytes 98312 | tf_op jit(solution)/shard_map/ppermute | solution.py:17
  279.8 8.8 %collective-permute-start.33 = (f32[8192]{0:T(1024)S(1)}, f32[8192]{0:T(1024)S(1)}, u32[]{:S(2)}, u32[]{:S(2)}) collective-permute-start(f32[8192]{0:T(1024)S(1)} %add.245), channel_id=1, source_target_pairs={{0,256},{4,260},{8,264},{12,268},{16,272},{20,276},{24,280},{28,28... | collective-permute-start | bytes 98312 | tf_op jit(solution)/shard_map/ppermute | solution.py:17
  290.4 6.6 %fusion.41 = f32[1,256]{1,0:T(1,128)S(1)} fusion(f32[256,8192]{1,0:T(8,128)S(1)} %bitcast.215, f32[8192,1]{0,1:T(1,128)S(1)} %bitcast.244), kind=kOutput, calls=%fused_computation.98 | convolution fusion | flops 25165824 | bytes 8422400 | tf_op jit(solution)/shard_map/dot_general | solution.py:110
  309.4 11.7 %while.38 = (s32[]{:T(128)}, bf16[2,128,8192]{2,1,0:T(8,128)(2,1)}, f32[2,128,128]{2,1,0:T(8,128)S(1)}, bf16[2,128,128]{2,1,0:T(8,128)(2,1)S(1)}, bf16[8192,128]...) while((s32[]{:T(128)}, bf16[2,128,8192]{2,1,0:T(8,128)(2,1)}, ...), condition=%wide.region_8.9_spmd, body=%wide.region_7.8_spmd.sunk | while | flops 544227328 | bytes 14816889 | solution.py:123
  309.4 5.0 %bitcast_dynamic-update-slice_fusion.19 = (bf16[2,128,8192]{2,1,0:T(8,128)(2,1)}, bf16[128,8192]{1,0:T(8,128)(2,1)S(1)}) fusion(bf16[2,128,8192]{2,1,0:T(8,128)(2,1)} %get-tuple-element.371, s32[]{:T(128)} %get-tuple-element.370, f32[8192]{0:T(1024)S(1)} %get-tuple-element.390, f32[2,128,8192]{2,1,0:T(8,128)} %get-tuple-element.389, ...), kind=kOutput, calls=%fused_computation.18.clone.1 | convolution fusion | flops 275775488 | bytes 10553856 | tf_op jit(solution)/shard_map/while/body/eval_jaxpr/dot_general | solution.py:58
  315.2 5.1 %bitcast_dynamic-update-slice_fusion.19 = (bf16[2,128,8192]{2,1,0:T(8,128)(2,1)}, bf16[128,8192]{1,0:T(8,128)(2,1)S(1)}) fusion(bf16[2,128,8192]{2,1,0:T(8,128)(2,1)} %get-tuple-element.371, s32[]{:T(128)} %get-tuple-element.370, f32[8192]{0:T(1024)S(1)} %get-tuple-element.390, f32[2,128,8192]{2,1,0:T(8,128)} %get-tuple-element.389, ...), kind=kOutput, calls=%fused_computation.18.clone.1 | convolution fusion | flops 275775488 | bytes 10553856 | tf_op jit(solution)/shard_map/while/body/eval_jaxpr/dot_general | solution.py:58
  333.0 25.2 %collective-permute-done.37 = f32[2048,128]{1,0:T(8,128)S(1)} collective-permute-done((f32[2048,128]{1,0:T(8,128)S(1)}, f32[2048,128]{1,0:T(8,128)S(1)}, u32[]{:S(2)}, u32[]{:S(2)}) %collective-permute-start.37) | collective-permute-done | bytes 1048608 | tf_op jit(solution)/shard_map/ppermute | solution.py:17
  360.3 25.2 %collective-permute-done.38 = f32[1024,128]{1,0:T(8,128)S(1)} collective-permute-done((f32[1024,128]{1,0:T(8,128)S(1)}, f32[1024,128]{1,0:T(8,128)S(1)}, u32[]{:S(2)}, u32[]{:S(2)}) %collective-permute-start.38) | collective-permute-done | bytes 524320 | tf_op jit(solution)/shard_map/ppermute | solution.py:17
  385.6 5.1 %collective-permute-start.39 = (f32[512,128]{1,0:T(8,128)S(1)}, f32[512,128]{1,0:T(8,128)S(1)}, u32[]{:S(2)}, u32[]{:S(2)}) collective-permute-start(f32[512,128]{1,0:T(8,128)S(1)} %dynamic-slice_bitcast_fusion.3), channel_id=1, source_target_pairs={{0,32},{4,36},{8,40},{12,44},{16,48},{20,52},{24,56},{28,60},{32,0... | collective-permute-start | bytes 786440 | tf_op jit(solution)/shard_map/ppermute | solution.py:17
  390.8 13.4 %collective-permute-done.39 = f32[512,128]{1,0:T(8,128)S(1)} collective-permute-done((f32[512,128]{1,0:T(8,128)S(1)}, f32[512,128]{1,0:T(8,128)S(1)}, u32[]{:S(2)}, u32[]{:S(2)}) %collective-permute-start.39) | collective-permute-done | bytes 262176 | tf_op jit(solution)/shard_map/ppermute | solution.py:17
  411.6 5.0 %collective-permute-start.41 = (f32[128,128]{1,0:T(8,128)S(1)}, f32[128,128]{1,0:T(8,128)S(1)}, u32[]{:S(2)}, u32[]{:S(2)}) collective-permute-start(f32[128,128]{1,0:T(8,128)S(1)} %dynamic-slice_bitcast_fusion.5), channel_id=1, source_target_pairs={{0,128},{4,132},{8,136},{12,140},{16,144},{20,148},{24,152},{28,15... | collective-permute-start | bytes 196616 | tf_op jit(solution)/shard_map/ppermute | solution.py:17
  420.0 7.3 %collective-permute-start.42 = (f32[64,128]{1,0:T(8,128)S(1)}, f32[64,128]{1,0:T(8,128)S(1)}, u32[]{:S(2)}, u32[]{:S(2)}) collective-permute-start(f32[64,128]{1,0:T(8,128)S(1)} %dynamic-slice_bitcast_fusion.6), channel_id=1, source_target_pairs={{0,256},{4,260},{8,264},{12,268},{16,272},{20,276},{24,280},{28,28... | collective-permute-start | bytes 98312 | tf_op jit(solution)/shard_map/ppermute | solution.py:17
  (175 shorter events, 194.5 us)
Async XLA Ops:
  1.4 12.6 %collective-permute-start = (bf16[64,128]{1,0:T(8,128)(2,1)S(1)}, bf16[64,128]{1,0:T(8,128)(2,1)S(1)}, u32[]{:S(2)}, u32[]{:S(2)}) collective-permute-start(bf16[64,128]{1,0:T(8,128)(2,1)S(1)} %get-tuple-element.160), channel_id=1, source_target_pairs={{0,256},{4,260},{8,264},{12,268},{16,272},{20,276},{24,280},{28,28... | collective-permute-start | bytes 49160 | tf_op jit(solution)/shard_map/ppermute | solution.py:17
  14.1 6.7 %collective-permute-start.1 = (bf16[128,128]{1,0:T(8,128)(2,1)S(1)}, bf16[128,128]{1,0:T(8,128)(2,1)S(1)}, u32[]{:S(2)}, u32[]{:S(2)}) collective-permute-start(bf16[128,128]{1,0:T(8,128)(2,1)S(1)} %bitcast.254), channel_id=1, source_target_pairs={{0,128},{4,132},{8,136},{12,140},{16,144},{20,148},{24,152},{28,15... | collective-permute-start | bytes 98312 | tf_op jit(solution)/shard_map/ppermute | solution.py:17
  20.8 6.1 %collective-permute-start.2 = (bf16[256,128]{1,0:T(8,128)(2,1)S(1)}, bf16[256,128]{1,0:T(8,128)(2,1)S(1)}, u32[]{:S(2)}, u32[]{:S(2)}) collective-permute-start(bf16[256,128]{1,0:T(8,128)(2,1)S(1)} %bitcast.242), channel_id=1, source_target_pairs={{0,64},{4,68},{8,72},{12,76},{16,80},{20,84},{24,88},{28,92},{32,9... | collective-permute-start | bytes 196616 | tf_op jit(solution)/shard_map/ppermute | solution.py:17
  26.9 11.7 %collective-permute-start.3 = (bf16[512,128]{1,0:T(8,128)(2,1)S(1)}, bf16[512,128]{1,0:T(8,128)(2,1)S(1)}, u32[]{:S(2)}, u32[]{:S(2)}) collective-permute-start(bf16[512,128]{1,0:T(8,128)(2,1)S(1)} %bitcast.237), channel_id=1, source_target_pairs={{0,32},{4,36},{8,40},{12,44},{16,48},{20,52},{24,56},{28,60},{32,0... | collective-permute-start | bytes 393224 | tf_op jit(solution)/shard_map/ppermute | solution.py:17
  38.6 12.5 %collective-permute-start.4 = (bf16[1024,128]{1,0:T(8,128)(2,1)S(1)}, bf16[1024,128]{1,0:T(8,128)(2,1)S(1)}, u32[]{:S(2)}, u32[]{:S(2)}) collective-permute-start(bf16[1024,128]{1,0:T(8,128)(2,1)S(1)} %bitcast.229), channel_id=1, source_target_pairs={{0,16},{4,20},{8,24},{12,28},{16,0},{20,4},{24,8},{28,12},{32,48},... | collective-permute-start | bytes 786440 | tf_op jit(solution)/shard_map/ppermute | solution.py:17
  51.2 13.3 %collective-permute-start.5 = (bf16[2048,128]{1,0:T(8,128)(2,1)S(1)}, bf16[2048,128]{1,0:T(8,128)(2,1)S(1)}, u32[]{:S(2)}, u32[]{:S(2)}) collective-permute-start(bf16[2048,128]{1,0:T(8,128)(2,1)S(1)} %bitcast.227), channel_id=1, source_target_pairs={{0,8},{4,12},{8,0},{12,4},{16,24},{20,28},{24,16},{28,20},{32,40},... | collective-permute-start | bytes 1572872 | tf_op jit(solution)/shard_map/ppermute | solution.py:17
  86.3 7.0 %collective-permute-start.8 = (f32[3,256]{1,0:T(4,128)S(1)}, f32[3,256]{1,0:T(4,128)S(1)}, u32[]{:S(2)}, u32[]{:S(2)}) collective-permute-start(f32[3,256]{1,0:T(4,128)S(1)} %pad_maximum_fusion.1), channel_id=1, source_target_pairs={{0,2},{1,3},{2,0},{3,1},{4,6},{5,7},{6,4},{7,5},{8,10},{9,11},{10,... | collective-permute-start | bytes 9224 | tf_op jit(solution)/shard_map/ppermute | solution.py:17
  102.9 5.8 %collective-permute-start.10 = (f32[8192]{0:T(1024)S(1)}, f32[8192]{0:T(1024)S(1)}, u32[]{:S(2)}, u32[]{:S(2)}) collective-permute-start(f32[8192]{0:T(1024)S(1)} %add.222), channel_id=1, source_target_pairs={{0,8},{4,12},{8,0},{12,4},{16,24},{20,28},{24,16},{28,20},{32,40},... | collective-permute-start | bytes 98312 | tf_op jit(solution)/shard_map/ppermute | solution.py:17
  108.8 6.8 %collective-permute-start.11 = (f32[8192]{0:T(1024)S(1)}, f32[8192]{0:T(1024)S(1)}, u32[]{:S(2)}, u32[]{:S(2)}) collective-permute-start(f32[8192]{0:T(1024)S(1)} %add.223), channel_id=1, source_target_pairs={{0,16},{4,20},{8,24},{12,28},{16,0},{20,4},{24,8},{28,12},{32,48},... | collective-permute-start | bytes 98312 | tf_op jit(solution)/shard_map/ppermute | solution.py:17
  115.5 10.0 %collective-permute-start.12 = (f32[8192]{0:T(1024)S(1)}, f32[8192]{0:T(1024)S(1)}, u32[]{:S(2)}, u32[]{:S(2)}) collective-permute-start(f32[8192]{0:T(1024)S(1)} %add.224), channel_id=1, source_target_pairs={{0,32},{4,36},{8,40},{12,44},{16,48},{20,52},{24,56},{28,60},{32,0... | collective-permute-start | bytes 98312 | tf_op jit(solution)/shard_map/ppermute | solution.py:17
  131.3 6.7 %collective-permute-start.14 = (f32[8192]{0:T(1024)S(1)}, f32[8192]{0:T(1024)S(1)}, u32[]{:S(2)}, u32[]{:S(2)}) collective-permute-start(f32[8192]{0:T(1024)S(1)} %add.226), channel_id=1, source_target_pairs={{0,128},{4,132},{8,136},{12,140},{16,144},{20,148},{24,152},{28,15... | collective-permute-start | bytes 98312 | tf_op jit(solution)/shard_map/ppermute | solution.py:17
  138.0 9.7 %collective-permute-start.15 = (f32[8192]{0:T(1024)S(1)}, f32[8192]{0:T(1024)S(1)}, u32[]{:S(2)}, u32[]{:S(2)}) collective-permute-start(f32[8192]{0:T(1024)S(1)} %add.227), channel_id=1, source_target_pairs={{0,256},{4,260},{8,264},{12,268},{16,272},{20,276},{24,280},{28,28... | collective-permute-start | bytes 98312 | tf_op jit(solution)/shard_map/ppermute | solution.py:17
  159.8 7.0 %collective-permute-start.17 = (f32[256]{0:T(256)S(1)}, f32[256]{0:T(256)S(1)}, u32[]{:S(2)}, u32[]{:S(2)}) collective-permute-start(f32[256]{0:T(256)S(1)} %add.229), channel_id=1, source_target_pairs={{0,2},{1,3},{2,0},{3,1},{4,6},{5,7},{6,4},{7,5},{8,10},{9,11},{10,... | collective-permute-start | bytes 3080 | tf_op jit(solution)/shard_map/ppermute | solution.py:17
  179.7 6.7 %collective-permute-start.20 = (f32[8192]{0:T(1024)S(1)}, f32[8192]{0:T(1024)S(1)}, u32[]{:S(2)}, u32[]{:S(2)}) collective-permute-start(f32[8192]{0:T(1024)S(1)} %add.232), channel_id=1, source_target_pairs={{0,16},{4,20},{8,24},{12,28},{16,0},{20,4},{24,8},{28,12},{32,48},... | collective-permute-start | bytes 98312 | tf_op jit(solution)/shard_map/ppermute | solution.py:17
  186.4 9.7 %collective-permute-start.21 = (f32[8192]{0:T(1024)S(1)}, f32[8192]{0:T(1024)S(1)}, u32[]{:S(2)}, u32[]{:S(2)}) collective-permute-start(f32[8192]{0:T(1024)S(1)} %add.233), channel_id=1, source_target_pairs={{0,32},{4,36},{8,40},{12,44},{16,48},{20,52},{24,56},{28,60},{32,0... | collective-permute-start | bytes 98312 | tf_op jit(solution)/shard_map/ppermute | solution.py:17
  202.0 7.0 %collective-permute-start.23 = (f32[8192]{0:T(1024)S(1)}, f32[8192]{0:T(1024)S(1)}, u32[]{:S(2)}, u32[]{:S(2)}) collective-permute-start(f32[8192]{0:T(1024)S(1)} %add.235), channel_id=1, source_target_pairs={{0,128},{4,132},{8,136},{12,140},{16,144},{20,148},{24,152},{28,15... | collective-permute-start | bytes 98312 | tf_op jit(solution)/shard_map/ppermute | solution.py:17
  209.0 9.7 %collective-permute-start.24 = (f32[8192]{0:T(1024)S(1)}, f32[8192]{0:T(1024)S(1)}, u32[]{:S(2)}, u32[]{:S(2)}) collective-permute-start(f32[8192]{0:T(1024)S(1)} %add.236), channel_id=1, source_target_pairs={{0,256},{4,260},{8,264},{12,268},{16,272},{20,276},{24,280},{28,28... | collective-permute-start | bytes 98312 | tf_op jit(solution)/shard_map/ppermute | solution.py:17
  230.7 7.0 %collective-permute-start.26 = (f32[256]{0:T(256)S(1)}, f32[256]{0:T(256)S(1)}, u32[]{:S(2)}, u32[]{:S(2)}) collective-permute-start(f32[256]{0:T(256)S(1)} %add.238), channel_id=1, source_target_pairs={{0,2},{1,3},{2,0},{3,1},{4,6},{5,7},{6,4},{7,5},{8,10},{9,11},{10,... | collective-permute-start | bytes 3080 | tf_op jit(solution)/shard_map/ppermute | solution.py:17
  250.6 6.7 %collective-permute-start.29 = (f32[8192]{0:T(1024)S(1)}, f32[8192]{0:T(1024)S(1)}, u32[]{:S(2)}, u32[]{:S(2)}) collective-permute-start(f32[8192]{0:T(1024)S(1)} %add.241), channel_id=1, source_target_pairs={{0,16},{4,20},{8,24},{12,28},{16,0},{20,4},{24,8},{28,12},{32,48},... | collective-permute-start | bytes 98312 | tf_op jit(solution)/shard_map/ppermute | solution.py:17
  257.3 9.7 %collective-permute-start.30 = (f32[8192]{0:T(1024)S(1)}, f32[8192]{0:T(1024)S(1)}, u32[]{:S(2)}, u32[]{:S(2)}) collective-permute-start(f32[8192]{0:T(1024)S(1)} %add.242), channel_id=1, source_target_pairs={{0,32},{4,36},{8,40},{12,44},{16,48},{20,52},{24,56},{28,60},{32,0... | collective-permute-start | bytes 98312 | tf_op jit(solution)/shard_map/ppermute | solution.py:17
  272.9 7.0 %collective-permute-start.32 = (f32[8192]{0:T(1024)S(1)}, f32[8192]{0:T(1024)S(1)}, u32[]{:S(2)}, u32[]{:S(2)}) collective-permute-start(f32[8192]{0:T(1024)S(1)} %add.244), channel_id=1, source_target_pairs={{0,128},{4,132},{8,136},{12,140},{16,144},{20,148},{24,152},{28,15... | collective-permute-start | bytes 98312 | tf_op jit(solution)/shard_map/ppermute | solution.py:17
  279.8 10.6 %collective-permute-start.33 = (f32[8192]{0:T(1024)S(1)}, f32[8192]{0:T(1024)S(1)}, u32[]{:S(2)}, u32[]{:S(2)}) collective-permute-start(f32[8192]{0:T(1024)S(1)} %add.245), channel_id=1, source_target_pairs={{0,256},{4,260},{8,264},{12,268},{16,272},{20,276},{24,280},{28,28... | collective-permute-start | bytes 98312 | tf_op jit(solution)/shard_map/ppermute | solution.py:17
  302.4 7.0 %collective-permute-start.35 = (f32[256]{0:T(256)S(1)}, f32[256]{0:T(256)S(1)}, u32[]{:S(2)}, u32[]{:S(2)}) collective-permute-start(f32[256]{0:T(256)S(1)} %add.247), channel_id=1, source_target_pairs={{0,2},{1,3},{2,0},{3,1},{4,6},{5,7},{6,4},{7,5},{8,10},{9,11},{10,... | collective-permute-start | bytes 3080 | tf_op jit(solution)/shard_map/ppermute | solution.py:17
  324.8 6.1 %collective-permute-start.36 = (f32[4096,128]{1,0:T(8,128)S(1)}, f32[4096,128]{1,0:T(8,128)S(1)}, u32[]{:S(2)}, u32[]{:S(2)}) collective-permute-start(f32[4096,128]{1,0:T(8,128)S(1)} %dynamic-slice_bitcast_fusion), channel_id=1, source_target_pairs={{0,4},{4,0},{8,12},{12,8},{16,20},{20,16},{24,28},{28,24},{32,36},... | collective-permute-start | bytes 6291464 | tf_op jit(solution)/shard_map/ppermute | solution.py:17
  331.1 27.1 %collective-permute-start.37 = (f32[2048,128]{1,0:T(8,128)S(1)}, f32[2048,128]{1,0:T(8,128)S(1)}, u32[]{:S(2)}, u32[]{:S(2)}) collective-permute-start(f32[2048,128]{1,0:T(8,128)S(1)} %dynamic-slice_bitcast_fusion.1), channel_id=1, source_target_pairs={{0,8},{4,12},{8,0},{12,4},{16,24},{20,28},{24,16},{28,20},{32,40},... | collective-permute-start | bytes 3145736 | tf_op jit(solution)/shard_map/ppermute | solution.py:17
  358.4 27.2 %collective-permute-start.38 = (f32[1024,128]{1,0:T(8,128)S(1)}, f32[1024,128]{1,0:T(8,128)S(1)}, u32[]{:S(2)}, u32[]{:S(2)}) collective-permute-start(f32[1024,128]{1,0:T(8,128)S(1)} %dynamic-slice_bitcast_fusion.2), channel_id=1, source_target_pairs={{0,16},{4,20},{8,24},{12,28},{16,0},{20,4},{24,8},{28,12},{32,48},... | collective-permute-start | bytes 1572872 | tf_op jit(solution)/shard_map/ppermute | solution.py:17
  385.6 18.6 %collective-permute-start.39 = (f32[512,128]{1,0:T(8,128)S(1)}, f32[512,128]{1,0:T(8,128)S(1)}, u32[]{:S(2)}, u32[]{:S(2)}) collective-permute-start(f32[512,128]{1,0:T(8,128)S(1)} %dynamic-slice_bitcast_fusion.3), channel_id=1, source_target_pairs={{0,32},{4,36},{8,40},{12,44},{16,48},{20,52},{24,56},{28,60},{32,0... | collective-permute-start | bytes 786440 | tf_op jit(solution)/shard_map/ppermute | solution.py:17
  404.3 7.3 %collective-permute-start.40 = (f32[256,128]{1,0:T(8,128)S(1)}, f32[256,128]{1,0:T(8,128)S(1)}, u32[]{:S(2)}, u32[]{:S(2)}) collective-permute-start(f32[256,128]{1,0:T(8,128)S(1)} %dynamic-slice_bitcast_fusion.4), channel_id=1, source_target_pairs={{0,64},{4,68},{8,72},{12,76},{16,80},{20,84},{24,88},{28,92},{32,9... | collective-permute-start | bytes 393224 | tf_op jit(solution)/shard_map/ppermute | solution.py:17
  407.8 8.8 %collective-permute-start.43 = (f32[256,128]{1,0:T(8,128)S(1)}, f32[256,128]{1,0:T(8,128)S(1)}, u32[]{:S(2)}, u32[]{:S(2)}) collective-permute-start(f32[256,128]{1,0:T(8,128)S(1)} %bitcast.253), channel_id=1, source_target_pairs={{0,1},{1,0},{2,3},{3,2},{4,5},{5,4},{6,7},{7,6},{8,9},{9,8},{10,11... | collective-permute-start | bytes 393224 | tf_op jit(solution)/shard_map/ppermute | solution.py:17
  411.6 8.4 %collective-permute-start.41 = (f32[128,128]{1,0:T(8,128)S(1)}, f32[128,128]{1,0:T(8,128)S(1)}, u32[]{:S(2)}, u32[]{:S(2)}) collective-permute-start(f32[128,128]{1,0:T(8,128)S(1)} %dynamic-slice_bitcast_fusion.5), channel_id=1, source_target_pairs={{0,128},{4,132},{8,136},{12,140},{16,144},{20,148},{24,152},{28,15... | collective-permute-start | bytes 196616 | tf_op jit(solution)/shard_map/ppermute | solution.py:17
  416.7 10.7 %collective-permute-start.44 = (f32[256,128]{1,0:T(8,128)S(1)}, f32[256,128]{1,0:T(8,128)S(1)}, u32[]{:S(2)}, u32[]{:S(2)}) collective-permute-start(f32[256,128]{1,0:T(8,128)S(1)} %bitcast_add_fusion.7), channel_id=1, source_target_pairs={{0,2},{1,3},{2,0},{3,1},{4,6},{5,7},{6,4},{7,5},{8,10},{9,11},{10,... | collective-permute-start | bytes 393224 | tf_op jit(solution)/shard_map/ppermute | solution.py:17
  420.0 9.7 %collective-permute-start.42 = (f32[64,128]{1,0:T(8,128)S(1)}, f32[64,128]{1,0:T(8,128)S(1)}, u32[]{:S(2)}, u32[]{:S(2)}) collective-permute-start(f32[64,128]{1,0:T(8,128)S(1)} %dynamic-slice_bitcast_fusion.6), channel_id=1, source_target_pairs={{0,256},{4,260},{8,264},{12,268},{16,272},{20,276},{24,280},{28,28... | collective-permute-start | bytes 98312 | tf_op jit(solution)/shard_map/ppermute | solution.py:17
  (16 other events, 143.5 us)

commit v2 on v1

--- a/solution.py
+++ b/solution.py
@@ -21,21 +21,33 @@
     return int(math.log2(lax.axis_size(axis)))
 
 
-def tree_butterfly(x, axis, combine):
-    for k in range(bits(axis)):
-        x = combine(x, swap(x, axis, k))
-    return x
+GATHER_ORDER = ((6, 5, 4, 3, 2, 1, 0), (3, 2, 1, 6, 5, 4, 0))
 
 
-def sum_over(x, axis):
-    return tree_butterfly(x, axis, lambda a, b: a + b)
+def core_swap(x, axis, step, orders):
+    n = lax.axis_size(axis)
+    pairs = [(i, i ^ (1 << orders[i & 1][step])) for i in range(n)]
+    return lax.ppermute(x, axis, pairs)
+
+
+def core_bit(me, step, orders):
+    k = jnp.where((me & 1) == 0, orders[0][step], orders[1][step])
+    return (me >> k) & 1
+
+
+def swap_halves(x):
+    rows = x.shape[0]
+    return x.reshape((8, 8, rows // 64) + x.shape[1:]).swapaxes(0, 1).reshape(x.shape)
 
 
 def gather_blocks(x, axis):
     me = lax.axis_index(axis)
-    for k in reversed(range(bits(axis))):
-        bit = (me >> k) & 1
-        other = swap(x, axis, k)
+    steps = len(GATHER_ORDER[0])
+    for step in range(steps):
+        bit = core_bit(me, step, GATHER_ORDER)
+        other = core_swap(x, axis, step, GATHER_ORDER)
+        if step == steps - 1:
+            other = swap_halves(other)
         buf = jnp.zeros((2,) + x.shape, x.dtype)
         buf = lax.dynamic_update_index_in_dim(buf, x, bit, 0)
         buf = lax.dynamic_update_index_in_dim(buf, other, 1 - bit, 0)
@@ -45,13 +57,34 @@
 
 def scatter_blocks(x, axis):
     me = lax.axis_index(axis)
-    for k in range(bits(axis)):
-        bit = (me >> k) & 1
+    orders = tuple(tuple(reversed(o)) for o in GATHER_ORDER)
+    for step in range(len(orders[0])):
+        bit = core_bit(me, step, orders)
         x = x.reshape((2, x.shape[0] // 2) + x.shape[1:])
         keep = lax.dynamic_index_in_dim(x, bit, 0, keepdims=False)
         send = lax.dynamic_index_in_dim(x, 1 - bit, 0, keepdims=False)
-        x = keep + swap(send, axis, k)
+        other = core_swap(send, axis, step, orders)
+        if step == 0:
+            other = swap_halves(other)
+        x = keep + other
     return x
+
+
+def column_sum(x, axis):
+    for k in range(bits(axis)):
+        other = swap(x, axis, k)
+        if k == 0:
+            other = other.reshape(2, 8, 8, -1).swapaxes(1, 2).reshape(x.shape)
+        x = x + other
+    return x
+
+
+def proto_sum(x):
+    parts = lax.all_gather(x, "proto", axis=0, tiled=False)
+    total = parts[0]
+    for j in range(1, parts.shape[0]):
+        total = total + parts[j]
+    return total
 
 
 def contract_rows(left, right):
@@ -97,18 +130,21 @@
     )
     student_local = student_local.reshape(rows_here)
     total_local = total_local.reshape(rows_here)
-    stats = tree_butterfly(
-        jnp.stack([teacher_local, student_local, total_local]), "proto", combine_stats
+    every = lax.all_gather(
+        jnp.stack([teacher_local, student_local, total_local]), "proto", axis=0, tiled=False
     )
+    stats = every[0]
+    for j in range(1, every.shape[0]):
+        stats = combine_stats(stats, every[j])
     teacher_top, student_top, total = stats[0], stats[1], stats[2]
     shift = jnp.exp((teacher_local - teacher_top) / teacher_temp)
     row_scale = jnp.ones((rows_here,), jnp.float32)
     col_scale = jnp.ones((base_local.shape[1],), jnp.float32)
     for step in range(ITERS):
         partial_cols = jnp.dot(row_scale * shift, base_local, precision=lax.Precision.HIGHEST)
-        col_scale = 1.0 / sum_over(partial_cols, "dp")
+        col_scale = 1.0 / column_sum(partial_cols, "dp")
         partial_rows = shift * jnp.dot(base_local, col_scale, precision=lax.Precision.HIGHEST)
-        row_scale = 1.0 / sum_over(partial_rows, "proto")
+        row_scale = 1.0 / lax.psum(partial_rows, "proto")
     row_factor = row_scale * shift
     student_factor = jnp.exp(student_local - student_top) / total
 
@@ -131,7 +167,7 @@
         ),
     )
     grad_logits = grad_logits.reshape(rows_here, -1)
-    grad_student = sum_over(student_terms.reshape(rows_here, width), "proto")
+    grad_student = proto_sum(student_terms.reshape(rows_here, width))
     grad_prototypes = scatter_blocks(
         lax.dot_general(
             grad_logits, student_emb, (((0,), (0,)), ((), ())), preferred_element_type=jnp.float32

time: 438 us -> 419 us (0.957)
  waiting for transfers between devices: 185 us -> 129 us
  blocking collectives: 0 us -> 50.4 us
  starting transfers between devices: 179 us -> 155 us
  matrix products: 52.5 us -> 66.1 us
    ppermute x45 -> x21, waiting for transfers between devices: 185 us -> 53.7 us  [swap(): return lax.ppermute(x, axis, [(i, i ^ 1 << k) for i in range(n)])]
    ppermute x45 -> x21, starting transfers between devices: 179 us -> 91 us  [swap(): return lax.ppermute(x, axis, [(i, i ^ 1 << k) for i in range(n)])]
    ppermute x0 -> x14, waiting for transfers between devices: none -> 74.9 us  [core_swap(): return lax.ppermute(x, axis, pairs)]
    ppermute x0 -> x14, starting transfers between devices: none -> 64.2 us  [core_swap(): return lax.ppermute(x, axis, pairs)]
    psum x0 -> x3, blocking collectives: none -> 25.4 us  [per_device(): row_scale = 1.0 / lax.psum(partial_rows, 'proto')]
    all_gather x0 -> x2, blocking collectives: none -> 25 us  [the longest x1 13.1 us: proto_sum(): parts = lax.all_gather(x, 'proto', axis=0, tiled=False)]
    dot_general x3, matrix products: 19.7 us -> 26.7 us  [per_device(): jnp.dot(base_local, col_scale, precision=lax.Precision.HIGHEST)]
    dot_general x3, matrix products: 14.5 us -> 21.2 us  [per_device(): jnp.dot(row_scale * shift, base_local, precision=lax.Precision.HIGHEST)]
  transfers between devices with their start and end apart: 45 -> 35, of which waited for: 42 -> 34; matrix products, arithmetic and copies ran while one was open for 0% -> 0% of each run, Pallas kernels for 0% -> 0%
where the time goes in v2:
time: 419 us; the launch traced here: 415 us
  starting transfers between devices  155 us (37%)
  waiting for transfers between devices  129 us (31%)
  matrix products  66.1 us (16%)
  blocking collectives  50.4 us (12%)
  other arithmetic  9.6 us (2%)
    ppermute x21, starting transfers between devices, swap(): return lax.ppermute(x, axis, [(i, i ^ 1 << k) for i in range(n)])  91 us
    ppermute x14, waiting for transfers between devices, core_swap(): return lax.ppermute(x, axis, pairs)  74.9 us
    ppermute x14, starting transfers between devices, core_swap(): return lax.ppermute(x, axis, pairs)  64.2 us
    ppermute x21, waiting for transfers between devices, swap(): return lax.ppermute(x, axis, [(i, i ^ 1 << k) for i in range(n)])  53.7 us
    dot_general x3, matrix products, per_device(): jnp.dot(base_local, col_scale, precision=lax.Precision.HIGHEST)  26.7 us
    psum x3, blocking collectives, per_device(): row_scale = 1.0 / lax.psum(partial_rows, 'proto')  25.4 us
    dot_general x3, matrix products, per_device(): jnp.dot(row_scale * shift, base_local, precision=lax.Precision.HIGHEST)  21.2 us
    dot_general x6, matrix products, contract_rows(): lax.dot_general(left, right, (((1,), (1,)), ((), ())), preferred_element_...  13.3 us
  transfers between devices with their start and end apart: 35, of which 34 were waited for; matrix products, arithmetic and copies ran while one was open for 0% of the time, Pallas kernels for 0%

profile of v2, /device:TPU:6, one launch (start us, length us, event | category | flops | bytes accessed | tf_op | source)
XLA Modules:
  0.0 415.3 jit_solution(4055983734558393730)
XLA Ops:
  1.4 10.9 %collective-permute-start = (bf16[64,128]{1,0:T(8,128)(2,1)S(1)}, bf16[64,128]{1,0:T(8,128)(2,1)S(1)}, u32[]{:S(2)}, u32[]{:S(2)}) collective-permute-start(bf16[64,128]{1,0:T(8,128)(2,1)S(1)} %get-tuple-element.160), channel_id=1, source_target_pairs={{0,256},{4,36},{8,264},{12,44},{16,272},{20,52},{24,280},{28,60},{... | collective-permute-start | bytes 49160 | tf_op jit(solution)/shard_map/ppermute | solution.py:30
  26.9 7.7 %collective-permute-start.3 = (bf16[512,128]{1,0:T(8,128)(2,1)S(1)}, bf16[512,128]{1,0:T(8,128)(2,1)S(1)}, u32[]{:S(2)}, u32[]{:S(2)}) collective-permute-start(bf16[512,128]{1,0:T(8,128)(2,1)S(1)} %bitcast.251), channel_id=1, source_target_pairs={{0,32},{4,260},{8,40},{12,268},{16,48},{20,276},{24,56},{28,284},{... | collective-permute-start | bytes 393224 | tf_op jit(solution)/shard_map/ppermute | solution.py:30
  38.6 4.9 %collective-permute-start.4 = (bf16[1024,128]{1,0:T(8,128)(2,1)S(1)}, bf16[1024,128]{1,0:T(8,128)(2,1)S(1)}, u32[]{:S(2)}, u32[]{:S(2)}) collective-permute-start(bf16[1024,128]{1,0:T(8,128)(2,1)S(1)} %bitcast.243), channel_id=1, source_target_pairs={{0,16},{4,132},{8,24},{12,140},{16,0},{20,148},{24,8},{28,156},{32... | collective-permute-start | bytes 786440 | tf_op jit(solution)/shard_map/ppermute | solution.py:30
  43.7 7.0 %collective-permute-done.4 = bf16[1024,128]{1,0:T(8,128)(2,1)S(1)} collective-permute-done((bf16[1024,128]{1,0:T(8,128)(2,1)S(1)}, bf16[1024,128]{1,0:T(8,128)(2,1)S(1)}, u32[]{:S(2)}, u32[]{:S(2)}) %collective-permute-start.4) | collective-permute-done | bytes 262176 | tf_op jit(solution)/shard_map/ppermute | solution.py:30
  52.9 8.9 %collective-permute-done.5 = bf16[2048,128]{1,0:T(8,128)(2,1)S(1)} collective-permute-done((bf16[2048,128]{1,0:T(8,128)(2,1)S(1)}, bf16[2048,128]{1,0:T(8,128)(2,1)S(1)}, u32[]{:S(2)}, u32[]{:S(2)}) %collective-permute-start.5) | collective-permute-done | bytes 524320 | tf_op jit(solution)/shard_map/ppermute | solution.py:30
  68.0 6.9 %while.37 = (s32[]{:T(128)}, f32[2,128,8192]{2,1,0:T(8,128)}, f32[2,128]{1,0:T(2,128)S(1)}, bf16[2,128,128]{2,1,0:T(8,128)(2,1)S(1)}, bf16[8192,128]{1,0:T(8,128)(2,1)S(1)}, /*index=5*/s32[]{:T(128)}, s32[]{:T(128)}) while((s32[]{:T(128)}, f32[2,128,8192]{2,1,0:T(8,128)}, f32[2,128]{1,0:T(2,128)S(1)}, bf16[2,128,128]{2,1,0:T(8,128)(2,1)S(1)}, ...), condition=%wide.region_2.3_spmd, body=%wide.region_0.2_spmd.sunk | while | flops 271581056 | bytes 14715477 | solution.py:117
  78.2 11.9 %all-gather.1 = f32[4,3,256]{2,1,0:T(4,128)S(1)} all-gather(f32[1,3,256]{2,1,0:T(4,128)S(1)} %maximum_bitcast_fusion), channel_id=2, replica_groups=mesh['dp'=128,'proto'=4] {'proto'}, dimensions={0}, use_global_device_ids=true | all-gather | bytes 15360 | tf_op jit(solution)/shard_map/all_gather | solution.py:133
  90.2 6.3 %fusion.34 = f32[1,8192,1]{1,0,2:T(1,128)S(1)} fusion(f32[2,128,1]{1,2,0:T(1,128)S(1)} %bitcast.281, f32[2,128,8192]{2,1,0:T(8,128)} %get-tuple-element.369), kind=kOutput, calls=%fused_computation.91 | convolution fusion | flops 25165824 | bytes 8422400 | tf_op jit(solution)/shard_map/dot_general | solution.py:144
  112.4 7.1 %collective-permute-start.10 = (f32[8192]{0:T(1024)S(1)}, f32[8192]{0:T(1024)S(1)}, u32[]{:S(2)}, u32[]{:S(2)}) collective-permute-start(f32[8192]{0:T(1024)S(1)} %add.222), channel_id=1, source_target_pairs={{0,32},{4,36},{8,40},{12,44},{16,48},{20,52},{24,56},{28,60},{32,0... | collective-permute-start | bytes 98312 | tf_op jit(solution)/shard_map/ppermute | solution.py:17
  134.9 9.1 %collective-permute-start.13 = (f32[8192]{0:T(1024)S(1)}, f32[8192]{0:T(1024)S(1)}, u32[]{:S(2)}, u32[]{:S(2)}) collective-permute-start(f32[8192]{0:T(1024)S(1)} %add.225), channel_id=1, source_target_pairs={{0,256},{4,260},{8,264},{12,268},{16,272},{20,276},{24,280},{28,28... | collective-permute-start | bytes 98312 | tf_op jit(solution)/shard_map/ppermute | solution.py:17
  145.8 8.9 %fusion.35 = f32[1,256]{1,0:T(1,128)S(1)} fusion(f32[256,8192]{1,0:T(8,128)} %bitcast.224, f32[8192,1]{0,1:T(1,128)S(1)} %bitcast.268), kind=kOutput, calls=%fused_computation.92 | convolution fusion | flops 25165824 | bytes 8422400 | tf_op jit(solution)/shard_map/dot_general | solution.py:146
  154.8 7.7 %psum.21 = f32[256]{0:T(256)S(1)} all-reduce(f32[256]{0:T(256)S(1)} %get-tuple-element.157), channel_id=1, replica_groups=mesh['dp'=128,'proto'=4] {'proto'}, use_global_device_ids=true, to_apply=%region_7.8 | all-reduce | flops 256 | bytes 2048 | tf_op jit(solution)/shard_map/psum | solution.py:147
  162.4 7.4 %fusion.36 = f32[1,8192]{1,0:T(1,128)S(1)} fusion(f32[256,1]{0,1:T(1,128)S(1)} %bitcast.282, f32[256,8192]{1,0:T(8,128)} %bitcast.225), kind=kOutput, calls=%fused_computation.93 | convolution fusion | flops 25165824 | bytes 8422400 | tf_op jit(solution)/shard_map/dot_general | solution.py:144
  185.6 6.9 %collective-permute-start.17 = (f32[8192]{0:T(1024)S(1)}, f32[8192]{0:T(1024)S(1)}, u32[]{:S(2)}, u32[]{:S(2)}) collective-permute-start(f32[8192]{0:T(1024)S(1)} %add.229), channel_id=1, source_target_pairs={{0,32},{4,36},{8,40},{12,44},{16,48},{20,52},{24,56},{28,60},{32,0... | collective-permute-start | bytes 98312 | tf_op jit(solution)/shard_map/ppermute | solution.py:17
  201.3 4.7 %collective-permute-start.19 = (f32[8192]{0:T(1024)S(1)}, f32[8192]{0:T(1024)S(1)}, u32[]{:S(2)}, u32[]{:S(2)}) collective-permute-start(f32[8192]{0:T(1024)S(1)} %add.231), channel_id=1, source_target_pairs={{0,128},{4,132},{8,136},{12,140},{16,144},{20,148},{24,152},{28,15... | collective-permute-start | bytes 98312 | tf_op jit(solution)/shard_map/ppermute | solution.py:17
  208.0 8.1 %collective-permute-start.20 = (f32[8192]{0:T(1024)S(1)}, f32[8192]{0:T(1024)S(1)}, u32[]{:S(2)}, u32[]{:S(2)}) collective-permute-start(f32[8192]{0:T(1024)S(1)} %add.232), channel_id=1, source_target_pairs={{0,256},{4,260},{8,264},{12,268},{16,272},{20,276},{24,280},{28,28... | collective-permute-start | bytes 98312 | tf_op jit(solution)/shard_map/ppermute | solution.py:17
  218.0 8.9 %fusion.37 = f32[1,256]{1,0:T(1,128)S(1)} fusion(f32[256,8192]{1,0:T(8,128)} %bitcast.226, f32[8192,1]{0,1:T(1,128)S(1)} %bitcast.269), kind=kOutput, calls=%fused_computation.94 | convolution fusion | flops 25165824 | bytes 8422400 | tf_op jit(solution)/shard_map/dot_general | solution.py:146
  226.9 10.0 %psum.22 = f32[256]{0:T(256)S(1)} all-reduce(f32[256]{0:T(256)S(1)} %mul.78), channel_id=1, replica_groups=mesh['dp'=128,'proto'=4] {'proto'}, use_global_device_ids=true, to_apply=%region_8.9 | all-reduce | flops 256 | bytes 2048 | tf_op jit(solution)/shard_map/psum | solution.py:147
  236.9 7.4 %fusion.38 = f32[1,8192]{1,0:T(1,128)S(1)} fusion(f32[256,1]{0,1:T(1,128)S(1)} %bitcast.284, f32[256,8192]{1,0:T(8,128)} %bitcast.227), kind=kOutput, calls=%fused_computation.95 | convolution fusion | flops 25165824 | bytes 8422400 | tf_op jit(solution)/shard_map/dot_general | solution.py:144
  260.1 7.0 %collective-permute-start.24 = (f32[8192]{0:T(1024)S(1)}, f32[8192]{0:T(1024)S(1)}, u32[]{:S(2)}, u32[]{:S(2)}) collective-permute-start(f32[8192]{0:T(1024)S(1)} %add.236), channel_id=1, source_target_pairs={{0,32},{4,36},{8,40},{12,44},{16,48},{20,52},{24,56},{28,60},{32,0... | collective-permute-start | bytes 98312 | tf_op jit(solution)/shard_map/ppermute | solution.py:17
  282.6 8.0 %collective-permute-start.27 = (f32[8192]{0:T(1024)S(1)}, f32[8192]{0:T(1024)S(1)}, u32[]{:S(2)}, u32[]{:S(2)}) collective-permute-start(f32[8192]{0:T(1024)S(1)} %add.239), channel_id=1, source_target_pairs={{0,256},{4,260},{8,264},{12,268},{16,272},{20,276},{24,280},{28,28... | collective-permute-start | bytes 98312 | tf_op jit(solution)/shard_map/ppermute | solution.py:17
  292.5 8.9 %fusion.39 = f32[1,256]{1,0:T(1,128)S(1)} fusion(f32[256,8192]{1,0:T(8,128)} %bitcast.228, f32[8192,1]{0,1:T(1,128)S(1)} %bitcast.261), kind=kOutput, calls=%fused_computation.96 | convolution fusion | flops 25165824 | bytes 8422400 | tf_op jit(solution)/shard_map/dot_general | solution.py:146
  301.4 7.7 %psum.23 = f32[256]{0:T(256)S(1)} all-reduce(f32[256]{0:T(256)S(1)} %mul.80), channel_id=1, replica_groups=mesh['dp'=128,'proto'=4] {'proto'}, use_global_device_ids=true, to_apply=%region_9.10 | all-reduce | flops 256 | bytes 2048 | tf_op jit(solution)/shard_map/psum | solution.py:147
  309.1 11.7 %while.38 = (s32[]{:T(128)}, bf16[2,128,8192]{2,1,0:T(8,128)(2,1)}, f32[2,128,128]{2,1,0:T(8,128)S(1)}, bf16[2,128,128]{2,1,0:T(8,128)(2,1)S(1)}, bf16[8192,128]...) while((s32[]{:T(128)}, bf16[2,128,8192]{2,1,0:T(8,128)(2,1)}, ...), condition=%wide.region_11.12_spmd, body=%wide.region_10.11_spmd.sunk | while | flops 544227328 | bytes 14816889 | solution.py:159
  309.2 5.1 %bitcast_dynamic-update-slice_fusion.18 = (bf16[2,128,8192]{2,1,0:T(8,128)(2,1)}, bf16[128,8192]{1,0:T(8,128)(2,1)S(1)}) fusion(bf16[2,128,8192]{2,1,0:T(8,128)(2,1)} %get-tuple-element.373, s32[]{:T(128)} %get-tuple-element.372, f32[8192]{0:T(1024)S(1)} %get-tuple-element.392, f32[2,128,8192]{2,1,0:T(8,128)} %get-tuple-element.391, ...), kind=kOutput, calls=%fused_computation.18.clone.1 | convolution fusion | flops 275775488 | bytes 10553856 | tf_op jit(solution)/shard_map/while/body/eval_jaxpr/dot_general | solution.py:91
  315.0 5.1 %bitcast_dynamic-update-slice_fusion.18 = (bf16[2,128,8192]{2,1,0:T(8,128)(2,1)}, bf16[128,8192]{1,0:T(8,128)(2,1)S(1)}) fusion(bf16[2,128,8192]{2,1,0:T(8,128)(2,1)} %get-tuple-element.373, s32[]{:T(128)} %get-tuple-element.372, f32[8192]{0:T(1024)S(1)} %get-tuple-element.392, f32[2,128,8192]{2,1,0:T(8,128)} %get-tuple-element.391, ...), kind=kOutput, calls=%fused_computation.18.clone.1 | convolution fusion | flops 275775488 | bytes 10553856 | tf_op jit(solution)/shard_map/while/body/eval_jaxpr/dot_general | solution.py:91
  333.2 14.8 %collective-permute-done.29 = f32[2048,128]{1,0:T(8,128)S(1)} collective-permute-done((f32[2048,128]{1,0:T(8,128)S(1)}, f32[2048,128]{1,0:T(8,128)S(1)}, u32[]{:S(2)}, u32[]{:S(2)}) %collective-permute-start.29) | collective-permute-done | bytes 1048608 | tf_op jit(solution)/shard_map/ppermute | solution.py:30
  350.7 14.4 %collective-permute-done.30 = f32[1024,128]{1,0:T(8,128)S(1)} collective-permute-done((f32[1024,128]{1,0:T(8,128)S(1)}, f32[1024,128]{1,0:T(8,128)S(1)}, u32[]{:S(2)}, u32[]{:S(2)}) %collective-permute-start.30) | collective-permute-done | bytes 524320 | tf_op jit(solution)/shard_map/ppermute | solution.py:30
  365.3 6.9 %collective-permute-start.31 = (f32[512,128]{1,0:T(8,128)S(1)}, f32[512,128]{1,0:T(8,128)S(1)}, u32[]{:S(2)}, u32[]{:S(2)}) collective-permute-start(f32[512,128]{1,0:T(8,128)S(1)} %dynamic-slice_bitcast_fusion.3), channel_id=1, source_target_pairs={{0,32},{4,260},{8,40},{12,268},{16,48},{20,276},{24,56},{28,284},{... | collective-permute-start | bytes 786440 | tf_op jit(solution)/shard_map/ppermute | solution.py:30
  372.1 8.1 %collective-permute-done.31 = f32[512,128]{1,0:T(8,128)S(1)} collective-permute-done((f32[512,128]{1,0:T(8,128)S(1)}, f32[512,128]{1,0:T(8,128)S(1)}, u32[]{:S(2)}, u32[]{:S(2)}) %collective-permute-start.31) | collective-permute-done | bytes 262176 | tf_op jit(solution)/shard_map/ppermute | solution.py:30
  391.9 13.1 %all_gather.11 = f32[4,256,128]{2,1,0:T(8,128)S(1)} all-gather(f32[1,256,128]{2,1,0:T(8,128)S(1)} %bitcast.270), channel_id=1, replica_groups=mesh['dp'=128,'proto'=4] {'proto'}, dimensions={0}, use_global_device_ids=true | all-gather | bytes 655360 | tf_op jit(solution)/shard_map/all_gather | solution.py:83
  405.0 7.7 %collective-permute-start.34 = (f32[64,128]{1,0:T(8,128)S(1)}, f32[64,128]{1,0:T(8,128)S(1)}, u32[]{:S(2)}, u32[]{:S(2)}) collective-permute-start(f32[64,128]{1,0:T(8,128)S(1)} %dynamic-slice_bitcast_fusion.6), channel_id=1, source_target_pairs={{0,256},{4,36},{8,264},{12,44},{16,272},{20,52},{24,280},{28,60},{... | collective-permute-start | bytes 98312 | tf_op jit(solution)/shard_map/ppermute | solution.py:30
  (163 shorter events, 166.5 us)
Async XLA Ops:
  1.4 12.6 %collective-permute-start = (bf16[64,128]{1,0:T(8,128)(2,1)S(1)}, bf16[64,128]{1,0:T(8,128)(2,1)S(1)}, u32[]{:S(2)}, u32[]{:S(2)}) collective-permute-start(bf16[64,128]{1,0:T(8,128)(2,1)S(1)} %get-tuple-element.160), channel_id=1, source_target_pairs={{0,256},{4,36},{8,264},{12,44},{16,272},{20,52},{24,280},{28,60},{... | collective-permute-start | bytes 49160 | tf_op jit(solution)/shard_map/ppermute | solution.py:30
  14.1 6.7 %collective-permute-start.1 = (bf16[128,128]{1,0:T(8,128)(2,1)S(1)}, bf16[128,128]{1,0:T(8,128)(2,1)S(1)}, u32[]{:S(2)}, u32[]{:S(2)}) collective-permute-start(bf16[128,128]{1,0:T(8,128)(2,1)S(1)} %bitcast.271), channel_id=1, source_target_pairs={{0,128},{4,20},{8,136},{12,28},{16,144},{20,4},{24,152},{28,12},{3... | collective-permute-start | bytes 98312 | tf_op jit(solution)/shard_map/ppermute | solution.py:30
  20.8 6.1 %collective-permute-start.2 = (bf16[256,128]{1,0:T(8,128)(2,1)S(1)}, bf16[256,128]{1,0:T(8,128)(2,1)S(1)}, u32[]{:S(2)}, u32[]{:S(2)}) collective-permute-start(bf16[256,128]{1,0:T(8,128)(2,1)S(1)} %bitcast.259), channel_id=1, source_target_pairs={{0,64},{4,12},{8,72},{12,4},{16,80},{20,28},{24,88},{28,20},{32,96... | collective-permute-start | bytes 196616 | tf_op jit(solution)/shard_map/ppermute | solution.py:30
  26.9 11.6 %collective-permute-start.3 = (bf16[512,128]{1,0:T(8,128)(2,1)S(1)}, bf16[512,128]{1,0:T(8,128)(2,1)S(1)}, u32[]{:S(2)}, u32[]{:S(2)}) collective-permute-start(bf16[512,128]{1,0:T(8,128)(2,1)S(1)} %bitcast.251), channel_id=1, source_target_pairs={{0,32},{4,260},{8,40},{12,268},{16,48},{20,276},{24,56},{28,284},{... | collective-permute-start | bytes 393224 | tf_op jit(solution)/shard_map/ppermute | solution.py:30
  38.6 12.1 %collective-permute-start.4 = (bf16[1024,128]{1,0:T(8,128)(2,1)S(1)}, bf16[1024,128]{1,0:T(8,128)(2,1)S(1)}, u32[]{:S(2)}, u32[]{:S(2)}) collective-permute-start(bf16[1024,128]{1,0:T(8,128)(2,1)S(1)} %bitcast.243), channel_id=1, source_target_pairs={{0,16},{4,132},{8,24},{12,140},{16,0},{20,148},{24,8},{28,156},{32... | collective-permute-start | bytes 786440 | tf_op jit(solution)/shard_map/ppermute | solution.py:30
  50.7 11.1 %collective-permute-start.5 = (bf16[2048,128]{1,0:T(8,128)(2,1)S(1)}, bf16[2048,128]{1,0:T(8,128)(2,1)S(1)}, u32[]{:S(2)}, u32[]{:S(2)}) collective-permute-start(bf16[2048,128]{1,0:T(8,128)(2,1)S(1)} %bitcast.241), channel_id=1, source_target_pairs={{0,8},{4,68},{8,0},{12,76},{16,24},{20,84},{24,16},{28,92},{32,40}... | collective-permute-start | bytes 1572872 | tf_op jit(solution)/shard_map/ppermute | solution.py:30
  61.9 4.7 %collective-permute-start.6 = (bf16[4096,128]{1,0:T(8,128)(2,1)S(1)}, bf16[4096,128]{1,0:T(8,128)(2,1)}, u32[]{:S(2)}, u32[]{:S(2)}) collective-permute-start(bf16[4096,128]{1,0:T(8,128)(2,1)S(1)} %bitcast.234), channel_id=1, source_target_pairs={{0,4},{4,0},{8,12},{12,8},{16,20},{20,16},{24,28},{28,24},{32,36},... | collective-permute-start | bytes 3145736 | tf_op jit(solution)/shard_map/ppermute | solution.py:30
  99.8 5.8 %collective-permute-start.8 = (f32[8192]{0:T(1024)S(1)}, f32[8192]{0:T(1024)S(1)}, u32[]{:S(2)}, u32[]{:S(2)}) collective-permute-start(f32[8192]{0:T(1024)S(1)} %add.220), channel_id=1, source_target_pairs={{0,8},{4,12},{8,0},{12,4},{16,24},{20,28},{24,16},{28,20},{32,40},... | collective-permute-start | bytes 98312 | tf_op jit(solution)/shard_map/ppermute | solution.py:17
  105.6 6.8 %collective-permute-start.9 = (f32[8192]{0:T(1024)S(1)}, f32[8192]{0:T(1024)S(1)}, u32[]{:S(2)}, u32[]{:S(2)}) collective-permute-start(f32[8192]{0:T(1024)S(1)} %add.221), channel_id=1, source_target_pairs={{0,16},{4,20},{8,24},{12,28},{16,0},{20,4},{24,8},{28,12},{32,48},... | collective-permute-start | bytes 98312 | tf_op jit(solution)/shard_map/ppermute | solution.py:17
  112.4 9.9 %collective-permute-start.10 = (f32[8192]{0:T(1024)S(1)}, f32[8192]{0:T(1024)S(1)}, u32[]{:S(2)}, u32[]{:S(2)}) collective-permute-start(f32[8192]{0:T(1024)S(1)} %add.222), channel_id=1, source_target_pairs={{0,32},{4,36},{8,40},{12,44},{16,48},{20,52},{24,56},{28,60},{32,0... | collective-permute-start | bytes 98312 | tf_op jit(solution)/shard_map/ppermute | solution.py:17
  122.3 5.8 %collective-permute-start.11 = (f32[8192]{0:T(1024)S(1)}, f32[8192]{0:T(1024)S(1)}, u32[]{:S(2)}, u32[]{:S(2)}) collective-permute-start(f32[8192]{0:T(1024)S(1)} %add.223), channel_id=1, source_target_pairs={{0,64},{4,68},{8,72},{12,76},{16,80},{20,84},{24,88},{28,92},{32,9... | collective-permute-start | bytes 98312 | tf_op jit(solution)/shard_map/ppermute | solution.py:17
  128.1 6.7 %collective-permute-start.12 = (f32[8192]{0:T(1024)S(1)}, f32[8192]{0:T(1024)S(1)}, u32[]{:S(2)}, u32[]{:S(2)}) collective-permute-start(f32[8192]{0:T(1024)S(1)} %add.224), channel_id=1, source_target_pairs={{0,128},{4,132},{8,136},{12,140},{16,144},{20,148},{24,152},{28,15... | collective-permute-start | bytes 98312 | tf_op jit(solution)/shard_map/ppermute | solution.py:17
  134.9 11.0 %collective-permute-start.13 = (f32[8192]{0:T(1024)S(1)}, f32[8192]{0:T(1024)S(1)}, u32[]{:S(2)}, u32[]{:S(2)}) collective-permute-start(f32[8192]{0:T(1024)S(1)} %add.225), channel_id=1, source_target_pairs={{0,256},{4,260},{8,264},{12,268},{16,272},{20,276},{24,280},{28,28... | collective-permute-start | bytes 98312 | tf_op jit(solution)/shard_map/ppermute | solution.py:17
  173.1 5.8 %collective-permute-start.15 = (f32[8192]{0:T(1024)S(1)}, f32[8192]{0:T(1024)S(1)}, u32[]{:S(2)}, u32[]{:S(2)}) collective-permute-start(f32[8192]{0:T(1024)S(1)} %add.227), channel_id=1, source_target_pairs={{0,8},{4,12},{8,0},{12,4},{16,24},{20,28},{24,16},{28,20},{32,40},... | collective-permute-start | bytes 98312 | tf_op jit(solution)/shard_map/ppermute | solution.py:17
  178.9 6.7 %collective-permute-start.16 = (f32[8192]{0:T(1024)S(1)}, f32[8192]{0:T(1024)S(1)}, u32[]{:S(2)}, u32[]{:S(2)}) collective-permute-start(f32[8192]{0:T(1024)S(1)} %add.228), channel_id=1, source_target_pairs={{0,16},{4,20},{8,24},{12,28},{16,0},{20,4},{24,8},{28,12},{32,48},... | collective-permute-start | bytes 98312 | tf_op jit(solution)/shard_map/ppermute | solution.py:17
  185.6 9.9 %collective-permute-start.17 = (f32[8192]{0:T(1024)S(1)}, f32[8192]{0:T(1024)S(1)}, u32[]{:S(2)}, u32[]{:S(2)}) collective-permute-start(f32[8192]{0:T(1024)S(1)} %add.229), channel_id=1, source_target_pairs={{0,32},{4,36},{8,40},{12,44},{16,48},{20,52},{24,56},{28,60},{32,0... | collective-permute-start | bytes 98312 | tf_op jit(solution)/shard_map/ppermute | solution.py:17
  195.5 5.8 %collective-permute-start.18 = (f32[8192]{0:T(1024)S(1)}, f32[8192]{0:T(1024)S(1)}, u32[]{:S(2)}, u32[]{:S(2)}) collective-permute-start(f32[8192]{0:T(1024)S(1)} %add.230), channel_id=1, source_target_pairs={{0,64},{4,68},{8,72},{12,76},{16,80},{20,84},{24,88},{28,92},{32,9... | collective-permute-start | bytes 98312 | tf_op jit(solution)/shard_map/ppermute | solution.py:17
  201.3 6.7 %collective-permute-start.19 = (f32[8192]{0:T(1024)S(1)}, f32[8192]{0:T(1024)S(1)}, u32[]{:S(2)}, u32[]{:S(2)}) collective-permute-start(f32[8192]{0:T(1024)S(1)} %add.231), channel_id=1, source_target_pairs={{0,128},{4,132},{8,136},{12,140},{16,144},{20,148},{24,152},{28,15... | collective-permute-start | bytes 98312 | tf_op jit(solution)/shard_map/ppermute | solution.py:17
  208.0 10.0 %collective-permute-start.20 = (f32[8192]{0:T(1024)S(1)}, f32[8192]{0:T(1024)S(1)}, u32[]{:S(2)}, u32[]{:S(2)}) collective-permute-start(f32[8192]{0:T(1024)S(1)} %add.232), channel_id=1, source_target_pairs={{0,256},{4,260},{8,264},{12,268},{16,272},{20,276},{24,280},{28,28... | collective-permute-start | bytes 98312 | tf_op jit(solution)/shard_map/ppermute | solution.py:17
  247.6 5.8 %collective-permute-start.22 = (f32[8192]{0:T(1024)S(1)}, f32[8192]{0:T(1024)S(1)}, u32[]{:S(2)}, u32[]{:S(2)}) collective-permute-start(f32[8192]{0:T(1024)S(1)} %add.234), channel_id=1, source_target_pairs={{0,8},{4,12},{8,0},{12,4},{16,24},{20,28},{24,16},{28,20},{32,40},... | collective-permute-start | bytes 98312 | tf_op jit(solution)/shard_map/ppermute | solution.py:17
  253.4 6.7 %collective-permute-start.23 = (f32[8192]{0:T(1024)S(1)}, f32[8192]{0:T(1024)S(1)}, u32[]{:S(2)}, u32[]{:S(2)}) collective-permute-start(f32[8192]{0:T(1024)S(1)} %add.235), channel_id=1, source_target_pairs={{0,16},{4,20},{8,24},{12,28},{16,0},{20,4},{24,8},{28,12},{32,48},... | collective-permute-start | bytes 98312 | tf_op jit(solution)/shard_map/ppermute | solution.py:17
  260.1 9.9 %collective-permute-start.24 = (f32[8192]{0:T(1024)S(1)}, f32[8192]{0:T(1024)S(1)}, u32[]{:S(2)}, u32[]{:S(2)}) collective-permute-start(f32[8192]{0:T(1024)S(1)} %add.236), channel_id=1, source_target_pairs={{0,32},{4,36},{8,40},{12,44},{16,48},{20,52},{24,56},{28,60},{32,0... | collective-permute-start | bytes 98312 | tf_op jit(solution)/shard_map/ppermute | solution.py:17
  270.1 5.8 %collective-permute-start.25 = (f32[8192]{0:T(1024)S(1)}, f32[8192]{0:T(1024)S(1)}, u32[]{:S(2)}, u32[]{:S(2)}) collective-permute-start(f32[8192]{0:T(1024)S(1)} %add.237), channel_id=1, source_target_pairs={{0,64},{4,68},{8,72},{12,76},{16,80},{20,84},{24,88},{28,92},{32,9... | collective-permute-start | bytes 98312 | tf_op jit(solution)/shard_map/ppermute | solution.py:17
  275.9 6.7 %collective-permute-start.26 = (f32[8192]{0:T(1024)S(1)}, f32[8192]{0:T(1024)S(1)}, u32[]{:S(2)}, u32[]{:S(2)}) collective-permute-start(f32[8192]{0:T(1024)S(1)} %add.238), channel_id=1, source_target_pairs={{0,128},{4,132},{8,136},{12,140},{16,144},{20,148},{24,152},{28,15... | collective-permute-start | bytes 98312 | tf_op jit(solution)/shard_map/ppermute | solution.py:17
  282.6 9.9 %collective-permute-start.27 = (f32[8192]{0:T(1024)S(1)}, f32[8192]{0:T(1024)S(1)}, u32[]{:S(2)}, u32[]{:S(2)}) collective-permute-start(f32[8192]{0:T(1024)S(1)} %add.239), channel_id=1, source_target_pairs={{0,256},{4,260},{8,264},{12,268},{16,272},{20,276},{24,280},{28,28... | collective-permute-start | bytes 98312 | tf_op jit(solution)/shard_map/ppermute | solution.py:17
  324.6 6.1 %collective-permute-start.28 = (f32[4096,128]{1,0:T(8,128)S(1)}, f32[4096,128]{1,0:T(8,128)S(1)}, u32[]{:S(2)}, u32[]{:S(2)}) collective-permute-start(f32[4096,128]{1,0:T(8,128)S(1)} %get-tuple-element.169), channel_id=1, source_target_pairs={{0,4},{4,0},{8,12},{12,8},{16,20},{20,16},{24,28},{28,24},{32,36},... | collective-permute-start | bytes 6291464 | tf_op jit(solution)/shard_map/ppermute | solution.py:30
  331.3 16.7 %collective-permute-start.29 = (f32[2048,128]{1,0:T(8,128)S(1)}, f32[2048,128]{1,0:T(8,128)S(1)}, u32[]{:S(2)}, u32[]{:S(2)}) collective-permute-start(f32[2048,128]{1,0:T(8,128)S(1)} %dynamic-slice_bitcast_fusion.1), channel_id=1, source_target_pairs={{0,8},{4,68},{8,0},{12,76},{16,24},{20,84},{24,16},{28,92},{32,40}... | collective-permute-start | bytes 3145736 | tf_op jit(solution)/shard_map/ppermute | solution.py:30
  348.1 17.0 %collective-permute-start.30 = (f32[1024,128]{1,0:T(8,128)S(1)}, f32[1024,128]{1,0:T(8,128)S(1)}, u32[]{:S(2)}, u32[]{:S(2)}) collective-permute-start(f32[1024,128]{1,0:T(8,128)S(1)} %dynamic-slice_bitcast_fusion.2), channel_id=1, source_target_pairs={{0,16},{4,132},{8,24},{12,140},{16,0},{20,148},{24,8},{28,156},{32... | collective-permute-start | bytes 1572872 | tf_op jit(solution)/shard_map/ppermute | solution.py:30
  365.3 15.0 %collective-permute-start.31 = (f32[512,128]{1,0:T(8,128)S(1)}, f32[512,128]{1,0:T(8,128)S(1)}, u32[]{:S(2)}, u32[]{:S(2)}) collective-permute-start(f32[512,128]{1,0:T(8,128)S(1)} %dynamic-slice_bitcast_fusion.3), channel_id=1, source_target_pairs={{0,32},{4,260},{8,40},{12,268},{16,48},{20,276},{24,56},{28,284},{... | collective-permute-start | bytes 786440 | tf_op jit(solution)/shard_map/ppermute | solution.py:30
  380.3 6.9 %collective-permute-start.32 = (f32[256,128]{1,0:T(8,128)S(1)}, f32[256,128]{1,0:T(8,128)S(1)}, u32[]{:S(2)}, u32[]{:S(2)}) collective-permute-start(f32[256,128]{1,0:T(8,128)S(1)} %dynamic-slice_bitcast_fusion.4), channel_id=1, source_target_pairs={{0,64},{4,12},{8,72},{12,4},{16,80},{20,28},{24,88},{28,20},{32,96... | collective-permute-start | bytes 393224 | tf_op jit(solution)/shard_map/ppermute | solution.py:30
  387.2 17.7 %collective-permute-start.33 = (f32[128,128]{1,0:T(8,128)S(1)}, f32[128,128]{1,0:T(8,128)S(1)}, u32[]{:S(2)}, u32[]{:S(2)}) collective-permute-start(f32[128,128]{1,0:T(8,128)S(1)} %dynamic-slice_bitcast_fusion.5), channel_id=1, source_target_pairs={{0,128},{4,20},{8,136},{12,28},{16,144},{20,4},{24,152},{28,12},{3... | collective-permute-start | bytes 196616 | tf_op jit(solution)/shard_map/ppermute | solution.py:30
  405.0 9.7 %collective-permute-start.34 = (f32[64,128]{1,0:T(8,128)S(1)}, f32[64,128]{1,0:T(8,128)S(1)}, u32[]{:S(2)}, u32[]{:S(2)}) collective-permute-start(f32[64,128]{1,0:T(8,128)S(1)} %dynamic-slice_bitcast_fusion.6), channel_id=1, source_target_pairs={{0,256},{4,36},{8,264},{12,44},{16,272},{20,52},{24,280},{28,60},{... | collective-permute-start | bytes 98312 | tf_op jit(solution)/shard_map/ppermute | solution.py:30
  (5 other events, 20.4 us)

commit v3 on v2

--- a/solution.py
+++ b/solution.py
@@ -70,6 +70,12 @@
     return x
 
 
+def sum_over(x, axis):
+    for k in range(bits(axis)):
+        x = x + swap(x, axis, k)
+    return x
+
+
 def column_sum(x, axis):
     for k in range(bits(axis)):
         other = swap(x, axis, k)
@@ -77,14 +83,6 @@
             other = other.reshape(2, 8, 8, -1).swapaxes(1, 2).reshape(x.shape)
         x = x + other
     return x
-
-
-def proto_sum(x):
-    parts = lax.all_gather(x, "proto", axis=0, tiled=False)
-    total = parts[0]
-    for j in range(1, parts.shape[0]):
-        total = total + parts[j]
-    return total
 
 
 def contract_rows(left, right):
@@ -144,7 +142,7 @@
         partial_cols = jnp.dot(row_scale * shift, base_local, precision=lax.Precision.HIGHEST)
         col_scale = 1.0 / column_sum(partial_cols, "dp")
         partial_rows = shift * jnp.dot(base_local, col_scale, precision=lax.Precision.HIGHEST)
-        row_scale = 1.0 / lax.psum(partial_rows, "proto")
+        row_scale = 1.0 / sum_over(partial_rows, "proto")
     row_factor = row_scale * shift
     student_factor = jnp.exp(student_local - student_top) / total
 
@@ -167,7 +165,7 @@
         ),
     )
     grad_logits = grad_logits.reshape(rows_here, -1)
-    grad_student = proto_sum(student_terms.reshape(rows_here, width))
+    grad_student = sum_over(student_terms.reshape(rows_here, width), "proto")
     grad_prototypes = scatter_blocks(
         lax.dot_general(
             grad_logits, student_emb, (((0,), (0,)), ((), ())), preferred_element_type=jnp.float32

time: 419 us -> 420 us (level)
  blocking collectives: 50.4 us -> 11.9 us
  starting transfers between devices: 155 us -> 177 us
  waiting for transfers between devices: 129 us -> 148 us
    psum x3 -> x0, blocking collectives: 25.4 us -> none  [per_device(): row_scale = 1.0 / lax.psum(partial_rows, 'proto')]
    ppermute x21 -> x29, waiting for transfers between devices: 53.7 us -> 74.9 us  [swap(): return lax.ppermute(x, axis, [(i, i ^ 1 << k) for i in range(n)])]
    ppermute x21 -> x29, starting transfers between devices: 91 us -> 112 us  [swap(): return lax.ppermute(x, axis, [(i, i ^ 1 << k) for i in range(n)])]
    all_gather x1 -> x0, blocking collectives: 13.1 us -> none  [proto_sum(): parts = lax.all_gather(x, 'proto', axis=0, tiled=False)]
  transfers between devices with their start and end apart: 35 -> 43, of which waited for: 34 -> 40; matrix products, arithmetic and copies ran while one was open for 0% -> 0% of each run, Pallas kernels for 0% -> 0%
where the time goes in v3:
time: 420 us; the launch traced here: 417 us
  starting transfers between devices  177 us (42%)
  waiting for transfers between devices  148 us (35%)
  matrix products  66.1 us (16%)
  blocking collectives  11.9 us (3%)
  other arithmetic  9.66 us (2%)
    ppermute x29, starting transfers between devices, swap(): return lax.ppermute(x, axis, [(i, i ^ 1 << k) for i in range(n)])  112 us
    ppermute x29, waiting for transfers between devices, swap(): return lax.ppermute(x, axis, [(i, i ^ 1 << k) for i in range(n)])  74.9 us
    ppermute x14, waiting for transfers between devices, core_swap(): return lax.ppermute(x, axis, pairs)  72.9 us
    ppermute x14, starting transfers between devices, core_swap(): return lax.ppermute(x, axis, pairs)  64.5 us
    dot_general x3, matrix products, per_device(): jnp.dot(base_local, col_scale, precision=lax.Precision.HIGHEST)  26.7 us
    dot_general x3, matrix products, per_device(): jnp.dot(row_scale * shift, base_local, precision=lax.Precision.HIGHEST)  21.2 us
    dot_general x6, matrix products, contract_rows(): lax.dot_general(left, right, (((1,), (1,)), ((), ())), preferred_element_...  13.3 us
    all_gather x1, blocking collectives, per_device(): lax.all_gather(jnp.stack([teacher_local, student_local, total_local]), 'p...  11.9 us
  transfers between devices with their start and end apart: 43, of which 40 were waited for; matrix products, arithmetic and copies ran while one was open for 0% of the time, Pallas kernels for 0%

profile of v3, /device:TPU:6, one launch (start us, length us, event | category | flops | bytes accessed | tf_op | source)
XLA Modules:
  0.0 417.4 jit_solution(1425298465203733156)
XLA Ops:
  1.4 10.9 %collective-permute-start = (bf16[64,128]{1,0:T(8,128)(2,1)S(1)}, bf16[64,128]{1,0:T(8,128)(2,1)S(1)}, u32[]{:S(2)}, u32[]{:S(2)}) collective-permute-start(bf16[64,128]{1,0:T(8,128)(2,1)S(1)} %get-tuple-element.160), channel_id=1, source_target_pairs={{0,256},{4,36},{8,264},{12,44},{16,272},{20,52},{24,280},{28,60},{... | collective-permute-start | bytes 49160 | tf_op jit(solution)/shard_map/ppermute | solution.py:30
  14.1 4.4 %collective-permute-start.1 = (bf16[128,128]{1,0:T(8,128)(2,1)S(1)}, bf16[128,128]{1,0:T(8,128)(2,1)S(1)}, u32[]{:S(2)}, u32[]{:S(2)}) collective-permute-start(bf16[128,128]{1,0:T(8,128)(2,1)S(1)} %bitcast.270), channel_id=1, source_target_pairs={{0,128},{4,20},{8,136},{12,28},{16,144},{20,4},{24,152},{28,12},{3... | collective-permute-start | bytes 98312 | tf_op jit(solution)/shard_map/ppermute | solution.py:30
  26.9 7.7 %collective-permute-start.3 = (bf16[512,128]{1,0:T(8,128)(2,1)S(1)}, bf16[512,128]{1,0:T(8,128)(2,1)S(1)}, u32[]{:S(2)}, u32[]{:S(2)}) collective-permute-start(bf16[512,128]{1,0:T(8,128)(2,1)S(1)} %bitcast.250), channel_id=1, source_target_pairs={{0,32},{4,260},{8,40},{12,268},{16,48},{20,276},{24,56},{28,284},{... | collective-permute-start | bytes 393224 | tf_op jit(solution)/shard_map/ppermute | solution.py:30
  38.6 4.9 %collective-permute-start.4 = (bf16[1024,128]{1,0:T(8,128)(2,1)S(1)}, bf16[1024,128]{1,0:T(8,128)(2,1)S(1)}, u32[]{:S(2)}, u32[]{:S(2)}) collective-permute-start(bf16[1024,128]{1,0:T(8,128)(2,1)S(1)} %bitcast.242), channel_id=1, source_target_pairs={{0,16},{4,132},{8,24},{12,140},{16,0},{20,148},{24,8},{28,156},{32... | collective-permute-start | bytes 786440 | tf_op jit(solution)/shard_map/ppermute | solution.py:30
  43.7 7.0 %collective-permute-done.4 = bf16[1024,128]{1,0:T(8,128)(2,1)S(1)} collective-permute-done((bf16[1024,128]{1,0:T(8,128)(2,1)S(1)}, bf16[1024,128]{1,0:T(8,128)(2,1)S(1)}, u32[]{:S(2)}, u32[]{:S(2)}) %collective-permute-start.4) | collective-permute-done | bytes 262176 | tf_op jit(solution)/shard_map/ppermute | solution.py:30
  52.9 8.9 %collective-permute-done.5 = bf16[2048,128]{1,0:T(8,128)(2,1)S(1)} collective-permute-done((bf16[2048,128]{1,0:T(8,128)(2,1)S(1)}, bf16[2048,128]{1,0:T(8,128)(2,1)S(1)}, u32[]{:S(2)}, u32[]{:S(2)}) %collective-permute-start.5) | collective-permute-done | bytes 524320 | tf_op jit(solution)/shard_map/ppermute | solution.py:30
  68.0 6.9 %while.37 = (s32[]{:T(128)}, f32[2,128,8192]{2,1,0:T(8,128)}, f32[2,128]{1,0:T(2,128)S(1)}, bf16[2,128,128]{2,1,0:T(8,128)(2,1)S(1)}, bf16[8192,128]{1,0:T(8,128)(2,1)S(1)}, /*index=5*/s32[]{:T(128)}, s32[]{:T(128)}) while((s32[]{:T(128)}, f32[2,128,8192]{2,1,0:T(8,128)}, f32[2,128]{1,0:T(2,128)S(1)}, bf16[2,128,128]{2,1,0:T(8,128)(2,1)S(1)}, ...), condition=%wide.region_2.3_spmd, body=%wide.region_0.2_spmd.sunk | while | flops 271581056 | bytes 14715477 | solution.py:115
  78.2 11.9 %all-gather.1 = f32[4,3,256]{2,1,0:T(4,128)S(1)} all-gather(f32[1,3,256]{2,1,0:T(4,128)S(1)} %maximum_bitcast_fusion), channel_id=2, replica_groups=mesh['dp'=128,'proto'=4] {'proto'}, dimensions={0}, use_global_device_ids=true | all-gather | bytes 15360 | tf_op jit(solution)/shard_map/all_gather | solution.py:131
  90.2 6.3 %fusion.33 = f32[1,8192,1]{1,0,2:T(1,128)S(1)} fusion(f32[2,128,1]{1,2,0:T(1,128)S(1)} %bitcast.280, f32[2,128,8192]{2,1,0:T(8,128)} %get-tuple-element.369), kind=kOutput, calls=%fused_computation.88 | convolution fusion | flops 25165824 | bytes 8422400 | tf_op jit(solution)/shard_map/dot_general | solution.py:142
  112.4 7.1 %collective-permute-start.10 = (f32[8192]{0:T(1024)S(1)}, f32[8192]{0:T(1024)S(1)}, u32[]{:S(2)}, u32[]{:S(2)}) collective-permute-start(f32[8192]{0:T(1024)S(1)} %add.226), channel_id=1, source_target_pairs={{0,32},{4,36},{8,40},{12,44},{16,48},{20,52},{24,56},{28,60},{32,0... | collective-permute-start | bytes 98312 | tf_op jit(solution)/shard_map/ppermute | solution.py:17
  128.2 4.6 %collective-permute-start.12 = (f32[8192]{0:T(1024)S(1)}, f32[8192]{0:T(1024)S(1)}, u32[]{:S(2)}, u32[]{:S(2)}) collective-permute-start(f32[8192]{0:T(1024)S(1)} %add.228), channel_id=1, source_target_pairs={{0,128},{4,132},{8,136},{12,140},{16,144},{20,148},{24,152},{28,15... | collective-permute-start | bytes 98312 | tf_op jit(solution)/shard_map/ppermute | solution.py:17
  134.9 9.1 %collective-permute-start.13 = (f32[8192]{0:T(1024)S(1)}, f32[8192]{0:T(1024)S(1)}, u32[]{:S(2)}, u32[]{:S(2)}) collective-permute-start(f32[8192]{0:T(1024)S(1)} %add.229), channel_id=1, source_target_pairs={{0,256},{4,260},{8,264},{12,268},{16,272},{20,276},{24,280},{28,28... | collective-permute-start | bytes 98312 | tf_op jit(solution)/shard_map/ppermute | solution.py:17
  145.9 8.9 %fusion.34 = f32[1,256]{1,0:T(1,128)S(1)} fusion(f32[256,8192]{1,0:T(8,128)} %bitcast.223, f32[8192,1]{0,1:T(1,128)S(1)} %bitcast.267), kind=kOutput, calls=%fused_computation.89 | convolution fusion | flops 25165824 | bytes 8422400 | tf_op jit(solution)/shard_map/dot_general | solution.py:144
  167.2 7.4 %fusion.35 = f32[1,8192]{1,0:T(1,128)S(1)} fusion(f32[256,1]{0,1:T(1,128)S(1)} %bitcast.283, f32[256,8192]{1,0:T(8,128)} %bitcast.224), kind=kOutput, calls=%fused_computation.90 | convolution fusion | flops 25165824 | bytes 8422400 | tf_op jit(solution)/shard_map/dot_general | solution.py:142
  190.4 6.9 %collective-permute-start.19 = (f32[8192]{0:T(1024)S(1)}, f32[8192]{0:T(1024)S(1)}, u32[]{:S(2)}, u32[]{:S(2)}) collective-permute-start(f32[8192]{0:T(1024)S(1)} %add.235), channel_id=1, source_target_pairs={{0,32},{4,36},{8,40},{12,44},{16,48},{20,52},{24,56},{28,60},{32,0... | collective-permute-start | bytes 98312 | tf_op jit(solution)/shard_map/ppermute | solution.py:17
  206.1 4.7 %collective-permute-start.21 = (f32[8192]{0:T(1024)S(1)}, f32[8192]{0:T(1024)S(1)}, u32[]{:S(2)}, u32[]{:S(2)}) collective-permute-start(f32[8192]{0:T(1024)S(1)} %add.237), channel_id=1, source_target_pairs={{0,128},{4,132},{8,136},{12,140},{16,144},{20,148},{24,152},{28,15... | collective-permute-start | bytes 98312 | tf_op jit(solution)/shard_map/ppermute | solution.py:17
  212.8 8.1 %collective-permute-start.22 = (f32[8192]{0:T(1024)S(1)}, f32[8192]{0:T(1024)S(1)}, u32[]{:S(2)}, u32[]{:S(2)}) collective-permute-start(f32[8192]{0:T(1024)S(1)} %add.238), channel_id=1, source_target_pairs={{0,256},{4,260},{8,264},{12,268},{16,272},{20,276},{24,280},{28,28... | collective-permute-start | bytes 98312 | tf_op jit(solution)/shard_map/ppermute | solution.py:17
  222.8 8.9 %fusion.36 = f32[1,256]{1,0:T(1,128)S(1)} fusion(f32[256,8192]{1,0:T(8,128)} %bitcast.225, f32[8192,1]{0,1:T(1,128)S(1)} %bitcast.268), kind=kOutput, calls=%fused_computation.91 | convolution fusion | flops 25165824 | bytes 8422400 | tf_op jit(solution)/shard_map/dot_general | solution.py:144
  244.1 7.4 %fusion.37 = f32[1,8192]{1,0:T(1,128)S(1)} fusion(f32[256,1]{0,1:T(1,128)S(1)} %bitcast.284, f32[256,8192]{1,0:T(8,128)} %bitcast.226), kind=kOutput, calls=%fused_computation.92 | convolution fusion | flops 25165824 | bytes 8422400 | tf_op jit(solution)/shard_map/dot_general | solution.py:142
  267.3 6.8 %collective-permute-start.28 = (f32[8192]{0:T(1024)S(1)}, f32[8192]{0:T(1024)S(1)}, u32[]{:S(2)}, u32[]{:S(2)}) collective-permute-start(f32[8192]{0:T(1024)S(1)} %add.244), channel_id=1, source_target_pairs={{0,32},{4,36},{8,40},{12,44},{16,48},{20,52},{24,56},{28,60},{32,0... | collective-permute-start | bytes 98312 | tf_op jit(solution)/shard_map/ppermute | solution.py:17
  282.8 4.6 %collective-permute-start.30 = (f32[8192]{0:T(1024)S(1)}, f32[8192]{0:T(1024)S(1)}, u32[]{:S(2)}, u32[]{:S(2)}) collective-permute-start(f32[8192]{0:T(1024)S(1)} %add.246), channel_id=1, source_target_pairs={{0,128},{4,132},{8,136},{12,140},{16,144},{20,148},{24,152},{28,15... | collective-permute-start | bytes 98312 | tf_op jit(solution)/shard_map/ppermute | solution.py:17
  289.5 8.0 %collective-permute-start.31 = (f32[8192]{0:T(1024)S(1)}, f32[8192]{0:T(1024)S(1)}, u32[]{:S(2)}, u32[]{:S(2)}) collective-permute-start(f32[8192]{0:T(1024)S(1)} %add.247), channel_id=1, source_target_pairs={{0,256},{4,260},{8,264},{12,268},{16,272},{20,276},{24,280},{28,28... | collective-permute-start | bytes 98312 | tf_op jit(solution)/shard_map/ppermute | solution.py:17
  299.4 8.9 %fusion.38 = f32[1,256]{1,0:T(1,128)S(1)} fusion(f32[256,8192]{1,0:T(8,128)} %bitcast.227, f32[8192,1]{0,1:T(1,128)S(1)} %bitcast.260), kind=kOutput, calls=%fused_computation.93 | convolution fusion | flops 25165824 | bytes 8422400 | tf_op jit(solution)/shard_map/dot_general | solution.py:144
  320.8 11.7 %while.38 = (s32[]{:T(128)}, bf16[2,128,8192]{2,1,0:T(8,128)(2,1)}, f32[2,128,128]{2,1,0:T(8,128)S(1)}, bf16[2,128,128]{2,1,0:T(8,128)(2,1)S(1)}, bf16[8192,128]...) while((s32[]{:T(128)}, bf16[2,128,8192]{2,1,0:T(8,128)(2,1)}, ...), condition=%wide.region_8.9_spmd, body=%wide.region_7.8_spmd.sunk | while | flops 544227328 | bytes 14816889 | solution.py:157
  320.8 5.0 %bitcast_dynamic-update-slice_fusion.18 = (bf16[2,128,8192]{2,1,0:T(8,128)(2,1)}, bf16[128,8192]{1,0:T(8,128)(2,1)S(1)}) fusion(bf16[2,128,8192]{2,1,0:T(8,128)(2,1)} %get-tuple-element.373, s32[]{:T(128)} %get-tuple-element.372, f32[8192]{0:T(1024)S(1)} %get-tuple-element.392, f32[2,128,8192]{2,1,0:T(8,128)} %get-tuple-element.391, ...), kind=kOutput, calls=%fused_computation.18.clone.1 | convolution fusion | flops 275775488 | bytes 10553856 | tf_op jit(solution)/shard_map/while/body/eval_jaxpr/dot_general | solution.py:89
  326.6 5.1 %bitcast_dynamic-update-slice_fusion.18 = (bf16[2,128,8192]{2,1,0:T(8,128)(2,1)}, bf16[128,8192]{1,0:T(8,128)(2,1)S(1)}) fusion(bf16[2,128,8192]{2,1,0:T(8,128)(2,1)} %get-tuple-element.373, s32[]{:T(128)} %get-tuple-element.372, f32[8192]{0:T(1024)S(1)} %get-tuple-element.392, f32[2,128,8192]{2,1,0:T(8,128)} %get-tuple-element.391, ...), kind=kOutput, calls=%fused_computation.18.clone.1 | convolution fusion | flops 275775488 | bytes 10553856 | tf_op jit(solution)/shard_map/while/body/eval_jaxpr/dot_general | solution.py:89
  344.7 14.8 %collective-permute-done.35 = f32[2048,128]{1,0:T(8,128)S(1)} collective-permute-done((f32[2048,128]{1,0:T(8,128)S(1)}, f32[2048,128]{1,0:T(8,128)S(1)}, u32[]{:S(2)}, u32[]{:S(2)}) %collective-permute-start.35) | collective-permute-done | bytes 1048608 | tf_op jit(solution)/shard_map/ppermute | solution.py:30
  362.3 14.4 %collective-permute-done.36 = f32[1024,128]{1,0:T(8,128)S(1)} collective-permute-done((f32[1024,128]{1,0:T(8,128)S(1)}, f32[1024,128]{1,0:T(8,128)S(1)}, u32[]{:S(2)}, u32[]{:S(2)}) %collective-permute-start.36) | collective-permute-done | bytes 524320 | tf_op jit(solution)/shard_map/ppermute | solution.py:30
  376.8 6.9 %collective-permute-start.37 = (f32[512,128]{1,0:T(8,128)S(1)}, f32[512,128]{1,0:T(8,128)S(1)}, u32[]{:S(2)}, u32[]{:S(2)}) collective-permute-start(f32[512,128]{1,0:T(8,128)S(1)} %dynamic-slice_bitcast_fusion.3), channel_id=1, source_target_pairs={{0,32},{4,260},{8,40},{12,268},{16,48},{20,276},{24,56},{28,284},{... | collective-permute-start | bytes 786440 | tf_op jit(solution)/shard_map/ppermute | solution.py:30
  383.7 8.1 %collective-permute-done.37 = f32[512,128]{1,0:T(8,128)S(1)} collective-permute-done((f32[512,128]{1,0:T(8,128)S(1)}, f32[512,128]{1,0:T(8,128)S(1)}, u32[]{:S(2)}, u32[]{:S(2)}) %collective-permute-start.37) | collective-permute-done | bytes 262176 | tf_op jit(solution)/shard_map/ppermute | solution.py:30
  398.8 4.6 %collective-permute-start.39 = (f32[128,128]{1,0:T(8,128)S(1)}, f32[128,128]{1,0:T(8,128)S(1)}, u32[]{:S(2)}, u32[]{:S(2)}) collective-permute-start(f32[128,128]{1,0:T(8,128)S(1)} %dynamic-slice_bitcast_fusion.5), channel_id=1, source_target_pairs={{0,128},{4,20},{8,136},{12,28},{16,144},{20,4},{24,152},{28,12},{3... | collective-permute-start | bytes 196616 | tf_op jit(solution)/shard_map/ppermute | solution.py:30
  406.9 8.0 %collective-permute-start.40 = (f32[64,128]{1,0:T(8,128)S(1)}, f32[64,128]{1,0:T(8,128)S(1)}, u32[]{:S(2)}, u32[]{:S(2)}) collective-permute-start(f32[64,128]{1,0:T(8,128)S(1)} %dynamic-slice_bitcast_fusion.6), channel_id=1, source_target_pairs={{0,256},{4,36},{8,264},{12,44},{16,272},{20,52},{24,280},{28,60},{... | collective-permute-start | bytes 98312 | tf_op jit(solution)/shard_map/ppermute | solution.py:30
  (179 shorter events, 188.6 us)
Async XLA Ops:
  1.4 12.6 %collective-permute-start = (bf16[64,128]{1,0:T(8,128)(2,1)S(1)}, bf16[64,128]{1,0:T(8,128)(2,1)S(1)}, u32[]{:S(2)}, u32[]{:S(2)}) collective-permute-start(bf16[64,128]{1,0:T(8,128)(2,1)S(1)} %get-tuple-element.160), channel_id=1, source_target_pairs={{0,256},{4,36},{8,264},{12,44},{16,272},{20,52},{24,280},{28,60},{... | collective-permute-start | bytes 49160 | tf_op jit(solution)/shard_map/ppermute | solution.py:30
  14.1 6.7 %collective-permute-start.1 = (bf16[128,128]{1,0:T(8,128)(2,1)S(1)}, bf16[128,128]{1,0:T(8,128)(2,1)S(1)}, u32[]{:S(2)}, u32[]{:S(2)}) collective-permute-start(bf16[128,128]{1,0:T(8,128)(2,1)S(1)} %bitcast.270), channel_id=1, source_target_pairs={{0,128},{4,20},{8,136},{12,28},{16,144},{20,4},{24,152},{28,12},{3... | collective-permute-start | bytes 98312 | tf_op jit(solution)/shard_map/ppermute | solution.py:30
  20.8 6.1 %collective-permute-start.2 = (bf16[256,128]{1,0:T(8,128)(2,1)S(1)}, bf16[256,128]{1,0:T(8,128)(2,1)S(1)}, u32[]{:S(2)}, u32[]{:S(2)}) collective-permute-start(bf16[256,128]{1,0:T(8,128)(2,1)S(1)} %bitcast.258), channel_id=1, source_target_pairs={{0,64},{4,12},{8,72},{12,4},{16,80},{20,28},{24,88},{28,20},{32,96... | collective-permute-start | bytes 196616 | tf_op jit(solution)/shard_map/ppermute | solution.py:30
  26.9 11.6 %collective-permute-start.3 = (bf16[512,128]{1,0:T(8,128)(2,1)S(1)}, bf16[512,128]{1,0:T(8,128)(2,1)S(1)}, u32[]{:S(2)}, u32[]{:S(2)}) collective-permute-start(bf16[512,128]{1,0:T(8,128)(2,1)S(1)} %bitcast.250), channel_id=1, source_target_pairs={{0,32},{4,260},{8,40},{12,268},{16,48},{20,276},{24,56},{28,284},{... | collective-permute-start | bytes 393224 | tf_op jit(solution)/shard_map/ppermute | solution.py:30
  38.6 12.1 %collective-permute-start.4 = (bf16[1024,128]{1,0:T(8,128)(2,1)S(1)}, bf16[1024,128]{1,0:T(8,128)(2,1)S(1)}, u32[]{:S(2)}, u32[]{:S(2)}) collective-permute-start(bf16[1024,128]{1,0:T(8,128)(2,1)S(1)} %bitcast.242), channel_id=1, source_target_pairs={{0,16},{4,132},{8,24},{12,140},{16,0},{20,148},{24,8},{28,156},{32... | collective-permute-start | bytes 786440 | tf_op jit(solution)/shard_map/ppermute | solution.py:30
  50.7 11.1 %collective-permute-start.5 = (bf16[2048,128]{1,0:T(8,128)(2,1)S(1)}, bf16[2048,128]{1,0:T(8,128)(2,1)S(1)}, u32[]{:S(2)}, u32[]{:S(2)}) collective-permute-start(bf16[2048,128]{1,0:T(8,128)(2,1)S(1)} %bitcast.240), channel_id=1, source_target_pairs={{0,8},{4,68},{8,0},{12,76},{16,24},{20,84},{24,16},{28,92},{32,40}... | collective-permute-start | bytes 1572872 | tf_op jit(solution)/shard_map/ppermute | solution.py:30
  99.8 5.8 %collective-permute-start.8 = (f32[8192]{0:T(1024)S(1)}, f32[8192]{0:T(1024)S(1)}, u32[]{:S(2)}, u32[]{:S(2)}) collective-permute-start(f32[8192]{0:T(1024)S(1)} %add.224), channel_id=1, source_target_pairs={{0,8},{4,12},{8,0},{12,4},{16,24},{20,28},{24,16},{28,20},{32,40},... | collective-permute-start | bytes 98312 | tf_op jit(solution)/shard_map/ppermute | solution.py:17
  105.6 6.8 %collective-permute-start.9 = (f32[8192]{0:T(1024)S(1)}, f32[8192]{0:T(1024)S(1)}, u32[]{:S(2)}, u32[]{:S(2)}) collective-permute-start(f32[8192]{0:T(1024)S(1)} %add.225), channel_id=1, source_target_pairs={{0,16},{4,20},{8,24},{12,28},{16,0},{20,4},{24,8},{28,12},{32,48},... | collective-permute-start | bytes 98312 | tf_op jit(solution)/shard_map/ppermute | solution.py:17
  112.4 9.9 %collective-permute-start.10 = (f32[8192]{0:T(1024)S(1)}, f32[8192]{0:T(1024)S(1)}, u32[]{:S(2)}, u32[]{:S(2)}) collective-permute-start(f32[8192]{0:T(1024)S(1)} %add.226), channel_id=1, source_target_pairs={{0,32},{4,36},{8,40},{12,44},{16,48},{20,52},{24,56},{28,60},{32,0... | collective-permute-start | bytes 98312 | tf_op jit(solution)/shard_map/ppermute | solution.py:17
  128.2 6.7 %collective-permute-start.12 = (f32[8192]{0:T(1024)S(1)}, f32[8192]{0:T(1024)S(1)}, u32[]{:S(2)}, u32[]{:S(2)}) collective-permute-start(f32[8192]{0:T(1024)S(1)} %add.228), channel_id=1, source_target_pairs={{0,128},{4,132},{8,136},{12,140},{16,144},{20,148},{24,152},{28,15... | collective-permute-start | bytes 98312 | tf_op jit(solution)/shard_map/ppermute | solution.py:17
  134.9 11.0 %collective-permute-start.13 = (f32[8192]{0:T(1024)S(1)}, f32[8192]{0:T(1024)S(1)}, u32[]{:S(2)}, u32[]{:S(2)}) collective-permute-start(f32[8192]{0:T(1024)S(1)} %add.229), channel_id=1, source_target_pairs={{0,256},{4,260},{8,264},{12,268},{16,272},{20,276},{24,280},{28,28... | collective-permute-start | bytes 98312 | tf_op jit(solution)/shard_map/ppermute | solution.py:17
  160.2 7.0 %collective-permute-start.15 = (f32[256]{0:T(256)S(1)}, f32[256]{0:T(256)S(1)}, u32[]{:S(2)}, u32[]{:S(2)}) collective-permute-start(f32[256]{0:T(256)S(1)} %add.231), channel_id=1, source_target_pairs={{0,2},{1,3},{2,0},{3,1},{4,6},{5,7},{6,4},{7,5},{8,10},{9,11},{10,... | collective-permute-start | bytes 3080 | tf_op jit(solution)/shard_map/ppermute | solution.py:17
  183.7 6.7 %collective-permute-start.18 = (f32[8192]{0:T(1024)S(1)}, f32[8192]{0:T(1024)S(1)}, u32[]{:S(2)}, u32[]{:S(2)}) collective-permute-start(f32[8192]{0:T(1024)S(1)} %add.234), channel_id=1, source_target_pairs={{0,16},{4,20},{8,24},{12,28},{16,0},{20,4},{24,8},{28,12},{32,48},... | collective-permute-start | bytes 98312 | tf_op jit(solution)/shard_map/ppermute | solution.py:17
  190.4 9.9 %collective-permute-start.19 = (f32[8192]{0:T(1024)S(1)}, f32[8192]{0:T(1024)S(1)}, u32[]{:S(2)}, u32[]{:S(2)}) collective-permute-start(f32[8192]{0:T(1024)S(1)} %add.235), channel_id=1, source_target_pairs={{0,32},{4,36},{8,40},{12,44},{16,48},{20,52},{24,56},{28,60},{32,0... | collective-permute-start | bytes 98312 | tf_op jit(solution)/shard_map/ppermute | solution.py:17
  206.1 6.7 %collective-permute-start.21 = (f32[8192]{0:T(1024)S(1)}, f32[8192]{0:T(1024)S(1)}, u32[]{:S(2)}, u32[]{:S(2)}) collective-permute-start(f32[8192]{0:T(1024)S(1)} %add.237), channel_id=1, source_target_pairs={{0,128},{4,132},{8,136},{12,140},{16,144},{20,148},{24,152},{28,15... | collective-permute-start | bytes 98312 | tf_op jit(solution)/shard_map/ppermute | solution.py:17
  212.8 10.0 %collective-permute-start.22 = (f32[8192]{0:T(1024)S(1)}, f32[8192]{0:T(1024)S(1)}, u32[]{:S(2)}, u32[]{:S(2)}) collective-permute-start(f32[8192]{0:T(1024)S(1)} %add.238), channel_id=1, source_target_pairs={{0,256},{4,260},{8,264},{12,268},{16,272},{20,276},{24,280},{28,28... | collective-permute-start | bytes 98312 | tf_op jit(solution)/shard_map/ppermute | solution.py:17
  237.2 7.0 %collective-permute-start.24 = (f32[256]{0:T(256)S(1)}, f32[256]{0:T(256)S(1)}, u32[]{:S(2)}, u32[]{:S(2)}) collective-permute-start(f32[256]{0:T(256)S(1)} %add.240), channel_id=1, source_target_pairs={{0,2},{1,3},{2,0},{3,1},{4,6},{5,7},{6,4},{7,5},{8,10},{9,11},{10,... | collective-permute-start | bytes 3080 | tf_op jit(solution)/shard_map/ppermute | solution.py:17
  254.8 5.8 %collective-permute-start.26 = (f32[8192]{0:T(1024)S(1)}, f32[8192]{0:T(1024)S(1)}, u32[]{:S(2)}, u32[]{:S(2)}) collective-permute-start(f32[8192]{0:T(1024)S(1)} %add.242), channel_id=1, source_target_pairs={{0,8},{4,12},{8,0},{12,4},{16,24},{20,28},{24,16},{28,20},{32,40},... | collective-permute-start | bytes 98312 | tf_op jit(solution)/shard_map/ppermute | solution.py:17
  260.6 6.7 %collective-permute-start.27 = (f32[8192]{0:T(1024)S(1)}, f32[8192]{0:T(1024)S(1)}, u32[]{:S(2)}, u32[]{:S(2)}) collective-permute-start(f32[8192]{0:T(1024)S(1)} %add.243), channel_id=1, source_target_pairs={{0,16},{4,20},{8,24},{12,28},{16,0},{20,4},{24,8},{28,12},{32,48},... | collective-permute-start | bytes 98312 | tf_op jit(solution)/shard_map/ppermute | solution.py:17
  267.3 9.7 %collective-permute-start.28 = (f32[8192]{0:T(1024)S(1)}, f32[8192]{0:T(1024)S(1)}, u32[]{:S(2)}, u32[]{:S(2)}) collective-permute-start(f32[8192]{0:T(1024)S(1)} %add.244), channel_id=1, source_target_pairs={{0,32},{4,36},{8,40},{12,44},{16,48},{20,52},{24,56},{28,60},{32,0... | collective-permute-start | bytes 98312 | tf_op jit(solution)/shard_map/ppermute | solution.py:17
  282.8 6.7 %collective-permute-start.30 = (f32[8192]{0:T(1024)S(1)}, f32[8192]{0:T(1024)S(1)}, u32[]{:S(2)}, u32[]{:S(2)}) collective-permute-start(f32[8192]{0:T(1024)S(1)} %add.246), channel_id=1, source_target_pairs={{0,128},{4,132},{8,136},{12,140},{16,144},{20,148},{24,152},{28,15... | collective-permute-start | bytes 98312 | tf_op jit(solution)/shard_map/ppermute | solution.py:17
  289.5 9.9 %collective-permute-start.31 = (f32[8192]{0:T(1024)S(1)}, f32[8192]{0:T(1024)S(1)}, u32[]{:S(2)}, u32[]{:S(2)}) collective-permute-start(f32[8192]{0:T(1024)S(1)} %add.247), channel_id=1, source_target_pairs={{0,256},{4,260},{8,264},{12,268},{16,272},{20,276},{24,280},{28,28... | collective-permute-start | bytes 98312 | tf_op jit(solution)/shard_map/ppermute | solution.py:17
  313.8 7.0 %collective-permute-start.33 = (f32[256]{0:T(256)S(1)}, f32[256]{0:T(256)S(1)}, u32[]{:S(2)}, u32[]{:S(2)}) collective-permute-start(f32[256]{0:T(256)S(1)} %add.249), channel_id=1, source_target_pairs={{0,2},{1,3},{2,0},{3,1},{4,6},{5,7},{6,4},{7,5},{8,10},{9,11},{10,... | collective-permute-start | bytes 3080 | tf_op jit(solution)/shard_map/ppermute | solution.py:17
  336.2 6.1 %collective-permute-start.34 = (f32[4096,128]{1,0:T(8,128)S(1)}, f32[4096,128]{1,0:T(8,128)S(1)}, u32[]{:S(2)}, u32[]{:S(2)}) collective-permute-start(f32[4096,128]{1,0:T(8,128)S(1)} %get-tuple-element.169), channel_id=1, source_target_pairs={{0,4},{4,0},{8,12},{12,8},{16,20},{20,16},{24,28},{28,24},{32,36},... | collective-permute-start | bytes 6291464 | tf_op jit(solution)/shard_map/ppermute | solution.py:30
  342.8 16.7 %collective-permute-start.35 = (f32[2048,128]{1,0:T(8,128)S(1)}, f32[2048,128]{1,0:T(8,128)S(1)}, u32[]{:S(2)}, u32[]{:S(2)}) collective-permute-start(f32[2048,128]{1,0:T(8,128)S(1)} %dynamic-slice_bitcast_fusion.1), channel_id=1, source_target_pairs={{0,8},{4,68},{8,0},{12,76},{16,24},{20,84},{24,16},{28,92},{32,40}... | collective-permute-start | bytes 3145736 | tf_op jit(solution)/shard_map/ppermute | solution.py:30
  359.7 17.0 %collective-permute-start.36 = (f32[1024,128]{1,0:T(8,128)S(1)}, f32[1024,128]{1,0:T(8,128)S(1)}, u32[]{:S(2)}, u32[]{:S(2)}) collective-permute-start(f32[1024,128]{1,0:T(8,128)S(1)} %dynamic-slice_bitcast_fusion.2), channel_id=1, source_target_pairs={{0,16},{4,132},{8,24},{12,140},{16,0},{20,148},{24,8},{28,156},{32... | collective-permute-start | bytes 1572872 | tf_op jit(solution)/shard_map/ppermute | solution.py:30
  376.8 15.0 %collective-permute-start.37 = (f32[512,128]{1,0:T(8,128)S(1)}, f32[512,128]{1,0:T(8,128)S(1)}, u32[]{:S(2)}, u32[]{:S(2)}) collective-permute-start(f32[512,128]{1,0:T(8,128)S(1)} %dynamic-slice_bitcast_fusion.3), channel_id=1, source_target_pairs={{0,32},{4,260},{8,40},{12,268},{16,48},{20,276},{24,56},{28,284},{... | collective-permute-start | bytes 786440 | tf_op jit(solution)/shard_map/ppermute | solution.py:30
  391.9 6.9 %collective-permute-start.38 = (f32[256,128]{1,0:T(8,128)S(1)}, f32[256,128]{1,0:T(8,128)S(1)}, u32[]{:S(2)}, u32[]{:S(2)}) collective-permute-start(f32[256,128]{1,0:T(8,128)S(1)} %dynamic-slice_bitcast_fusion.4), channel_id=1, source_target_pairs={{0,64},{4,12},{8,72},{12,4},{16,80},{20,28},{24,88},{28,20},{32,96... | collective-permute-start | bytes 393224 | tf_op jit(solution)/shard_map/ppermute | solution.py:30
  395.3 8.1 %collective-permute-start.41 = (f32[256,128]{1,0:T(8,128)S(1)}, f32[256,128]{1,0:T(8,128)S(1)}, u32[]{:S(2)}, u32[]{:S(2)}) collective-permute-start(f32[256,128]{1,0:T(8,128)S(1)} %bitcast.269), channel_id=1, source_target_pairs={{0,1},{1,0},{2,3},{3,2},{4,5},{5,4},{6,7},{7,6},{8,9},{9,8},{10,11... | collective-permute-start | bytes 393224 | tf_op jit(solution)/shard_map/ppermute | solution.py:17
  398.8 8.1 %collective-permute-start.39 = (f32[128,128]{1,0:T(8,128)S(1)}, f32[128,128]{1,0:T(8,128)S(1)}, u32[]{:S(2)}, u32[]{:S(2)}) collective-permute-start(f32[128,128]{1,0:T(8,128)S(1)} %dynamic-slice_bitcast_fusion.5), channel_id=1, source_target_pairs={{0,128},{4,20},{8,136},{12,28},{16,144},{20,4},{24,152},{28,12},{3... | collective-permute-start | bytes 196616 | tf_op jit(solution)/shard_map/ppermute | solution.py:30
  403.4 11.4 %collective-permute-start.42 = (f32[256,128]{1,0:T(8,128)S(1)}, f32[256,128]{1,0:T(8,128)S(1)}, u32[]{:S(2)}, u32[]{:S(2)}) collective-permute-start(f32[256,128]{1,0:T(8,128)S(1)} %bitcast_add_fusion.6), channel_id=1, source_target_pairs={{0,2},{1,3},{2,0},{3,1},{4,6},{5,7},{6,4},{7,5},{8,10},{9,11},{10,... | collective-permute-start | bytes 393224 | tf_op jit(solution)/shard_map/ppermute | solution.py:17
  406.9 9.9 %collective-permute-start.40 = (f32[64,128]{1,0:T(8,128)S(1)}, f32[64,128]{1,0:T(8,128)S(1)}, u32[]{:S(2)}, u32[]{:S(2)}) collective-permute-start(f32[64,128]{1,0:T(8,128)S(1)} %dynamic-slice_bitcast_fusion.6), channel_id=1, source_target_pairs={{0,256},{4,36},{8,264},{12,44},{16,272},{20,52},{24,280},{28,60},{... | collective-permute-start | bytes 98312 | tf_op jit(solution)/shard_map/ppermute | solution.py:30
  (13 other events, 64.7 us)

commit v4 on v3

--- a/solution.py
+++ b/solution.py
@@ -139,9 +139,9 @@
     row_scale = jnp.ones((rows_here,), jnp.float32)
     col_scale = jnp.ones((base_local.shape[1],), jnp.float32)
     for step in range(ITERS):
-        partial_cols = jnp.dot(row_scale * shift, base_local, precision=lax.Precision.HIGHEST)
+        partial_cols = jnp.sum((row_scale * shift)[:, None] * base_local, axis=0)
         col_scale = 1.0 / column_sum(partial_cols, "dp")
-        partial_rows = shift * jnp.dot(base_local, col_scale, precision=lax.Precision.HIGHEST)
+        partial_rows = shift * jnp.sum(base_local * col_scale[None, :], axis=1)
         row_scale = 1.0 / sum_over(partial_rows, "proto")
     row_factor = row_scale * shift
     student_factor = jnp.exp(student_local - student_top) / total

time: 420 us -> 397 us (0.945)
  matrix products: 66.1 us -> 18.2 us
  other arithmetic: 9.66 us -> 35.1 us
    dot_general x6 -> x0, matrix products: 47.8 us -> none  [the longest x3 26.7 us: per_device(): jnp.dot(base_local, col_scale, precision=lax.Precision.HIGHEST)]
    reduce_sum x0 -> x6, other arithmetic: none -> 25.5 us  [the longest x3 13 us: per_device(): partial_cols = jnp.sum((row_scale * shift)[:, None] * base_local, axis=0)]
where the time goes in v4:
time: 397 us; the launch traced here: 395 us
  starting transfers between devices  177 us (45%)
  waiting for transfers between devices  148 us (37%)
  other arithmetic  35.1 us (9%)
  matrix products  18.2 us (5%)
  blocking collectives  11.9 us (3%)
    ppermute x29, starting transfers between devices, swap(): return lax.ppermute(x, axis, [(i, i ^ 1 << k) for i in range(n)])  112 us
    ppermute x29, waiting for transfers between devices, swap(): return lax.ppermute(x, axis, [(i, i ^ 1 << k) for i in range(n)])  74.9 us
    ppermute x14, waiting for transfers between devices, core_swap(): return lax.ppermute(x, axis, pairs)  72.7 us
    ppermute x14, starting transfers between devices, core_swap(): return lax.ppermute(x, axis, pairs)  64.5 us
    dot_general x6, matrix products, contract_rows(): lax.dot_general(left, right, (((1,), (1,)), ((), ())), preferred_element_...  13.3 us
    reduce_sum x3, other arithmetic, per_device(): partial_cols = jnp.sum((row_scale * shift)[:, None] * base_local, axis=0)  13 us
    reduce_sum x3, other arithmetic, per_device(): partial_rows = shift * jnp.sum(base_local * col_scale[None, :], axis=1)  12.5 us
    all_gather x1, blocking collectives, per_device(): lax.all_gather(jnp.stack([teacher_local, student_local, total_local]), 'p...  11.9 us
  transfers between devices with their start and end apart: 43, of which 40 were waited for; matrix products, arithmetic and copies ran while one was open for 0% of the time, Pallas kernels for 0%

profile of v4, /device:TPU:6, one launch (start us, length us, event | category | flops | bytes accessed | tf_op | source)
XLA Modules:
  0.0 395.0 jit_solution(7185691045061035947)
XLA Ops:
  1.4 10.9 %collective-permute-start = (bf16[64,128]{1,0:T(8,128)(2,1)S(1)}, bf16[64,128]{1,0:T(8,128)(2,1)S(1)}, u32[]{:S(2)}, u32[]{:S(2)}) collective-permute-start(bf16[64,128]{1,0:T(8,128)(2,1)S(1)} %get-tuple-element.160), channel_id=1, source_target_pairs={{0,256},{4,36},{8,264},{12,44},{16,272},{20,52},{24,280},{28,60},{... | collective-permute-start | bytes 49160 | tf_op jit(solution)/shard_map/ppermute | solution.py:30
  14.1 4.4 %collective-permute-start.1 = (bf16[128,128]{1,0:T(8,128)(2,1)S(1)}, bf16[128,128]{1,0:T(8,128)(2,1)S(1)}, u32[]{:S(2)}, u32[]{:S(2)}) collective-permute-start(bf16[128,128]{1,0:T(8,128)(2,1)S(1)} %bitcast.239), channel_id=1, source_target_pairs={{0,128},{4,20},{8,136},{12,28},{16,144},{20,4},{24,152},{28,12},{3... | collective-permute-start | bytes 98312 | tf_op jit(solution)/shard_map/ppermute | solution.py:30
  26.9 7.7 %collective-permute-start.3 = (bf16[512,128]{1,0:T(8,128)(2,1)S(1)}, bf16[512,128]{1,0:T(8,128)(2,1)S(1)}, u32[]{:S(2)}, u32[]{:S(2)}) collective-permute-start(bf16[512,128]{1,0:T(8,128)(2,1)S(1)} %bitcast.228), channel_id=1, source_target_pairs={{0,32},{4,260},{8,40},{12,268},{16,48},{20,276},{24,56},{28,284},{... | collective-permute-start | bytes 393224 | tf_op jit(solution)/shard_map/ppermute | solution.py:30
  38.6 4.9 %collective-permute-start.4 = (bf16[1024,128]{1,0:T(8,128)(2,1)S(1)}, bf16[1024,128]{1,0:T(8,128)(2,1)S(1)}, u32[]{:S(2)}, u32[]{:S(2)}) collective-permute-start(bf16[1024,128]{1,0:T(8,128)(2,1)S(1)} %bitcast.220), channel_id=1, source_target_pairs={{0,16},{4,132},{8,24},{12,140},{16,0},{20,148},{24,8},{28,156},{32... | collective-permute-start | bytes 786440 | tf_op jit(solution)/shard_map/ppermute | solution.py:30
  43.7 7.0 %collective-permute-done.4 = bf16[1024,128]{1,0:T(8,128)(2,1)S(1)} collective-permute-done((bf16[1024,128]{1,0:T(8,128)(2,1)S(1)}, bf16[1024,128]{1,0:T(8,128)(2,1)S(1)}, u32[]{:S(2)}, u32[]{:S(2)}) %collective-permute-start.4) | collective-permute-done | bytes 262176 | tf_op jit(solution)/shard_map/ppermute | solution.py:30
  52.9 8.9 %collective-permute-done.5 = bf16[2048,128]{1,0:T(8,128)(2,1)S(1)} collective-permute-done((bf16[2048,128]{1,0:T(8,128)(2,1)S(1)}, bf16[2048,128]{1,0:T(8,128)(2,1)S(1)}, u32[]{:S(2)}, u32[]{:S(2)}) %collective-permute-start.5) | collective-permute-done | bytes 524320 | tf_op jit(solution)/shard_map/ppermute | solution.py:30
  68.0 6.9 %while.37 = (s32[]{:T(128)}, f32[2,128,8192]{2,1,0:T(8,128)}, f32[2,128]{1,0:T(2,128)S(1)}, bf16[2,128,128]{2,1,0:T(8,128)(2,1)S(1)}, bf16[8192,128]{1,0:T(8,128)(2,1)S(1)}, /*index=5*/s32[]{:T(128)}, s32[]{:T(128)}) while((s32[]{:T(128)}, f32[2,128,8192]{2,1,0:T(8,128)}, f32[2,128]{1,0:T(2,128)S(1)}, bf16[2,128,128]{2,1,0:T(8,128)(2,1)S(1)}, ...), condition=%wide.region_2.3_spmd, body=%wide.region_0.2_spmd.sunk | while | flops 271581056 | bytes 14715477 | solution.py:115
  78.2 11.9 %all-gather.1 = f32[4,3,256]{2,1,0:T(4,128)S(1)} all-gather(f32[1,3,256]{2,1,0:T(4,128)S(1)} %maximum_bitcast_fusion), channel_id=2, replica_groups=mesh['dp'=128,'proto'=4] {'proto'}, dimensions={0}, use_global_device_ids=true | all-gather | bytes 15360 | tf_op jit(solution)/shard_map/all_gather | solution.py:131
  90.2 4.3 %multiply_reduce_fusion.5 = f32[8192]{0:T(1024)S(1)} fusion(f32[2,128,8192]{2,1,0:T(8,128)} %get-tuple-element.369, f32[2,128]{1,0:T(2,128)S(1)} %multiply_exponential_fusion), kind=kLoop, calls=%fused_computation.37 | loop fusion | flops 4186112 | bytes 8422400 | tf_op jit(solution)/shard_map/reduce_sum | solution.py:142
  110.4 7.1 %collective-permute-start.10 = (f32[8192]{0:T(1024)S(1)}, f32[8192]{0:T(1024)S(1)}, u32[]{:S(2)}, u32[]{:S(2)}) collective-permute-start(f32[8192]{0:T(1024)S(1)} %add.226), channel_id=1, source_target_pairs={{0,32},{4,36},{8,40},{12,44},{16,48},{20,52},{24,56},{28,60},{32,0... | collective-permute-start | bytes 98312 | tf_op jit(solution)/shard_map/ppermute | solution.py:17
  126.2 4.6 %collective-permute-start.12 = (f32[8192]{0:T(1024)S(1)}, f32[8192]{0:T(1024)S(1)}, u32[]{:S(2)}, u32[]{:S(2)}) collective-permute-start(f32[8192]{0:T(1024)S(1)} %add.228), channel_id=1, source_target_pairs={{0,128},{4,132},{8,136},{12,140},{16,144},{20,148},{24,152},{28,15... | collective-permute-start | bytes 98312 | tf_op jit(solution)/shard_map/ppermute | solution.py:17
  132.9 9.1 %collective-permute-start.13 = (f32[8192]{0:T(1024)S(1)}, f32[8192]{0:T(1024)S(1)}, u32[]{:S(2)}, u32[]{:S(2)}) collective-permute-start(f32[8192]{0:T(1024)S(1)} %add.229), channel_id=1, source_target_pairs={{0,256},{4,260},{8,264},{12,268},{16,272},{20,276},{24,280},{28,28... | collective-permute-start | bytes 98312 | tf_op jit(solution)/shard_map/ppermute | solution.py:17
  143.9 4.2 %multiply_reduce_fusion.4 = f32[2,128]{1,0:T(2,128)S(1)} fusion(f32[2,128,8192]{2,1,0:T(8,128)} %get-tuple-element.369, f32[8192]{0:T(1024)S(1)} %add_divide_fusion.2), kind=kLoop, calls=%fused_computation.36 | loop fusion | flops 4194048 | bytes 8422400 | tf_op jit(solution)/shard_map/reduce_sum | solution.py:144
  160.5 4.3 %multiply_reduce_fusion.3 = f32[8192]{0:T(1024)S(1)} fusion(f32[2,128,8192]{2,1,0:T(8,128)} %get-tuple-element.369, f32[2,128]{1,0:T(2,128)S(1)} %fusion.28), kind=kLoop, calls=%fused_computation.35 | loop fusion | flops 4186112 | bytes 8422400 | tf_op jit(solution)/shard_map/reduce_sum | solution.py:142
  180.6 6.9 %collective-permute-start.19 = (f32[8192]{0:T(1024)S(1)}, f32[8192]{0:T(1024)S(1)}, u32[]{:S(2)}, u32[]{:S(2)}) collective-permute-start(f32[8192]{0:T(1024)S(1)} %add.235), channel_id=1, source_target_pairs={{0,32},{4,36},{8,40},{12,44},{16,48},{20,52},{24,56},{28,60},{32,0... | collective-permute-start | bytes 98312 | tf_op jit(solution)/shard_map/ppermute | solution.py:17
  196.3 4.7 %collective-permute-start.21 = (f32[8192]{0:T(1024)S(1)}, f32[8192]{0:T(1024)S(1)}, u32[]{:S(2)}, u32[]{:S(2)}) collective-permute-start(f32[8192]{0:T(1024)S(1)} %add.237), channel_id=1, source_target_pairs={{0,128},{4,132},{8,136},{12,140},{16,144},{20,148},{24,152},{28,15... | collective-permute-start | bytes 98312 | tf_op jit(solution)/shard_map/ppermute | solution.py:17
  203.0 8.1 %collective-permute-start.22 = (f32[8192]{0:T(1024)S(1)}, f32[8192]{0:T(1024)S(1)}, u32[]{:S(2)}, u32[]{:S(2)}) collective-permute-start(f32[8192]{0:T(1024)S(1)} %add.238), channel_id=1, source_target_pairs={{0,256},{4,260},{8,264},{12,268},{16,272},{20,276},{24,280},{28,28... | collective-permute-start | bytes 98312 | tf_op jit(solution)/shard_map/ppermute | solution.py:17
  213.0 4.2 %multiply_reduce_fusion.2 = f32[2,128]{1,0:T(2,128)S(1)} fusion(f32[2,128,8192]{2,1,0:T(8,128)} %get-tuple-element.369, f32[8192]{0:T(1024)S(1)} %add_divide_fusion.1), kind=kLoop, calls=%fused_computation.34 | loop fusion | flops 4194048 | bytes 8422400 | tf_op jit(solution)/shard_map/reduce_sum | solution.py:144
  229.6 4.3 %multiply_reduce_fusion.1 = f32[8192]{0:T(1024)S(1)} fusion(f32[2,128,8192]{2,1,0:T(8,128)} %get-tuple-element.369, f32[2,128]{1,0:T(2,128)S(1)} %fusion.29), kind=kLoop, calls=%fused_computation.33 | loop fusion | flops 4186112 | bytes 8422400 | tf_op jit(solution)/shard_map/reduce_sum | solution.py:142
  249.8 6.8 %collective-permute-start.28 = (f32[8192]{0:T(1024)S(1)}, f32[8192]{0:T(1024)S(1)}, u32[]{:S(2)}, u32[]{:S(2)}) collective-permute-start(f32[8192]{0:T(1024)S(1)} %add.244), channel_id=1, source_target_pairs={{0,32},{4,36},{8,40},{12,44},{16,48},{20,52},{24,56},{28,60},{32,0... | collective-permute-start | bytes 98312 | tf_op jit(solution)/shard_map/ppermute | solution.py:17
  265.3 4.6 %collective-permute-start.30 = (f32[8192]{0:T(1024)S(1)}, f32[8192]{0:T(1024)S(1)}, u32[]{:S(2)}, u32[]{:S(2)}) collective-permute-start(f32[8192]{0:T(1024)S(1)} %add.246), channel_id=1, source_target_pairs={{0,128},{4,132},{8,136},{12,140},{16,144},{20,148},{24,152},{28,15... | collective-permute-start | bytes 98312 | tf_op jit(solution)/shard_map/ppermute | solution.py:17
  272.0 8.0 %collective-permute-start.31 = (f32[8192]{0:T(1024)S(1)}, f32[8192]{0:T(1024)S(1)}, u32[]{:S(2)}, u32[]{:S(2)}) collective-permute-start(f32[8192]{0:T(1024)S(1)} %add.247), channel_id=1, source_target_pairs={{0,256},{4,260},{8,264},{12,268},{16,272},{20,276},{24,280},{28,28... | collective-permute-start | bytes 98312 | tf_op jit(solution)/shard_map/ppermute | solution.py:17
  298.4 11.7 %while.38 = (s32[]{:T(128)}, bf16[2,128,8192]{2,1,0:T(8,128)(2,1)}, f32[2,128,128]{2,1,0:T(8,128)S(1)}, bf16[2,128,128]{2,1,0:T(8,128)(2,1)S(1)}, bf16[8192,128]...) while((s32[]{:T(128)}, bf16[2,128,8192]{2,1,0:T(8,128)(2,1)}, ...), condition=%wide.region_14.15_spmd, body=%wide.region_13.14_spmd.sunk | while | flops 544227328 | bytes 14816889 | solution.py:157
  298.4 5.1 %bitcast_dynamic-update-slice_fusion.18 = (bf16[2,128,8192]{2,1,0:T(8,128)(2,1)}, bf16[128,8192]{1,0:T(8,128)(2,1)S(1)}) fusion(bf16[2,128,8192]{2,1,0:T(8,128)(2,1)} %get-tuple-element.373, s32[]{:T(128)} %get-tuple-element.372, f32[8192]{0:T(1024)S(1)} %get-tuple-element.392, f32[2,128,8192]{2,1,0:T(8,128)} %get-tuple-element.391, ...), kind=kOutput, calls=%fused_computation.18.clone.1 | convolution fusion | flops 275775488 | bytes 10553856 | tf_op jit(solution)/shard_map/while/body/eval_jaxpr/dot_general | solution.py:89
  304.3 5.0 %bitcast_dynamic-update-slice_fusion.18 = (bf16[2,128,8192]{2,1,0:T(8,128)(2,1)}, bf16[128,8192]{1,0:T(8,128)(2,1)S(1)}) fusion(bf16[2,128,8192]{2,1,0:T(8,128)(2,1)} %get-tuple-element.373, s32[]{:T(128)} %get-tuple-element.372, f32[8192]{0:T(1024)S(1)} %get-tuple-element.392, f32[2,128,8192]{2,1,0:T(8,128)} %get-tuple-element.391, ...), kind=kOutput, calls=%fused_computation.18.clone.1 | convolution fusion | flops 275775488 | bytes 10553856 | tf_op jit(solution)/shard_map/while/body/eval_jaxpr/dot_general | solution.py:89
  315.8 4.1 %collective-permute-done.34 = f32[4096,128]{1,0:T(8,128)S(1)} collective-permute-done((f32[4096,128]{1,0:T(8,128)S(1)}, f32[4096,128]{1,0:T(8,128)S(1)}, u32[]{:S(2)}, u32[]{:S(2)}) %collective-permute-start.34) | collective-permute-done | bytes 2097184 | tf_op jit(solution)/shard_map/ppermute | solution.py:30
  322.4 14.8 %collective-permute-done.35 = f32[2048,128]{1,0:T(8,128)S(1)} collective-permute-done((f32[2048,128]{1,0:T(8,128)S(1)}, f32[2048,128]{1,0:T(8,128)S(1)}, u32[]{:S(2)}, u32[]{:S(2)}) %collective-permute-start.35) | collective-permute-done | bytes 1048608 | tf_op jit(solution)/shard_map/ppermute | solution.py:30
  340.0 14.4 %collective-permute-done.36 = f32[1024,128]{1,0:T(8,128)S(1)} collective-permute-done((f32[1024,128]{1,0:T(8,128)S(1)}, f32[1024,128]{1,0:T(8,128)S(1)}, u32[]{:S(2)}, u32[]{:S(2)}) %collective-permute-start.36) | collective-permute-done | bytes 524320 | tf_op jit(solution)/shard_map/ppermute | solution.py:30
  354.5 6.9 %collective-permute-start.37 = (f32[512,128]{1,0:T(8,128)S(1)}, f32[512,128]{1,0:T(8,128)S(1)}, u32[]{:S(2)}, u32[]{:S(2)}) collective-permute-start(f32[512,128]{1,0:T(8,128)S(1)} %dynamic-slice_bitcast_fusion.3), channel_id=1, source_target_pairs={{0,32},{4,260},{8,40},{12,268},{16,48},{20,276},{24,56},{28,284},{... | collective-permute-start | bytes 786440 | tf_op jit(solution)/shard_map/ppermute | solution.py:30
  361.4 8.1 %collective-permute-done.37 = f32[512,128]{1,0:T(8,128)S(1)} collective-permute-done((f32[512,128]{1,0:T(8,128)S(1)}, f32[512,128]{1,0:T(8,128)S(1)}, u32[]{:S(2)}, u32[]{:S(2)}) %collective-permute-start.37) | collective-permute-done | bytes 262176 | tf_op jit(solution)/shard_map/ppermute | solution.py:30
  376.5 4.6 %collective-permute-start.39 = (f32[128,128]{1,0:T(8,128)S(1)}, f32[128,128]{1,0:T(8,128)S(1)}, u32[]{:S(2)}, u32[]{:S(2)}) collective-permute-start(f32[128,128]{1,0:T(8,128)S(1)} %dynamic-slice_bitcast_fusion.5), channel_id=1, source_target_pairs={{0,128},{4,20},{8,136},{12,28},{16,144},{20,4},{24,152},{28,12},{3... | collective-permute-start | bytes 196616 | tf_op jit(solution)/shard_map/ppermute | solution.py:30
  384.6 8.0 %collective-permute-start.40 = (f32[64,128]{1,0:T(8,128)S(1)}, f32[64,128]{1,0:T(8,128)S(1)}, u32[]{:S(2)}, u32[]{:S(2)}) collective-permute-start(f32[64,128]{1,0:T(8,128)S(1)} %dynamic-slice_bitcast_fusion.6), channel_id=1, source_target_pairs={{0,256},{4,36},{8,264},{12,44},{16,272},{20,52},{24,280},{28,60},{... | collective-permute-start | bytes 98312 | tf_op jit(solution)/shard_map/ppermute | solution.py:30
  (179 shorter events, 188.6 us)
Async XLA Ops:
  1.4 12.6 %collective-permute-start = (bf16[64,128]{1,0:T(8,128)(2,1)S(1)}, bf16[64,128]{1,0:T(8,128)(2,1)S(1)}, u32[]{:S(2)}, u32[]{:S(2)}) collective-permute-start(bf16[64,128]{1,0:T(8,128)(2,1)S(1)} %get-tuple-element.160), channel_id=1, source_target_pairs={{0,256},{4,36},{8,264},{12,44},{16,272},{20,52},{24,280},{28,60},{... | collective-permute-start | bytes 49160 | tf_op jit(solution)/shard_map/ppermute | solution.py:30
  14.1 6.7 %collective-permute-start.1 = (bf16[128,128]{1,0:T(8,128)(2,1)S(1)}, bf16[128,128]{1,0:T(8,128)(2,1)S(1)}, u32[]{:S(2)}, u32[]{:S(2)}) collective-permute-start(bf16[128,128]{1,0:T(8,128)(2,1)S(1)} %bitcast.239), channel_id=1, source_target_pairs={{0,128},{4,20},{8,136},{12,28},{16,144},{20,4},{24,152},{28,12},{3... | collective-permute-start | bytes 98312 | tf_op jit(solution)/shard_map/ppermute | solution.py:30
  20.8 6.1 %collective-permute-start.2 = (bf16[256,128]{1,0:T(8,128)(2,1)S(1)}, bf16[256,128]{1,0:T(8,128)(2,1)S(1)}, u32[]{:S(2)}, u32[]{:S(2)}) collective-permute-start(bf16[256,128]{1,0:T(8,128)(2,1)S(1)} %bitcast.236), channel_id=1, source_target_pairs={{0,64},{4,12},{8,72},{12,4},{16,80},{20,28},{24,88},{28,20},{32,96... | collective-permute-start | bytes 196616 | tf_op jit(solution)/shard_map/ppermute | solution.py:30
  26.9 11.6 %collective-permute-start.3 = (bf16[512,128]{1,0:T(8,128)(2,1)S(1)}, bf16[512,128]{1,0:T(8,128)(2,1)S(1)}, u32[]{:S(2)}, u32[]{:S(2)}) collective-permute-start(bf16[512,128]{1,0:T(8,128)(2,1)S(1)} %bitcast.228), channel_id=1, source_target_pairs={{0,32},{4,260},{8,40},{12,268},{16,48},{20,276},{24,56},{28,284},{... | collective-permute-start | bytes 393224 | tf_op jit(solution)/shard_map/ppermute | solution.py:30
  38.6 12.1 %collective-permute-start.4 = (bf16[1024,128]{1,0:T(8,128)(2,1)S(1)}, bf16[1024,128]{1,0:T(8,128)(2,1)S(1)}, u32[]{:S(2)}, u32[]{:S(2)}) collective-permute-start(bf16[1024,128]{1,0:T(8,128)(2,1)S(1)} %bitcast.220), channel_id=1, source_target_pairs={{0,16},{4,132},{8,24},{12,140},{16,0},{20,148},{24,8},{28,156},{32... | collective-permute-start | bytes 786440 | tf_op jit(solution)/shard_map/ppermute | solution.py:30
  50.7 11.1 %collective-permute-start.5 = (bf16[2048,128]{1,0:T(8,128)(2,1)S(1)}, bf16[2048,128]{1,0:T(8,128)(2,1)S(1)}, u32[]{:S(2)}, u32[]{:S(2)}) collective-permute-start(bf16[2048,128]{1,0:T(8,128)(2,1)S(1)} %bitcast.218), channel_id=1, source_target_pairs={{0,8},{4,68},{8,0},{12,76},{16,24},{20,84},{24,16},{28,92},{32,40}... | collective-permute-start | bytes 1572872 | tf_op jit(solution)/shard_map/ppermute | solution.py:30
  97.8 5.8 %collective-permute-start.8 = (f32[8192]{0:T(1024)S(1)}, f32[8192]{0:T(1024)S(1)}, u32[]{:S(2)}, u32[]{:S(2)}) collective-permute-start(f32[8192]{0:T(1024)S(1)} %add.224), channel_id=1, source_target_pairs={{0,8},{4,12},{8,0},{12,4},{16,24},{20,28},{24,16},{28,20},{32,40},... | collective-permute-start | bytes 98312 | tf_op jit(solution)/shard_map/ppermute | solution.py:17
  103.6 6.8 %collective-permute-start.9 = (f32[8192]{0:T(1024)S(1)}, f32[8192]{0:T(1024)S(1)}, u32[]{:S(2)}, u32[]{:S(2)}) collective-permute-start(f32[8192]{0:T(1024)S(1)} %add.225), channel_id=1, source_target_pairs={{0,16},{4,20},{8,24},{12,28},{16,0},{20,4},{24,8},{28,12},{32,48},... | collective-permute-start | bytes 98312 | tf_op jit(solution)/shard_map/ppermute | solution.py:17
  110.4 9.9 %collective-permute-start.10 = (f32[8192]{0:T(1024)S(1)}, f32[8192]{0:T(1024)S(1)}, u32[]{:S(2)}, u32[]{:S(2)}) collective-permute-start(f32[8192]{0:T(1024)S(1)} %add.226), channel_id=1, source_target_pairs={{0,32},{4,36},{8,40},{12,44},{16,48},{20,52},{24,56},{28,60},{32,0... | collective-permute-start | bytes 98312 | tf_op jit(solution)/shard_map/ppermute | solution.py:17
  126.2 6.7 %collective-permute-start.12 = (f32[8192]{0:T(1024)S(1)}, f32[8192]{0:T(1024)S(1)}, u32[]{:S(2)}, u32[]{:S(2)}) collective-permute-start(f32[8192]{0:T(1024)S(1)} %add.228), channel_id=1, source_target_pairs={{0,128},{4,132},{8,136},{12,140},{16,144},{20,148},{24,152},{28,15... | collective-permute-start | bytes 98312 | tf_op jit(solution)/shard_map/ppermute | solution.py:17
  132.9 11.0 %collective-permute-start.13 = (f32[8192]{0:T(1024)S(1)}, f32[8192]{0:T(1024)S(1)}, u32[]{:S(2)}, u32[]{:S(2)}) collective-permute-start(f32[8192]{0:T(1024)S(1)} %add.229), channel_id=1, source_target_pairs={{0,256},{4,260},{8,264},{12,268},{16,272},{20,276},{24,280},{28,28... | collective-permute-start | bytes 98312 | tf_op jit(solution)/shard_map/ppermute | solution.py:17
  153.5 7.0 %collective-permute-start.15 = (f32[256]{0:T(256)S(1)}, f32[256]{0:T(256)S(1)}, u32[]{:S(2)}, u32[]{:S(2)}) collective-permute-start(f32[256]{0:T(256)S(1)} %add.231), channel_id=1, source_target_pairs={{0,2},{1,3},{2,0},{3,1},{4,6},{5,7},{6,4},{7,5},{8,10},{9,11},{10,... | collective-permute-start | bytes 3080 | tf_op jit(solution)/shard_map/ppermute | solution.py:17
  168.1 5.8 %collective-permute-start.17 = (f32[8192]{0:T(1024)S(1)}, f32[8192]{0:T(1024)S(1)}, u32[]{:S(2)}, u32[]{:S(2)}) collective-permute-start(f32[8192]{0:T(1024)S(1)} %add.233), channel_id=1, source_target_pairs={{0,8},{4,12},{8,0},{12,4},{16,24},{20,28},{24,16},{28,20},{32,40},... | collective-permute-start | bytes 98312 | tf_op jit(solution)/shard_map/ppermute | solution.py:17
  173.9 6.7 %collective-permute-start.18 = (f32[8192]{0:T(1024)S(1)}, f32[8192]{0:T(1024)S(1)}, u32[]{:S(2)}, u32[]{:S(2)}) collective-permute-start(f32[8192]{0:T(1024)S(1)} %add.234), channel_id=1, source_target_pairs={{0,16},{4,20},{8,24},{12,28},{16,0},{20,4},{24,8},{28,12},{32,48},... | collective-permute-start | bytes 98312 | tf_op jit(solution)/shard_map/ppermute | solution.py:17
  180.6 9.9 %collective-permute-start.19 = (f32[8192]{0:T(1024)S(1)}, f32[8192]{0:T(1024)S(1)}, u32[]{:S(2)}, u32[]{:S(2)}) collective-permute-start(f32[8192]{0:T(1024)S(1)} %add.235), channel_id=1, source_target_pairs={{0,32},{4,36},{8,40},{12,44},{16,48},{20,52},{24,56},{28,60},{32,0... | collective-permute-start | bytes 98312 | tf_op jit(solution)/shard_map/ppermute | solution.py:17
  196.3 6.7 %collective-permute-start.21 = (f32[8192]{0:T(1024)S(1)}, f32[8192]{0:T(1024)S(1)}, u32[]{:S(2)}, u32[]{:S(2)}) collective-permute-start(f32[8192]{0:T(1024)S(1)} %add.237), channel_id=1, source_target_pairs={{0,128},{4,132},{8,136},{12,140},{16,144},{20,148},{24,152},{28,15... | collective-permute-start | bytes 98312 | tf_op jit(solution)/shard_map/ppermute | solution.py:17
  203.0 10.0 %collective-permute-start.22 = (f32[8192]{0:T(1024)S(1)}, f32[8192]{0:T(1024)S(1)}, u32[]{:S(2)}, u32[]{:S(2)}) collective-permute-start(f32[8192]{0:T(1024)S(1)} %add.238), channel_id=1, source_target_pairs={{0,256},{4,260},{8,264},{12,268},{16,272},{20,276},{24,280},{28,28... | collective-permute-start | bytes 98312 | tf_op jit(solution)/shard_map/ppermute | solution.py:17
  222.7 7.0 %collective-permute-start.24 = (f32[256]{0:T(256)S(1)}, f32[256]{0:T(256)S(1)}, u32[]{:S(2)}, u32[]{:S(2)}) collective-permute-start(f32[256]{0:T(256)S(1)} %add.240), channel_id=1, source_target_pairs={{0,2},{1,3},{2,0},{3,1},{4,6},{5,7},{6,4},{7,5},{8,10},{9,11},{10,... | collective-permute-start | bytes 3080 | tf_op jit(solution)/shard_map/ppermute | solution.py:17
  243.1 6.7 %collective-permute-start.27 = (f32[8192]{0:T(1024)S(1)}, f32[8192]{0:T(1024)S(1)}, u32[]{:S(2)}, u32[]{:S(2)}) collective-permute-start(f32[8192]{0:T(1024)S(1)} %add.243), channel_id=1, source_target_pairs={{0,16},{4,20},{8,24},{12,28},{16,0},{20,4},{24,8},{28,12},{32,48},... | collective-permute-start | bytes 98312 | tf_op jit(solution)/shard_map/ppermute | solution.py:17
  249.8 9.7 %collective-permute-start.28 = (f32[8192]{0:T(1024)S(1)}, f32[8192]{0:T(1024)S(1)}, u32[]{:S(2)}, u32[]{:S(2)}) collective-permute-start(f32[8192]{0:T(1024)S(1)} %add.244), channel_id=1, source_target_pairs={{0,32},{4,36},{8,40},{12,44},{16,48},{20,52},{24,56},{28,60},{32,0... | collective-permute-start | bytes 98312 | tf_op jit(solution)/shard_map/ppermute | solution.py:17
  265.3 6.7 %collective-permute-start.30 = (f32[8192]{0:T(1024)S(1)}, f32[8192]{0:T(1024)S(1)}, u32[]{:S(2)}, u32[]{:S(2)}) collective-permute-start(f32[8192]{0:T(1024)S(1)} %add.246), channel_id=1, source_target_pairs={{0,128},{4,132},{8,136},{12,140},{16,144},{20,148},{24,152},{28,15... | collective-permute-start | bytes 98312 | tf_op jit(solution)/shard_map/ppermute | solution.py:17
  272.0 9.9 %collective-permute-start.31 = (f32[8192]{0:T(1024)S(1)}, f32[8192]{0:T(1024)S(1)}, u32[]{:S(2)}, u32[]{:S(2)}) collective-permute-start(f32[8192]{0:T(1024)S(1)} %add.247), channel_id=1, source_target_pairs={{0,256},{4,260},{8,264},{12,268},{16,272},{20,276},{24,280},{28,28... | collective-permute-start | bytes 98312 | tf_op jit(solution)/shard_map/ppermute | solution.py:17
  291.4 7.0 %collective-permute-start.33 = (f32[256]{0:T(256)S(1)}, f32[256]{0:T(256)S(1)}, u32[]{:S(2)}, u32[]{:S(2)}) collective-permute-start(f32[256]{0:T(256)S(1)} %add.249), channel_id=1, source_target_pairs={{0,2},{1,3},{2,0},{3,1},{4,6},{5,7},{6,4},{7,5},{8,10},{9,11},{10,... | collective-permute-start | bytes 3080 | tf_op jit(solution)/shard_map/ppermute | solution.py:17
  313.8 6.1 %collective-permute-start.34 = (f32[4096,128]{1,0:T(8,128)S(1)}, f32[4096,128]{1,0:T(8,128)S(1)}, u32[]{:S(2)}, u32[]{:S(2)}) collective-permute-start(f32[4096,128]{1,0:T(8,128)S(1)} %get-tuple-element.169), channel_id=1, source_target_pairs={{0,4},{4,0},{8,12},{12,8},{16,20},{20,16},{24,28},{28,24},{32,36},... | collective-permute-start | bytes 6291464 | tf_op jit(solution)/shard_map/ppermute | solution.py:30
  320.5 16.7 %collective-permute-start.35 = (f32[2048,128]{1,0:T(8,128)S(1)}, f32[2048,128]{1,0:T(8,128)S(1)}, u32[]{:S(2)}, u32[]{:S(2)}) collective-permute-start(f32[2048,128]{1,0:T(8,128)S(1)} %dynamic-slice_bitcast_fusion.1), channel_id=1, source_target_pairs={{0,8},{4,68},{8,0},{12,76},{16,24},{20,84},{24,16},{28,92},{32,40}... | collective-permute-start | bytes 3145736 | tf_op jit(solution)/shard_map/ppermute | solution.py:30
  337.4 17.0 %collective-permute-start.36 = (f32[1024,128]{1,0:T(8,128)S(1)}, f32[1024,128]{1,0:T(8,128)S(1)}, u32[]{:S(2)}, u32[]{:S(2)}) collective-permute-start(f32[1024,128]{1,0:T(8,128)S(1)} %dynamic-slice_bitcast_fusion.2), channel_id=1, source_target_pairs={{0,16},{4,132},{8,24},{12,140},{16,0},{20,148},{24,8},{28,156},{32... | collective-permute-start | bytes 1572872 | tf_op jit(solution)/shard_map/ppermute | solution.py:30
  354.5 15.0 %collective-permute-start.37 = (f32[512,128]{1,0:T(8,128)S(1)}, f32[512,128]{1,0:T(8,128)S(1)}, u32[]{:S(2)}, u32[]{:S(2)}) collective-permute-start(f32[512,128]{1,0:T(8,128)S(1)} %dynamic-slice_bitcast_fusion.3), channel_id=1, source_target_pairs={{0,32},{4,260},{8,40},{12,268},{16,48},{20,276},{24,56},{28,284},{... | collective-permute-start | bytes 786440 | tf_op jit(solution)/shard_map/ppermute | solution.py:30
  369.5 6.9 %collective-permute-start.38 = (f32[256,128]{1,0:T(8,128)S(1)}, f32[256,128]{1,0:T(8,128)S(1)}, u32[]{:S(2)}, u32[]{:S(2)}) collective-permute-start(f32[256,128]{1,0:T(8,128)S(1)} %dynamic-slice_bitcast_fusion.4), channel_id=1, source_target_pairs={{0,64},{4,12},{8,72},{12,4},{16,80},{20,28},{24,88},{28,20},{32,96... | collective-permute-start | bytes 393224 | tf_op jit(solution)/shard_map/ppermute | solution.py:30
  373.0 8.1 %collective-permute-start.41 = (f32[256,128]{1,0:T(8,128)S(1)}, f32[256,128]{1,0:T(8,128)S(1)}, u32[]{:S(2)}, u32[]{:S(2)}) collective-permute-start(f32[256,128]{1,0:T(8,128)S(1)} %bitcast.238), channel_id=1, source_target_pairs={{0,1},{1,0},{2,3},{3,2},{4,5},{5,4},{6,7},{7,6},{8,9},{9,8},{10,11... | collective-permute-start | bytes 393224 | tf_op jit(solution)/shard_map/ppermute | solution.py:17
  376.5 8.1 %collective-permute-start.39 = (f32[128,128]{1,0:T(8,128)S(1)}, f32[128,128]{1,0:T(8,128)S(1)}, u32[]{:S(2)}, u32[]{:S(2)}) collective-permute-start(f32[128,128]{1,0:T(8,128)S(1)} %dynamic-slice_bitcast_fusion.5), channel_id=1, source_target_pairs={{0,128},{4,20},{8,136},{12,28},{16,144},{20,4},{24,152},{28,12},{3... | collective-permute-start | bytes 196616 | tf_op jit(solution)/shard_map/ppermute | solution.py:30
  381.1 11.4 %collective-permute-start.42 = (f32[256,128]{1,0:T(8,128)S(1)}, f32[256,128]{1,0:T(8,128)S(1)}, u32[]{:S(2)}, u32[]{:S(2)}) collective-permute-start(f32[256,128]{1,0:T(8,128)S(1)} %bitcast_add_fusion.6), channel_id=1, source_target_pairs={{0,2},{1,3},{2,0},{3,1},{4,6},{5,7},{6,4},{7,5},{8,10},{9,11},{10,... | collective-permute-start | bytes 393224 | tf_op jit(solution)/shard_map/ppermute | solution.py:17
  384.6 9.9 %collective-permute-start.40 = (f32[64,128]{1,0:T(8,128)S(1)}, f32[64,128]{1,0:T(8,128)S(1)}, u32[]{:S(2)}, u32[]{:S(2)}) collective-permute-start(f32[64,128]{1,0:T(8,128)S(1)} %dynamic-slice_bitcast_fusion.6), channel_id=1, source_target_pairs={{0,256},{4,36},{8,264},{12,44},{16,272},{20,52},{24,280},{28,60},{... | collective-permute-start | bytes 98312 | tf_op jit(solution)/shard_map/ppermute | solution.py:30
  (13 other events, 64.7 us)

commit v5 on v4

--- a/solution.py
+++ b/solution.py
@@ -142,7 +142,7 @@
         partial_cols = jnp.sum((row_scale * shift)[:, None] * base_local, axis=0)
         col_scale = 1.0 / column_sum(partial_cols, "dp")
         partial_rows = shift * jnp.sum(base_local * col_scale[None, :], axis=1)
-        row_scale = 1.0 / sum_over(partial_rows, "proto")
+        row_scale = 1.0 / lax.psum(partial_rows, "proto")
     row_factor = row_scale * shift
     student_factor = jnp.exp(student_local - student_top) / total
 

time: 397 us -> 387 us (0.975)
  blocking collectives: 11.9 us -> 37.3 us
  waiting for transfers between devices: 148 us -> 125 us
  starting transfers between devices: 177 us -> 164 us
    psum x0 -> x3, blocking collectives: none -> 25.4 us  [per_device(): row_scale = 1.0 / lax.psum(partial_rows, 'proto')]
    ppermute x29 -> x23, waiting for transfers between devices: 74.9 us -> 53.7 us  [swap(): return lax.ppermute(x, axis, [(i, i ^ 1 << k) for i in range(n)])]
    ppermute x29 -> x23, starting transfers between devices: 112 us -> 99.3 us  [swap(): return lax.ppermute(x, axis, [(i, i ^ 1 << k) for i in range(n)])]
  transfers between devices with their start and end apart: 43 -> 37, of which waited for: 40 -> 34; matrix products, arithmetic and copies ran while one was open for 0% -> 0% of each run, Pallas kernels for 0% -> 0%
where the time goes in v5:
time: 387 us; the launch traced here: 385 us
  starting transfers between devices  164 us (42%)
  waiting for transfers between devices  125 us (32%)
  blocking collectives  37.3 us (10%)
  other arithmetic  35 us (9%)
  matrix products  18.2 us (5%)
    ppermute x23, starting transfers between devices, swap(): return lax.ppermute(x, axis, [(i, i ^ 1 << k) for i in range(n)])  99.3 us
    ppermute x14, waiting for transfers between devices, core_swap(): return lax.ppermute(x, axis, pairs)  71.4 us
    ppermute x14, starting transfers between devices, core_swap(): return lax.ppermute(x, axis, pairs)  64.5 us
    ppermute x23, waiting for transfers between devices, swap(): return lax.ppermute(x, axis, [(i, i ^ 1 << k) for i in range(n)])  53.7 us
    psum x3, blocking collectives, per_device(): row_scale = 1.0 / lax.psum(partial_rows, 'proto')  25.4 us
    dot_general x6, matrix products, contract_rows(): lax.dot_general(left, right, (((1,), (1,)), ((), ())), preferred_element_...  13.2 us
    reduce_sum x3, other arithmetic, per_device(): partial_cols = jnp.sum((row_scale * shift)[:, None] * base_local, axis=0)  13 us
    reduce_sum x3, other arithmetic, per_device(): partial_rows = shift * jnp.sum(base_local * col_scale[None, :], axis=1)  12.5 us
  transfers between devices with their start and end apart: 37, of which 34 were waited for; matrix products, arithmetic and copies ran while one was open for 0% of the time, Pallas kernels for 0%

profile of v5, /device:TPU:6, one launch (start us, length us, event | category | flops | bytes accessed | tf_op | source)
XLA Modules:
  0.0 384.9 jit_solution(11618676590828777838)
XLA Ops:
  1.4 10.9 %collective-permute-start = (bf16[64,128]{1,0:T(8,128)(2,1)S(1)}, bf16[64,128]{1,0:T(8,128)(2,1)S(1)}, u32[]{:S(2)}, u32[]{:S(2)}) collective-permute-start(bf16[64,128]{1,0:T(8,128)(2,1)S(1)} %get-tuple-element.160), channel_id=1, source_target_pairs={{0,256},{4,36},{8,264},{12,44},{16,272},{20,52},{24,280},{28,60},{... | collective-permute-start | bytes 49160 | tf_op jit(solution)/shard_map/ppermute | solution.py:30
  14.1 4.4 %collective-permute-start.1 = (bf16[128,128]{1,0:T(8,128)(2,1)S(1)}, bf16[128,128]{1,0:T(8,128)(2,1)S(1)}, u32[]{:S(2)}, u32[]{:S(2)}) collective-permute-start(bf16[128,128]{1,0:T(8,128)(2,1)S(1)} %bitcast.239), channel_id=1, source_target_pairs={{0,128},{4,20},{8,136},{12,28},{16,144},{20,4},{24,152},{28,12},{3... | collective-permute-start | bytes 98312 | tf_op jit(solution)/shard_map/ppermute | solution.py:30
  26.9 7.7 %collective-permute-start.3 = (bf16[512,128]{1,0:T(8,128)(2,1)S(1)}, bf16[512,128]{1,0:T(8,128)(2,1)S(1)}, u32[]{:S(2)}, u32[]{:S(2)}) collective-permute-start(bf16[512,128]{1,0:T(8,128)(2,1)S(1)} %bitcast.228), channel_id=1, source_target_pairs={{0,32},{4,260},{8,40},{12,268},{16,48},{20,276},{24,56},{28,284},{... | collective-permute-start | bytes 393224 | tf_op jit(solution)/shard_map/ppermute | solution.py:30
  38.6 4.9 %collective-permute-start.4 = (bf16[1024,128]{1,0:T(8,128)(2,1)S(1)}, bf16[1024,128]{1,0:T(8,128)(2,1)S(1)}, u32[]{:S(2)}, u32[]{:S(2)}) collective-permute-start(bf16[1024,128]{1,0:T(8,128)(2,1)S(1)} %bitcast.220), channel_id=1, source_target_pairs={{0,16},{4,132},{8,24},{12,140},{16,0},{20,148},{24,8},{28,156},{32... | collective-permute-start | bytes 786440 | tf_op jit(solution)/shard_map/ppermute | solution.py:30
  43.7 7.0 %collective-permute-done.4 = bf16[1024,128]{1,0:T(8,128)(2,1)S(1)} collective-permute-done((bf16[1024,128]{1,0:T(8,128)(2,1)S(1)}, bf16[1024,128]{1,0:T(8,128)(2,1)S(1)}, u32[]{:S(2)}, u32[]{:S(2)}) %collective-permute-start.4) | collective-permute-done | bytes 262176 | tf_op jit(solution)/shard_map/ppermute | solution.py:30
  52.9 8.9 %collective-permute-done.5 = bf16[2048,128]{1,0:T(8,128)(2,1)S(1)} collective-permute-done((bf16[2048,128]{1,0:T(8,128)(2,1)S(1)}, bf16[2048,128]{1,0:T(8,128)(2,1)S(1)}, u32[]{:S(2)}, u32[]{:S(2)}) %collective-permute-start.5) | collective-permute-done | bytes 524320 | tf_op jit(solution)/shard_map/ppermute | solution.py:30
  68.0 6.8 %while.37 = (s32[]{:T(128)}, f32[2,128,8192]{2,1,0:T(8,128)}, f32[2,128]{1,0:T(2,128)S(1)}, bf16[2,128,128]{2,1,0:T(8,128)(2,1)S(1)}, bf16[8192,128]{1,0:T(8,128)(2,1)S(1)}, /*index=5*/s32[]{:T(128)}, s32[]{:T(128)}) while((s32[]{:T(128)}, f32[2,128,8192]{2,1,0:T(8,128)}, f32[2,128]{1,0:T(2,128)S(1)}, bf16[2,128,128]{2,1,0:T(8,128)(2,1)S(1)}, ...), condition=%wide.region_2.3_spmd, body=%wide.region_0.2_spmd.sunk | while | flops 271581056 | bytes 14715477 | solution.py:115
  78.2 11.9 %all-gather.1 = f32[4,3,256]{2,1,0:T(4,128)S(1)} all-gather(f32[1,3,256]{2,1,0:T(4,128)S(1)} %maximum_bitcast_fusion), channel_id=2, replica_groups=mesh['dp'=128,'proto'=4] {'proto'}, dimensions={0}, use_global_device_ids=true | all-gather | bytes 15360 | tf_op jit(solution)/shard_map/all_gather | solution.py:131
  110.3 7.1 %collective-permute-start.10 = (f32[8192]{0:T(1024)S(1)}, f32[8192]{0:T(1024)S(1)}, u32[]{:S(2)}, u32[]{:S(2)}) collective-permute-start(f32[8192]{0:T(1024)S(1)} %add.214), channel_id=1, source_target_pairs={{0,32},{4,36},{8,40},{12,44},{16,48},{20,52},{24,56},{28,60},{32,0... | collective-permute-start | bytes 98312 | tf_op jit(solution)/shard_map/ppermute | solution.py:17
  126.1 4.6 %collective-permute-start.12 = (f32[8192]{0:T(1024)S(1)}, f32[8192]{0:T(1024)S(1)}, u32[]{:S(2)}, u32[]{:S(2)}) collective-permute-start(f32[8192]{0:T(1024)S(1)} %add.216), channel_id=1, source_target_pairs={{0,128},{4,132},{8,136},{12,140},{16,144},{20,148},{24,152},{28,15... | collective-permute-start | bytes 98312 | tf_op jit(solution)/shard_map/ppermute | solution.py:17
  132.8 9.1 %collective-permute-start.13 = (f32[8192]{0:T(1024)S(1)}, f32[8192]{0:T(1024)S(1)}, u32[]{:S(2)}, u32[]{:S(2)}) collective-permute-start(f32[8192]{0:T(1024)S(1)} %add.217), channel_id=1, source_target_pairs={{0,256},{4,260},{8,264},{12,268},{16,272},{20,276},{24,280},{28,28... | collective-permute-start | bytes 98312 | tf_op jit(solution)/shard_map/ppermute | solution.py:17
  148.0 7.5 %psum.21 = f32[256]{0:T(256)S(1)} all-reduce(f32[256]{0:T(256)S(1)} %get-tuple-element.157), channel_id=1, replica_groups=mesh['dp'=128,'proto'=4] {'proto'}, use_global_device_ids=true, to_apply=%region_9.10 | all-reduce | flops 256 | bytes 2048 | tf_op jit(solution)/shard_map/psum | solution.py:145
  155.5 4.3 %multiply_reduce_fusion.3 = f32[8192]{0:T(1024)S(1)} fusion(f32[2,128,8192]{2,1,0:T(8,128)} %get-tuple-element.369, f32[2,128]{1,0:T(2,128)S(1)} %fusion.28), kind=kLoop, calls=%fused_computation.35 | loop fusion | flops 4186112 | bytes 8422400 | tf_op jit(solution)/shard_map/reduce_sum | solution.py:142
  175.6 6.9 %collective-permute-start.17 = (f32[8192]{0:T(1024)S(1)}, f32[8192]{0:T(1024)S(1)}, u32[]{:S(2)}, u32[]{:S(2)}) collective-permute-start(f32[8192]{0:T(1024)S(1)} %add.221), channel_id=1, source_target_pairs={{0,32},{4,36},{8,40},{12,44},{16,48},{20,52},{24,56},{28,60},{32,0... | collective-permute-start | bytes 98312 | tf_op jit(solution)/shard_map/ppermute | solution.py:17
  191.3 4.7 %collective-permute-start.19 = (f32[8192]{0:T(1024)S(1)}, f32[8192]{0:T(1024)S(1)}, u32[]{:S(2)}, u32[]{:S(2)}) collective-permute-start(f32[8192]{0:T(1024)S(1)} %add.223), channel_id=1, source_target_pairs={{0,128},{4,132},{8,136},{12,140},{16,144},{20,148},{24,152},{28,15... | collective-permute-start | bytes 98312 | tf_op jit(solution)/shard_map/ppermute | solution.py:17
  198.0 8.1 %collective-permute-start.20 = (f32[8192]{0:T(1024)S(1)}, f32[8192]{0:T(1024)S(1)}, u32[]{:S(2)}, u32[]{:S(2)}) collective-permute-start(f32[8192]{0:T(1024)S(1)} %add.224), channel_id=1, source_target_pairs={{0,256},{4,260},{8,264},{12,268},{16,272},{20,276},{24,280},{28,28... | collective-permute-start | bytes 98312 | tf_op jit(solution)/shard_map/ppermute | solution.py:17
  212.2 10.0 %psum.22 = f32[256]{0:T(256)S(1)} all-reduce(f32[256]{0:T(256)S(1)} %bitcast_multiply_fusion.2), channel_id=1, replica_groups=mesh['dp'=128,'proto'=4] {'proto'}, use_global_device_ids=true, to_apply=%region_12.13 | all-reduce | flops 256 | bytes 2048 | tf_op jit(solution)/shard_map/psum | solution.py:145
  222.2 4.3 %multiply_reduce_fusion.1 = f32[8192]{0:T(1024)S(1)} fusion(f32[2,128,8192]{2,1,0:T(8,128)} %get-tuple-element.369, f32[2,128]{1,0:T(2,128)S(1)} %fusion.29), kind=kLoop, calls=%fused_computation.33 | loop fusion | flops 4186112 | bytes 8422400 | tf_op jit(solution)/shard_map/reduce_sum | solution.py:142
  242.4 6.8 %collective-permute-start.24 = (f32[8192]{0:T(1024)S(1)}, f32[8192]{0:T(1024)S(1)}, u32[]{:S(2)}, u32[]{:S(2)}) collective-permute-start(f32[8192]{0:T(1024)S(1)} %add.228), channel_id=1, source_target_pairs={{0,32},{4,36},{8,40},{12,44},{16,48},{20,52},{24,56},{28,60},{32,0... | collective-permute-start | bytes 98312 | tf_op jit(solution)/shard_map/ppermute | solution.py:17
  257.9 4.6 %collective-permute-start.26 = (f32[8192]{0:T(1024)S(1)}, f32[8192]{0:T(1024)S(1)}, u32[]{:S(2)}, u32[]{:S(2)}) collective-permute-start(f32[8192]{0:T(1024)S(1)} %add.230), channel_id=1, source_target_pairs={{0,128},{4,132},{8,136},{12,140},{16,144},{20,148},{24,152},{28,15... | collective-permute-start | bytes 98312 | tf_op jit(solution)/shard_map/ppermute | solution.py:17
  264.6 8.0 %collective-permute-start.27 = (f32[8192]{0:T(1024)S(1)}, f32[8192]{0:T(1024)S(1)}, u32[]{:S(2)}, u32[]{:S(2)}) collective-permute-start(f32[8192]{0:T(1024)S(1)} %add.231), channel_id=1, source_target_pairs={{0,256},{4,260},{8,264},{12,268},{16,272},{20,276},{24,280},{28,28... | collective-permute-start | bytes 98312 | tf_op jit(solution)/shard_map/ppermute | solution.py:17
  278.5 7.9 %psum.23 = f32[256]{0:T(256)S(1)} all-reduce(f32[256]{0:T(256)S(1)} %bitcast_multiply_fusion.1), channel_id=1, replica_groups=mesh['dp'=128,'proto'=4] {'proto'}, use_global_device_ids=true, to_apply=%region_15.16 | all-reduce | flops 256 | bytes 2048 | tf_op jit(solution)/shard_map/psum | solution.py:145
  286.5 11.7 %while.38 = (s32[]{:T(128)}, bf16[2,128,8192]{2,1,0:T(8,128)(2,1)}, f32[2,128,128]{2,1,0:T(8,128)S(1)}, bf16[2,128,128]{2,1,0:T(8,128)(2,1)S(1)}, bf16[8192,128]...) while((s32[]{:T(128)}, bf16[2,128,8192]{2,1,0:T(8,128)(2,1)}, ...), condition=%wide.region_17.18_spmd, body=%wide.region_16.17_spmd.sunk | while | flops 544227328 | bytes 14816889 | solution.py:157
  286.5 5.1 %bitcast_dynamic-update-slice_fusion.18 = (bf16[2,128,8192]{2,1,0:T(8,128)(2,1)}, bf16[128,8192]{1,0:T(8,128)(2,1)S(1)}) fusion(bf16[2,128,8192]{2,1,0:T(8,128)(2,1)} %get-tuple-element.373, s32[]{:T(128)} %get-tuple-element.372, f32[8192]{0:T(1024)S(1)} %get-tuple-element.392, f32[2,128,8192]{2,1,0:T(8,128)} %get-tuple-element.391, ...), kind=kOutput, calls=%fused_computation.18.clone.1 | convolution fusion | flops 275775488 | bytes 10553856 | tf_op jit(solution)/shard_map/while/body/eval_jaxpr/dot_general | solution.py:89
  292.3 5.0 %bitcast_dynamic-update-slice_fusion.18 = (bf16[2,128,8192]{2,1,0:T(8,128)(2,1)}, bf16[128,8192]{1,0:T(8,128)(2,1)S(1)}) fusion(bf16[2,128,8192]{2,1,0:T(8,128)(2,1)} %get-tuple-element.373, s32[]{:T(128)} %get-tuple-element.372, f32[8192]{0:T(1024)S(1)} %get-tuple-element.392, f32[2,128,8192]{2,1,0:T(8,128)} %get-tuple-element.391, ...), kind=kOutput, calls=%fused_computation.18.clone.1 | convolution fusion | flops 275775488 | bytes 10553856 | tf_op jit(solution)/shard_map/while/body/eval_jaxpr/dot_general | solution.py:89
  310.4 14.8 %collective-permute-done.29 = f32[2048,128]{1,0:T(8,128)S(1)} collective-permute-done((f32[2048,128]{1,0:T(8,128)S(1)}, f32[2048,128]{1,0:T(8,128)S(1)}, u32[]{:S(2)}, u32[]{:S(2)}) %collective-permute-start.29) | collective-permute-done | bytes 1048608 | tf_op jit(solution)/shard_map/ppermute | solution.py:30
  328.0 14.4 %collective-permute-done.30 = f32[1024,128]{1,0:T(8,128)S(1)} collective-permute-done((f32[1024,128]{1,0:T(8,128)S(1)}, f32[1024,128]{1,0:T(8,128)S(1)}, u32[]{:S(2)}, u32[]{:S(2)}) %collective-permute-start.30) | collective-permute-done | bytes 524320 | tf_op jit(solution)/shard_map/ppermute | solution.py:30
  342.5 6.9 %collective-permute-start.31 = (f32[512,128]{1,0:T(8,128)S(1)}, f32[512,128]{1,0:T(8,128)S(1)}, u32[]{:S(2)}, u32[]{:S(2)}) collective-permute-start(f32[512,128]{1,0:T(8,128)S(1)} %dynamic-slice_bitcast_fusion.3), channel_id=1, source_target_pairs={{0,32},{4,260},{8,40},{12,268},{16,48},{20,276},{24,56},{28,284},{... | collective-permute-start | bytes 786440 | tf_op jit(solution)/shard_map/ppermute | solution.py:30
  349.4 8.1 %collective-permute-done.31 = f32[512,128]{1,0:T(8,128)S(1)} collective-permute-done((f32[512,128]{1,0:T(8,128)S(1)}, f32[512,128]{1,0:T(8,128)S(1)}, u32[]{:S(2)}, u32[]{:S(2)}) %collective-permute-start.31) | collective-permute-done | bytes 262176 | tf_op jit(solution)/shard_map/ppermute | solution.py:30
  364.4 4.8 %collective-permute-start.33 = (f32[128,128]{1,0:T(8,128)S(1)}, f32[128,128]{1,0:T(8,128)S(1)}, u32[]{:S(2)}, u32[]{:S(2)}) collective-permute-start(f32[128,128]{1,0:T(8,128)S(1)} %dynamic-slice_bitcast_fusion.5), channel_id=1, source_target_pairs={{0,128},{4,20},{8,136},{12,28},{16,144},{20,4},{24,152},{28,12},{3... | collective-permute-start | bytes 196616 | tf_op jit(solution)/shard_map/ppermute | solution.py:30
  369.3 5.2 %collective-permute-start.36 = (f32[256,128]{1,0:T(8,128)S(1)}, f32[256,128]{1,0:T(8,128)S(1)}, u32[]{:S(2)}, u32[]{:S(2)}) collective-permute-start(f32[256,128]{1,0:T(8,128)S(1)} %bitcast_add_fusion.6), channel_id=1, source_target_pairs={{0,2},{1,3},{2,0},{3,1},{4,6},{5,7},{6,4},{7,5},{8,10},{9,11},{10,... | collective-permute-start | bytes 393224 | tf_op jit(solution)/shard_map/ppermute | solution.py:17
  374.6 7.8 %collective-permute-start.34 = (f32[64,128]{1,0:T(8,128)S(1)}, f32[64,128]{1,0:T(8,128)S(1)}, u32[]{:S(2)}, u32[]{:S(2)}) collective-permute-start(f32[64,128]{1,0:T(8,128)S(1)} %dynamic-slice_bitcast_fusion.6), channel_id=1, source_target_pairs={{0,256},{4,36},{8,264},{12,44},{16,272},{20,52},{24,280},{28,60},{... | collective-permute-start | bytes 98312 | tf_op jit(solution)/shard_map/ppermute | solution.py:30
  (167 shorter events, 164.7 us)
Async XLA Ops:
  1.4 12.6 %collective-permute-start = (bf16[64,128]{1,0:T(8,128)(2,1)S(1)}, bf16[64,128]{1,0:T(8,128)(2,1)S(1)}, u32[]{:S(2)}, u32[]{:S(2)}) collective-permute-start(bf16[64,128]{1,0:T(8,128)(2,1)S(1)} %get-tuple-element.160), channel_id=1, source_target_pairs={{0,256},{4,36},{8,264},{12,44},{16,272},{20,52},{24,280},{28,60},{... | collective-permute-start | bytes 49160 | tf_op jit(solution)/shard_map/ppermute | solution.py:30
  14.1 6.7 %collective-permute-start.1 = (bf16[128,128]{1,0:T(8,128)(2,1)S(1)}, bf16[128,128]{1,0:T(8,128)(2,1)S(1)}, u32[]{:S(2)}, u32[]{:S(2)}) collective-permute-start(bf16[128,128]{1,0:T(8,128)(2,1)S(1)} %bitcast.239), channel_id=1, source_target_pairs={{0,128},{4,20},{8,136},{12,28},{16,144},{20,4},{24,152},{28,12},{3... | collective-permute-start | bytes 98312 | tf_op jit(solution)/shard_map/ppermute | solution.py:30
  20.8 6.1 %collective-permute-start.2 = (bf16[256,128]{1,0:T(8,128)(2,1)S(1)}, bf16[256,128]{1,0:T(8,128)(2,1)S(1)}, u32[]{:S(2)}, u32[]{:S(2)}) collective-permute-start(bf16[256,128]{1,0:T(8,128)(2,1)S(1)} %bitcast.236), channel_id=1, source_target_pairs={{0,64},{4,12},{8,72},{12,4},{16,80},{20,28},{24,88},{28,20},{32,96... | collective-permute-start | bytes 196616 | tf_op jit(solution)/shard_map/ppermute | solution.py:30
  26.9 11.6 %collective-permute-start.3 = (bf16[512,128]{1,0:T(8,128)(2,1)S(1)}, bf16[512,128]{1,0:T(8,128)(2,1)S(1)}, u32[]{:S(2)}, u32[]{:S(2)}) collective-permute-start(bf16[512,128]{1,0:T(8,128)(2,1)S(1)} %bitcast.228), channel_id=1, source_target_pairs={{0,32},{4,260},{8,40},{12,268},{16,48},{20,276},{24,56},{28,284},{... | collective-permute-start | bytes 393224 | tf_op jit(solution)/shard_map/ppermute | solution.py:30
  38.6 12.1 %collective-permute-start.4 = (bf16[1024,128]{1,0:T(8,128)(2,1)S(1)}, bf16[1024,128]{1,0:T(8,128)(2,1)S(1)}, u32[]{:S(2)}, u32[]{:S(2)}) collective-permute-start(bf16[1024,128]{1,0:T(8,128)(2,1)S(1)} %bitcast.220), channel_id=1, source_target_pairs={{0,16},{4,132},{8,24},{12,140},{16,0},{20,148},{24,8},{28,156},{32... | collective-permute-start | bytes 786440 | tf_op jit(solution)/shard_map/ppermute | solution.py:30
  50.7 11.1 %collective-permute-start.5 = (bf16[2048,128]{1,0:T(8,128)(2,1)S(1)}, bf16[2048,128]{1,0:T(8,128)(2,1)S(1)}, u32[]{:S(2)}, u32[]{:S(2)}) collective-permute-start(bf16[2048,128]{1,0:T(8,128)(2,1)S(1)} %bitcast.218), channel_id=1, source_target_pairs={{0,8},{4,68},{8,0},{12,76},{16,24},{20,84},{24,16},{28,92},{32,40}... | collective-permute-start | bytes 1572872 | tf_op jit(solution)/shard_map/ppermute | solution.py:30
  97.7 5.8 %collective-permute-start.8 = (f32[8192]{0:T(1024)S(1)}, f32[8192]{0:T(1024)S(1)}, u32[]{:S(2)}, u32[]{:S(2)}) collective-permute-start(f32[8192]{0:T(1024)S(1)} %add.212), channel_id=1, source_target_pairs={{0,8},{4,12},{8,0},{12,4},{16,24},{20,28},{24,16},{28,20},{32,40},... | collective-permute-start | bytes 98312 | tf_op jit(solution)/shard_map/ppermute | solution.py:17
  103.6 6.8 %collective-permute-start.9 = (f32[8192]{0:T(1024)S(1)}, f32[8192]{0:T(1024)S(1)}, u32[]{:S(2)}, u32[]{:S(2)}) collective-permute-start(f32[8192]{0:T(1024)S(1)} %add.213), channel_id=1, source_target_pairs={{0,16},{4,20},{8,24},{12,28},{16,0},{20,4},{24,8},{28,12},{32,48},... | collective-permute-start | bytes 98312 | tf_op jit(solution)/shard_map/ppermute | solution.py:17
  110.3 9.9 %collective-permute-start.10 = (f32[8192]{0:T(1024)S(1)}, f32[8192]{0:T(1024)S(1)}, u32[]{:S(2)}, u32[]{:S(2)}) collective-permute-start(f32[8192]{0:T(1024)S(1)} %add.214), channel_id=1, source_target_pairs={{0,32},{4,36},{8,40},{12,44},{16,48},{20,52},{24,56},{28,60},{32,0... | collective-permute-start | bytes 98312 | tf_op jit(solution)/shard_map/ppermute | solution.py:17
  120.3 5.8 %collective-permute-start.11 = (f32[8192]{0:T(1024)S(1)}, f32[8192]{0:T(1024)S(1)}, u32[]{:S(2)}, u32[]{:S(2)}) collective-permute-start(f32[8192]{0:T(1024)S(1)} %add.215), channel_id=1, source_target_pairs={{0,64},{4,68},{8,72},{12,76},{16,80},{20,84},{24,88},{28,92},{32,9... | collective-permute-start | bytes 98312 | tf_op jit(solution)/shard_map/ppermute | solution.py:17
  126.1 6.7 %collective-permute-start.12 = (f32[8192]{0:T(1024)S(1)}, f32[8192]{0:T(1024)S(1)}, u32[]{:S(2)}, u32[]{:S(2)}) collective-permute-start(f32[8192]{0:T(1024)S(1)} %add.216), channel_id=1, source_target_pairs={{0,128},{4,132},{8,136},{12,140},{16,144},{20,148},{24,152},{28,15... | collective-permute-start | bytes 98312 | tf_op jit(solution)/shard_map/ppermute | solution.py:17
  132.8 11.0 %collective-permute-start.13 = (f32[8192]{0:T(1024)S(1)}, f32[8192]{0:T(1024)S(1)}, u32[]{:S(2)}, u32[]{:S(2)}) collective-permute-start(f32[8192]{0:T(1024)S(1)} %add.217), channel_id=1, source_target_pairs={{0,256},{4,260},{8,264},{12,268},{16,272},{20,276},{24,280},{28,28... | collective-permute-start | bytes 98312 | tf_op jit(solution)/shard_map/ppermute | solution.py:17
  163.1 5.8 %collective-permute-start.15 = (f32[8192]{0:T(1024)S(1)}, f32[8192]{0:T(1024)S(1)}, u32[]{:S(2)}, u32[]{:S(2)}) collective-permute-start(f32[8192]{0:T(1024)S(1)} %add.219), channel_id=1, source_target_pairs={{0,8},{4,12},{8,0},{12,4},{16,24},{20,28},{24,16},{28,20},{32,40},... | collective-permute-start | bytes 98312 | tf_op jit(solution)/shard_map/ppermute | solution.py:17
  168.9 6.7 %collective-permute-start.16 = (f32[8192]{0:T(1024)S(1)}, f32[8192]{0:T(1024)S(1)}, u32[]{:S(2)}, u32[]{:S(2)}) collective-permute-start(f32[8192]{0:T(1024)S(1)} %add.220), channel_id=1, source_target_pairs={{0,16},{4,20},{8,24},{12,28},{16,0},{20,4},{24,8},{28,12},{32,48},... | collective-permute-start | bytes 98312 | tf_op jit(solution)/shard_map/ppermute | solution.py:17
  175.6 9.9 %collective-permute-start.17 = (f32[8192]{0:T(1024)S(1)}, f32[8192]{0:T(1024)S(1)}, u32[]{:S(2)}, u32[]{:S(2)}) collective-permute-start(f32[8192]{0:T(1024)S(1)} %add.221), channel_id=1, source_target_pairs={{0,32},{4,36},{8,40},{12,44},{16,48},{20,52},{24,56},{28,60},{32,0... | collective-permute-start | bytes 98312 | tf_op jit(solution)/shard_map/ppermute | solution.py:17
  185.5 5.8 %collective-permute-start.18 = (f32[8192]{0:T(1024)S(1)}, f32[8192]{0:T(1024)S(1)}, u32[]{:S(2)}, u32[]{:S(2)}) collective-permute-start(f32[8192]{0:T(1024)S(1)} %add.222), channel_id=1, source_target_pairs={{0,64},{4,68},{8,72},{12,76},{16,80},{20,84},{24,88},{28,92},{32,9... | collective-permute-start | bytes 98312 | tf_op jit(solution)/shard_map/ppermute | solution.py:17
  191.3 6.7 %collective-permute-start.19 = (f32[8192]{0:T(1024)S(1)}, f32[8192]{0:T(1024)S(1)}, u32[]{:S(2)}, u32[]{:S(2)}) collective-permute-start(f32[8192]{0:T(1024)S(1)} %add.223), channel_id=1, source_target_pairs={{0,128},{4,132},{8,136},{12,140},{16,144},{20,148},{24,152},{28,15... | collective-permute-start | bytes 98312 | tf_op jit(solution)/shard_map/ppermute | solution.py:17
  198.0 10.0 %collective-permute-start.20 = (f32[8192]{0:T(1024)S(1)}, f32[8192]{0:T(1024)S(1)}, u32[]{:S(2)}, u32[]{:S(2)}) collective-permute-start(f32[8192]{0:T(1024)S(1)} %add.224), channel_id=1, source_target_pairs={{0,256},{4,260},{8,264},{12,268},{16,272},{20,276},{24,280},{28,28... | collective-permute-start | bytes 98312 | tf_op jit(solution)/shard_map/ppermute | solution.py:17
  229.8 5.8 %collective-permute-start.22 = (f32[8192]{0:T(1024)S(1)}, f32[8192]{0:T(1024)S(1)}, u32[]{:S(2)}, u32[]{:S(2)}) collective-permute-start(f32[8192]{0:T(1024)S(1)} %add.226), channel_id=1, source_target_pairs={{0,8},{4,12},{8,0},{12,4},{16,24},{20,28},{24,16},{28,20},{32,40},... | collective-permute-start | bytes 98312 | tf_op jit(solution)/shard_map/ppermute | solution.py:17
  235.7 6.7 %collective-permute-start.23 = (f32[8192]{0:T(1024)S(1)}, f32[8192]{0:T(1024)S(1)}, u32[]{:S(2)}, u32[]{:S(2)}) collective-permute-start(f32[8192]{0:T(1024)S(1)} %add.227), channel_id=1, source_target_pairs={{0,16},{4,20},{8,24},{12,28},{16,0},{20,4},{24,8},{28,12},{32,48},... | collective-permute-start | bytes 98312 | tf_op jit(solution)/shard_map/ppermute | solution.py:17
  242.4 9.7 %collective-permute-start.24 = (f32[8192]{0:T(1024)S(1)}, f32[8192]{0:T(1024)S(1)}, u32[]{:S(2)}, u32[]{:S(2)}) collective-permute-start(f32[8192]{0:T(1024)S(1)} %add.228), channel_id=1, source_target_pairs={{0,32},{4,36},{8,40},{12,44},{16,48},{20,52},{24,56},{28,60},{32,0... | collective-permute-start | bytes 98312 | tf_op jit(solution)/shard_map/ppermute | solution.py:17
  257.9 6.7 %collective-permute-start.26 = (f32[8192]{0:T(1024)S(1)}, f32[8192]{0:T(1024)S(1)}, u32[]{:S(2)}, u32[]{:S(2)}) collective-permute-start(f32[8192]{0:T(1024)S(1)} %add.230), channel_id=1, source_target_pairs={{0,128},{4,132},{8,136},{12,140},{16,144},{20,148},{24,152},{28,15... | collective-permute-start | bytes 98312 | tf_op jit(solution)/shard_map/ppermute | solution.py:17
  264.6 9.9 %collective-permute-start.27 = (f32[8192]{0:T(1024)S(1)}, f32[8192]{0:T(1024)S(1)}, u32[]{:S(2)}, u32[]{:S(2)}) collective-permute-start(f32[8192]{0:T(1024)S(1)} %add.231), channel_id=1, source_target_pairs={{0,256},{4,260},{8,264},{12,268},{16,272},{20,276},{24,280},{28,28... | collective-permute-start | bytes 98312 | tf_op jit(solution)/shard_map/ppermute | solution.py:17
  301.9 6.1 %collective-permute-start.28 = (f32[4096,128]{1,0:T(8,128)S(1)}, f32[4096,128]{1,0:T(8,128)S(1)}, u32[]{:S(2)}, u32[]{:S(2)}) collective-permute-start(f32[4096,128]{1,0:T(8,128)S(1)} %get-tuple-element.169), channel_id=1, source_target_pairs={{0,4},{4,0},{8,12},{12,8},{16,20},{20,16},{24,28},{28,24},{32,36},... | collective-permute-start | bytes 6291464 | tf_op jit(solution)/shard_map/ppermute | solution.py:30
  308.5 16.7 %collective-permute-start.29 = (f32[2048,128]{1,0:T(8,128)S(1)}, f32[2048,128]{1,0:T(8,128)S(1)}, u32[]{:S(2)}, u32[]{:S(2)}) collective-permute-start(f32[2048,128]{1,0:T(8,128)S(1)} %dynamic-slice_bitcast_fusion.1), channel_id=1, source_target_pairs={{0,8},{4,68},{8,0},{12,76},{16,24},{20,84},{24,16},{28,92},{32,40}... | collective-permute-start | bytes 3145736 | tf_op jit(solution)/shard_map/ppermute | solution.py:30
  325.3 17.0 %collective-permute-start.30 = (f32[1024,128]{1,0:T(8,128)S(1)}, f32[1024,128]{1,0:T(8,128)S(1)}, u32[]{:S(2)}, u32[]{:S(2)}) collective-permute-start(f32[1024,128]{1,0:T(8,128)S(1)} %dynamic-slice_bitcast_fusion.2), channel_id=1, source_target_pairs={{0,16},{4,132},{8,24},{12,140},{16,0},{20,148},{24,8},{28,156},{32... | collective-permute-start | bytes 1572872 | tf_op jit(solution)/shard_map/ppermute | solution.py:30
  342.5 15.0 %collective-permute-start.31 = (f32[512,128]{1,0:T(8,128)S(1)}, f32[512,128]{1,0:T(8,128)S(1)}, u32[]{:S(2)}, u32[]{:S(2)}) collective-permute-start(f32[512,128]{1,0:T(8,128)S(1)} %dynamic-slice_bitcast_fusion.3), channel_id=1, source_target_pairs={{0,32},{4,260},{8,40},{12,268},{16,48},{20,276},{24,56},{28,284},{... | collective-permute-start | bytes 786440 | tf_op jit(solution)/shard_map/ppermute | solution.py:30
  357.5 6.9 %collective-permute-start.32 = (f32[256,128]{1,0:T(8,128)S(1)}, f32[256,128]{1,0:T(8,128)S(1)}, u32[]{:S(2)}, u32[]{:S(2)}) collective-permute-start(f32[256,128]{1,0:T(8,128)S(1)} %dynamic-slice_bitcast_fusion.4), channel_id=1, source_target_pairs={{0,64},{4,12},{8,72},{12,4},{16,80},{20,28},{24,88},{28,20},{32,96... | collective-permute-start | bytes 393224 | tf_op jit(solution)/shard_map/ppermute | solution.py:30
  360.9 8.3 %collective-permute-start.35 = (f32[256,128]{1,0:T(8,128)S(1)}, f32[256,128]{1,0:T(8,128)S(1)}, u32[]{:S(2)}, u32[]{:S(2)}) collective-permute-start(f32[256,128]{1,0:T(8,128)S(1)} %bitcast.238), channel_id=1, source_target_pairs={{0,1},{1,0},{2,3},{3,2},{4,5},{5,4},{6,7},{7,6},{8,9},{9,8},{10,11... | collective-permute-start | bytes 393224 | tf_op jit(solution)/shard_map/ppermute | solution.py:17
  364.4 10.1 %collective-permute-start.33 = (f32[128,128]{1,0:T(8,128)S(1)}, f32[128,128]{1,0:T(8,128)S(1)}, u32[]{:S(2)}, u32[]{:S(2)}) collective-permute-start(f32[128,128]{1,0:T(8,128)S(1)} %dynamic-slice_bitcast_fusion.5), channel_id=1, source_target_pairs={{0,128},{4,20},{8,136},{12,28},{16,144},{20,4},{24,152},{28,12},{3... | collective-permute-start | bytes 196616 | tf_op jit(solution)/shard_map/ppermute | solution.py:30
  369.3 13.1 %collective-permute-start.36 = (f32[256,128]{1,0:T(8,128)S(1)}, f32[256,128]{1,0:T(8,128)S(1)}, u32[]{:S(2)}, u32[]{:S(2)}) collective-permute-start(f32[256,128]{1,0:T(8,128)S(1)} %bitcast_add_fusion.6), channel_id=1, source_target_pairs={{0,2},{1,3},{2,0},{3,1},{4,6},{5,7},{6,4},{7,5},{8,10},{9,11},{10,... | collective-permute-start | bytes 393224 | tf_op jit(solution)/shard_map/ppermute | solution.py:17
  374.6 9.7 %collective-permute-start.34 = (f32[64,128]{1,0:T(8,128)S(1)}, f32[64,128]{1,0:T(8,128)S(1)}, u32[]{:S(2)}, u32[]{:S(2)}) collective-permute-start(f32[64,128]{1,0:T(8,128)S(1)} %dynamic-slice_bitcast_fusion.6), channel_id=1, source_target_pairs={{0,256},{4,36},{8,264},{12,44},{16,272},{20,52},{24,280},{28,60},{... | collective-permute-start | bytes 98312 | tf_op jit(solution)/shard_map/ppermute | solution.py:30
  (7 other events, 30.9 us)

commit v6 on v5

--- a/solution.py
+++ b/solution.py
@@ -21,7 +21,7 @@
     return int(math.log2(lax.axis_size(axis)))
 
 
-GATHER_ORDER = ((6, 5, 4, 3, 2, 1, 0), (3, 2, 1, 6, 5, 4, 0))
+GATHER_ORDER = ((6, 3, 5, 2, 4, 1, 0), (3, 6, 2, 5, 1, 4, 0))
 
 
 def core_swap(x, axis, step, orders):
@@ -36,8 +36,9 @@
 
 
 def swap_halves(x):
-    rows = x.shape[0]
-    return x.reshape((8, 8, rows // 64) + x.shape[1:]).swapaxes(0, 1).reshape(x.shape)
+    shape = (2,) * 6 + (x.shape[0] // 64,) + x.shape[1:]
+    dims = (1, 0, 3, 2, 5, 4) + tuple(range(6, len(shape)))
+    return x.reshape(shape).transpose(dims).reshape(x.shape)
 
 
 def gather_blocks(x, axis):
@@ -80,7 +81,7 @@
     for k in range(bits(axis)):
         other = swap(x, axis, k)
         if k == 0:
-            other = other.reshape(2, 8, 8, -1).swapaxes(1, 2).reshape(x.shape)
+            other = jax.vmap(swap_halves)(other.reshape(2, -1, 1)).reshape(x.shape)
         x = x + other
     return x
 

time: 387 us -> 380 us (0.982)
  waiting for transfers between devices: 125 us -> 116 us
    ppermute x14, waiting for transfers between devices: 71.4 us -> 64.6 us  [core_swap(): return lax.ppermute(x, axis, pairs)]
where the time goes in v6:
time: 380 us; the launch traced here: 377 us
  starting transfers between devices  165 us (43%)
  waiting for transfers between devices  116 us (31%)
  blocking collectives  37.2 us (10%)
  other arithmetic  35.1 us (9%)
  matrix products  18.2 us (5%)
  local copies, waits for them, and re-layouts  4.03 us (1%)
    ppermute x23, starting transfers between devices, swap(): return lax.ppermute(x, axis, [(i, i ^ 1 << k) for i in range(n)])  100 us
    ppermute x14, starting transfers between devices, core_swap(): return lax.ppermute(x, axis, pairs)  64.7 us
    ppermute x14, waiting for transfers between devices, core_swap(): return lax.ppermute(x, axis, pairs)  64.6 us
    ppermute x23, waiting for transfers between devices, swap(): return lax.ppermute(x, axis, [(i, i ^ 1 << k) for i in range(n)])  51.9 us
    psum x3, blocking collectives, per_device(): row_scale = 1.0 / lax.psum(partial_rows, 'proto')  25.2 us
    dot_general x6, matrix products, contract_rows(): lax.dot_general(left, right, (((1,), (1,)), ((), ())), preferred_element_...  13.2 us
    reduce_sum x3, other arithmetic, per_device(): partial_cols = jnp.sum((row_scale * shift)[:, None] * base_local, axis=0)  13 us
    reduce_sum x3, other arithmetic, per_device(): partial_rows = shift * jnp.sum(base_local * col_scale[None, :], axis=1)  12.5 us
  transfers between devices with their start and end apart: 37, of which 34 were waited for; matrix products, arithmetic and copies ran while one was open for 0% of the time, Pallas kernels for 0%

profile of v6, /device:TPU:6, one launch (start us, length us, event | category | flops | bytes accessed | tf_op | source)
XLA Modules:
  0.0 377.3 jit_solution(7065022139604765089)
XLA Ops:
  1.4 10.9 %collective-permute-start = (bf16[64,128]{1,0:T(8,128)(2,1)S(1)}, bf16[64,128]{1,0:T(8,128)(2,1)S(1)}, u32[]{:S(2)}, u32[]{:S(2)}) collective-permute-start(bf16[64,128]{1,0:T(8,128)(2,1)S(1)} %get-tuple-element.160), channel_id=1, source_target_pairs={{0,256},{4,36},{8,264},{12,44},{16,272},{20,52},{24,280},{28,60},{... | collective-permute-start | bytes 49160 | tf_op jit(solution)/shard_map/ppermute | solution.py:30
  14.1 7.7 %collective-permute-start.1 = (bf16[128,128]{1,0:T(8,128)(2,1)S(1)}, bf16[128,128]{1,0:T(8,128)(2,1)S(1)}, u32[]{:S(2)}, u32[]{:S(2)}) collective-permute-start(bf16[128,128]{1,0:T(8,128)(2,1)S(1)} %bitcast.239), channel_id=1, source_target_pairs={{0,32},{4,260},{8,40},{12,268},{16,48},{20,276},{24,56},{28,284},{... | collective-permute-start | bytes 98312 | tf_op jit(solution)/shard_map/ppermute | solution.py:30
  23.8 4.4 %collective-permute-start.2 = (bf16[256,128]{1,0:T(8,128)(2,1)S(1)}, bf16[256,128]{1,0:T(8,128)(2,1)S(1)}, u32[]{:S(2)}, u32[]{:S(2)}) collective-permute-start(bf16[256,128]{1,0:T(8,128)(2,1)S(1)} %bitcast.236), channel_id=1, source_target_pairs={{0,128},{4,20},{8,136},{12,28},{16,144},{20,4},{24,152},{28,12},{3... | collective-permute-start | bytes 196616 | tf_op jit(solution)/shard_map/ppermute | solution.py:30
  30.9 4.6 %collective-permute-start.3 = (bf16[512,128]{1,0:T(8,128)(2,1)S(1)}, bf16[512,128]{1,0:T(8,128)(2,1)S(1)}, u32[]{:S(2)}, u32[]{:S(2)}) collective-permute-start(bf16[512,128]{1,0:T(8,128)(2,1)S(1)} %bitcast.228), channel_id=1, source_target_pairs={{0,16},{4,132},{8,24},{12,140},{16,0},{20,148},{24,8},{28,156},{32... | collective-permute-start | bytes 393224 | tf_op jit(solution)/shard_map/ppermute | solution.py:30
  35.6 4.4 %collective-permute-done.3 = bf16[512,128]{1,0:T(8,128)(2,1)S(1)} collective-permute-done((bf16[512,128]{1,0:T(8,128)(2,1)S(1)}, bf16[512,128]{1,0:T(8,128)(2,1)S(1)}, u32[]{:S(2)}, u32[]{:S(2)}) %collective-permute-start.3) | collective-permute-done | bytes 131104 | tf_op jit(solution)/shard_map/ppermute | solution.py:30
  43.7 5.3 %collective-permute-done.4 = bf16[1024,128]{1,0:T(8,128)(2,1)S(1)} collective-permute-done((bf16[1024,128]{1,0:T(8,128)(2,1)S(1)}, bf16[1024,128]{1,0:T(8,128)(2,1)S(1)}, u32[]{:S(2)}, u32[]{:S(2)}) %collective-permute-start.4) | collective-permute-done | bytes 262176 | tf_op jit(solution)/shard_map/ppermute | solution.py:30
  51.3 8.8 %collective-permute-done.5 = bf16[2048,128]{1,0:T(8,128)(2,1)S(1)} collective-permute-done((bf16[2048,128]{1,0:T(8,128)(2,1)S(1)}, bf16[2048,128]{1,0:T(8,128)(2,1)S(1)}, u32[]{:S(2)}, u32[]{:S(2)}) %collective-permute-start.5) | collective-permute-done | bytes 524320 | tf_op jit(solution)/shard_map/ppermute | solution.py:30
  66.4 6.8 %while.37 = (s32[]{:T(128)}, f32[2,128,8192]{2,1,0:T(8,128)}, f32[2,128]{1,0:T(2,128)S(1)}, bf16[2,128,128]{2,1,0:T(8,128)(2,1)S(1)}, bf16[8192,128]{1,0:T(8,128)(2,1)S(1)}, /*index=5*/s32[]{:T(128)}, s32[]{:T(128)}) while((s32[]{:T(128)}, f32[2,128,8192]{2,1,0:T(8,128)}, f32[2,128]{1,0:T(2,128)S(1)}, bf16[2,128,128]{2,1,0:T(8,128)(2,1)S(1)}, ...), condition=%wide.region_2.3_spmd, body=%wide.region_0.2_spmd.sunk | while | flops 271581056 | bytes 14715477 | solution.py:116
  76.5 11.9 %all-gather.1 = f32[4,3,256]{2,1,0:T(4,128)S(1)} all-gather(f32[1,3,256]{2,1,0:T(4,128)S(1)} %maximum_bitcast_fusion), channel_id=2, replica_groups=mesh['dp'=128,'proto'=4] {'proto'}, dimensions={0}, use_global_device_ids=true | all-gather | bytes 15360 | tf_op jit(solution)/shard_map/all_gather | solution.py:132
  109.0 7.3 %collective-permute-start.10 = (f32[8192]{0:T(1024)S(1)}, f32[8192]{0:T(1024)S(1)}, u32[]{:S(2)}, u32[]{:S(2)}) collective-permute-start(f32[8192]{0:T(1024)S(1)} %add.214), channel_id=1, source_target_pairs={{0,32},{4,36},{8,40},{12,44},{16,48},{20,52},{24,56},{28,60},{32,0... | collective-permute-start | bytes 98312 | tf_op jit(solution)/shard_map/ppermute | solution.py:17
  124.9 5.0 %collective-permute-start.12 = (f32[8192]{0:T(1024)S(1)}, f32[8192]{0:T(1024)S(1)}, u32[]{:S(2)}, u32[]{:S(2)}) collective-permute-start(f32[8192]{0:T(1024)S(1)} %add.216), channel_id=1, source_target_pairs={{0,128},{4,132},{8,136},{12,140},{16,144},{20,148},{24,152},{28,15... | collective-permute-start | bytes 98312 | tf_op jit(solution)/shard_map/ppermute | solution.py:17
  131.8 8.1 %collective-permute-start.13 = (f32[8192]{0:T(1024)S(1)}, f32[8192]{0:T(1024)S(1)}, u32[]{:S(2)}, u32[]{:S(2)}) collective-permute-start(f32[8192]{0:T(1024)S(1)} %add.217), channel_id=1, source_target_pairs={{0,256},{4,260},{8,264},{12,268},{16,272},{20,276},{24,280},{28,28... | collective-permute-start | bytes 98312 | tf_op jit(solution)/shard_map/ppermute | solution.py:17
  146.0 7.5 %psum.21 = f32[256]{0:T(256)S(1)} all-reduce(f32[256]{0:T(256)S(1)} %get-tuple-element.157), channel_id=1, replica_groups=mesh['dp'=128,'proto'=4] {'proto'}, use_global_device_ids=true, to_apply=%region_9.10 | all-reduce | flops 256 | bytes 2048 | tf_op jit(solution)/shard_map/psum | solution.py:146
  174.0 6.7 %collective-permute-start.17 = (f32[8192]{0:T(1024)S(1)}, f32[8192]{0:T(1024)S(1)}, u32[]{:S(2)}, u32[]{:S(2)}) collective-permute-start(f32[8192]{0:T(1024)S(1)} %add.221), channel_id=1, source_target_pairs={{0,32},{4,36},{8,40},{12,44},{16,48},{20,52},{24,56},{28,60},{32,0... | collective-permute-start | bytes 98312 | tf_op jit(solution)/shard_map/ppermute | solution.py:17
  189.5 4.7 %collective-permute-start.19 = (f32[8192]{0:T(1024)S(1)}, f32[8192]{0:T(1024)S(1)}, u32[]{:S(2)}, u32[]{:S(2)}) collective-permute-start(f32[8192]{0:T(1024)S(1)} %add.223), channel_id=1, source_target_pairs={{0,128},{4,132},{8,136},{12,140},{16,144},{20,148},{24,152},{28,15... | collective-permute-start | bytes 98312 | tf_op jit(solution)/shard_map/ppermute | solution.py:17
  196.2 8.0 %collective-permute-start.20 = (f32[8192]{0:T(1024)S(1)}, f32[8192]{0:T(1024)S(1)}, u32[]{:S(2)}, u32[]{:S(2)}) collective-permute-start(f32[8192]{0:T(1024)S(1)} %add.224), channel_id=1, source_target_pairs={{0,256},{4,260},{8,264},{12,268},{16,272},{20,276},{24,280},{28,28... | collective-permute-start | bytes 98312 | tf_op jit(solution)/shard_map/ppermute | solution.py:17
  210.3 10.0 %psum.22 = f32[256]{0:T(256)S(1)} all-reduce(f32[256]{0:T(256)S(1)} %bitcast_multiply_fusion.2), channel_id=1, replica_groups=mesh['dp'=128,'proto'=4] {'proto'}, use_global_device_ids=true, to_apply=%region_12.13 | all-reduce | flops 256 | bytes 2048 | tf_op jit(solution)/shard_map/psum | solution.py:146
  220.3 4.3 %multiply_reduce_fusion.1 = f32[8192]{0:T(1024)S(1)} fusion(f32[2,128,8192]{2,1,0:T(8,128)} %get-tuple-element.369, f32[2,128]{1,0:T(2,128)S(1)} %fusion.29), kind=kLoop, calls=%fused_computation.33 | loop fusion | flops 4186112 | bytes 8422400 | tf_op jit(solution)/shard_map/reduce_sum | solution.py:143
  240.5 6.8 %collective-permute-start.24 = (f32[8192]{0:T(1024)S(1)}, f32[8192]{0:T(1024)S(1)}, u32[]{:S(2)}, u32[]{:S(2)}) collective-permute-start(f32[8192]{0:T(1024)S(1)} %add.228), channel_id=1, source_target_pairs={{0,32},{4,36},{8,40},{12,44},{16,48},{20,52},{24,56},{28,60},{32,0... | collective-permute-start | bytes 98312 | tf_op jit(solution)/shard_map/ppermute | solution.py:17
  256.0 4.6 %collective-permute-start.26 = (f32[8192]{0:T(1024)S(1)}, f32[8192]{0:T(1024)S(1)}, u32[]{:S(2)}, u32[]{:S(2)}) collective-permute-start(f32[8192]{0:T(1024)S(1)} %add.230), channel_id=1, source_target_pairs={{0,128},{4,132},{8,136},{12,140},{16,144},{20,148},{24,152},{28,15... | collective-permute-start | bytes 98312 | tf_op jit(solution)/shard_map/ppermute | solution.py:17
  262.7 8.2 %collective-permute-start.27 = (f32[8192]{0:T(1024)S(1)}, f32[8192]{0:T(1024)S(1)}, u32[]{:S(2)}, u32[]{:S(2)}) collective-permute-start(f32[8192]{0:T(1024)S(1)} %add.231), channel_id=1, source_target_pairs={{0,256},{4,260},{8,264},{12,268},{16,272},{20,276},{24,280},{28,28... | collective-permute-start | bytes 98312 | tf_op jit(solution)/shard_map/ppermute | solution.py:17
  276.7 7.7 %psum.23 = f32[256]{0:T(256)S(1)} all-reduce(f32[256]{0:T(256)S(1)} %bitcast_multiply_fusion.1), channel_id=1, replica_groups=mesh['dp'=128,'proto'=4] {'proto'}, use_global_device_ids=true, to_apply=%region_15.16 | all-reduce | flops 256 | bytes 2048 | tf_op jit(solution)/shard_map/psum | solution.py:146
  284.4 11.7 %while.38 = (s32[]{:T(128)}, bf16[2,128,8192]{2,1,0:T(8,128)(2,1)}, f32[2,128,128]{2,1,0:T(8,128)S(1)}, bf16[2,128,128]{2,1,0:T(8,128)(2,1)S(1)}, bf16[8192,128]...) while((s32[]{:T(128)}, bf16[2,128,8192]{2,1,0:T(8,128)(2,1)}, ...), condition=%wide.region_17.18_spmd, body=%wide.region_16.17_spmd.sunk | while | flops 544227328 | bytes 14816889 | solution.py:158
  284.5 5.1 %bitcast_dynamic-update-slice_fusion.18 = (bf16[2,128,8192]{2,1,0:T(8,128)(2,1)}, bf16[128,8192]{1,0:T(8,128)(2,1)S(1)}) fusion(bf16[2,128,8192]{2,1,0:T(8,128)(2,1)} %get-tuple-element.373, s32[]{:T(128)} %get-tuple-element.372, f32[8192]{0:T(1024)S(1)} %get-tuple-element.392, f32[2,128,8192]{2,1,0:T(8,128)} %get-tuple-element.391, ...), kind=kOutput, calls=%fused_computation.18.clone.1 | convolution fusion | flops 275775488 | bytes 10553856 | tf_op jit(solution)/shard_map/while/body/eval_jaxpr/dot_general | solution.py:90
  290.3 5.0 %bitcast_dynamic-update-slice_fusion.18 = (bf16[2,128,8192]{2,1,0:T(8,128)(2,1)}, bf16[128,8192]{1,0:T(8,128)(2,1)S(1)}) fusion(bf16[2,128,8192]{2,1,0:T(8,128)(2,1)} %get-tuple-element.373, s32[]{:T(128)} %get-tuple-element.372, f32[8192]{0:T(1024)S(1)} %get-tuple-element.392, f32[2,128,8192]{2,1,0:T(8,128)} %get-tuple-element.391, ...), kind=kOutput, calls=%fused_computation.18.clone.1 | convolution fusion | flops 275775488 | bytes 10553856 | tf_op jit(solution)/shard_map/while/body/eval_jaxpr/dot_general | solution.py:90
  308.6 14.6 %collective-permute-done.29 = f32[2048,128]{1,0:T(8,128)S(1)} collective-permute-done((f32[2048,128]{1,0:T(8,128)S(1)}, f32[2048,128]{1,0:T(8,128)S(1)}, u32[]{:S(2)}, u32[]{:S(2)}) %collective-permute-start.29) | collective-permute-done | bytes 1048608 | tf_op jit(solution)/shard_map/ppermute | solution.py:30
  326.7 7.7 %collective-permute-done.30 = f32[1024,128]{1,0:T(8,128)S(1)} collective-permute-done((f32[1024,128]{1,0:T(8,128)S(1)}, f32[1024,128]{1,0:T(8,128)S(1)}, u32[]{:S(2)}, u32[]{:S(2)}) %collective-permute-start.30) | collective-permute-done | bytes 524320 | tf_op jit(solution)/shard_map/ppermute | solution.py:30
  337.5 8.7 %collective-permute-done.31 = f32[512,128]{1,0:T(8,128)S(1)} collective-permute-done((f32[512,128]{1,0:T(8,128)S(1)}, f32[512,128]{1,0:T(8,128)S(1)}, u32[]{:S(2)}, u32[]{:S(2)}) %collective-permute-start.31) | collective-permute-done | bytes 262176 | tf_op jit(solution)/shard_map/ppermute | solution.py:30
  346.3 4.6 %collective-permute-start.32 = (f32[256,128]{1,0:T(8,128)S(1)}, f32[256,128]{1,0:T(8,128)S(1)}, u32[]{:S(2)}, u32[]{:S(2)}) collective-permute-start(f32[256,128]{1,0:T(8,128)S(1)} %dynamic-slice_bitcast_fusion.4), channel_id=1, source_target_pairs={{0,128},{4,20},{8,136},{12,28},{16,144},{20,4},{24,152},{28,12},{3... | collective-permute-start | bytes 393224 | tf_op jit(solution)/shard_map/ppermute | solution.py:30
  355.5 6.7 %collective-permute-start.33 = (f32[128,128]{1,0:T(8,128)S(1)}, f32[128,128]{1,0:T(8,128)S(1)}, u32[]{:S(2)}, u32[]{:S(2)}) collective-permute-start(f32[128,128]{1,0:T(8,128)S(1)} %dynamic-slice_bitcast_fusion.5), channel_id=1, source_target_pairs={{0,32},{4,260},{8,40},{12,268},{16,48},{20,276},{24,56},{28,284},{... | collective-permute-start | bytes 196616 | tf_op jit(solution)/shard_map/ppermute | solution.py:30
  362.2 4.6 %collective-permute-start.36 = (f32[256,128]{1,0:T(8,128)S(1)}, f32[256,128]{1,0:T(8,128)S(1)}, u32[]{:S(2)}, u32[]{:S(2)}) collective-permute-start(f32[256,128]{1,0:T(8,128)S(1)} %bitcast_add_fusion.7), channel_id=1, source_target_pairs={{0,2},{1,3},{2,0},{3,1},{4,6},{5,7},{6,4},{7,5},{8,10},{9,11},{10,... | collective-permute-start | bytes 393224 | tf_op jit(solution)/shard_map/ppermute | solution.py:17
  366.8 8.0 %collective-permute-start.34 = (f32[64,128]{1,0:T(8,128)S(1)}, f32[64,128]{1,0:T(8,128)S(1)}, u32[]{:S(2)}, u32[]{:S(2)}) collective-permute-start(f32[64,128]{1,0:T(8,128)S(1)} %dynamic-slice_bitcast_fusion.6), channel_id=1, source_target_pairs={{0,256},{4,36},{8,264},{12,44},{16,272},{20,52},{24,280},{28,60},{... | collective-permute-start | bytes 98312 | tf_op jit(solution)/shard_map/ppermute | solution.py:30
  (167 shorter events, 166.9 us)
Async XLA Ops:
  1.4 12.6 %collective-permute-start = (bf16[64,128]{1,0:T(8,128)(2,1)S(1)}, bf16[64,128]{1,0:T(8,128)(2,1)S(1)}, u32[]{:S(2)}, u32[]{:S(2)}) collective-permute-start(bf16[64,128]{1,0:T(8,128)(2,1)S(1)} %get-tuple-element.160), channel_id=1, source_target_pairs={{0,256},{4,36},{8,264},{12,44},{16,272},{20,52},{24,280},{28,60},{... | collective-permute-start | bytes 49160 | tf_op jit(solution)/shard_map/ppermute | solution.py:30
  14.1 9.7 %collective-permute-start.1 = (bf16[128,128]{1,0:T(8,128)(2,1)S(1)}, bf16[128,128]{1,0:T(8,128)(2,1)S(1)}, u32[]{:S(2)}, u32[]{:S(2)}) collective-permute-start(bf16[128,128]{1,0:T(8,128)(2,1)S(1)} %bitcast.239), channel_id=1, source_target_pairs={{0,32},{4,260},{8,40},{12,268},{16,48},{20,276},{24,56},{28,284},{... | collective-permute-start | bytes 98312 | tf_op jit(solution)/shard_map/ppermute | solution.py:30
  23.8 7.0 %collective-permute-start.2 = (bf16[256,128]{1,0:T(8,128)(2,1)S(1)}, bf16[256,128]{1,0:T(8,128)(2,1)S(1)}, u32[]{:S(2)}, u32[]{:S(2)}) collective-permute-start(bf16[256,128]{1,0:T(8,128)(2,1)S(1)} %bitcast.236), channel_id=1, source_target_pairs={{0,128},{4,20},{8,136},{12,28},{16,144},{20,4},{24,152},{28,12},{3... | collective-permute-start | bytes 196616 | tf_op jit(solution)/shard_map/ppermute | solution.py:30
  30.9 9.2 %collective-permute-start.3 = (bf16[512,128]{1,0:T(8,128)(2,1)S(1)}, bf16[512,128]{1,0:T(8,128)(2,1)S(1)}, u32[]{:S(2)}, u32[]{:S(2)}) collective-permute-start(bf16[512,128]{1,0:T(8,128)(2,1)S(1)} %bitcast.228), channel_id=1, source_target_pairs={{0,16},{4,132},{8,24},{12,140},{16,0},{20,148},{24,8},{28,156},{32... | collective-permute-start | bytes 393224 | tf_op jit(solution)/shard_map/ppermute | solution.py:30
  40.1 9.0 %collective-permute-start.4 = (bf16[1024,128]{1,0:T(8,128)(2,1)S(1)}, bf16[1024,128]{1,0:T(8,128)(2,1)S(1)}, u32[]{:S(2)}, u32[]{:S(2)}) collective-permute-start(bf16[1024,128]{1,0:T(8,128)(2,1)S(1)} %bitcast.220), channel_id=1, source_target_pairs={{0,64},{4,12},{8,72},{12,4},{16,80},{20,28},{24,88},{28,20},{32,96... | collective-permute-start | bytes 786440 | tf_op jit(solution)/shard_map/ppermute | solution.py:30
  49.0 11.1 %collective-permute-start.5 = (bf16[2048,128]{1,0:T(8,128)(2,1)S(1)}, bf16[2048,128]{1,0:T(8,128)(2,1)S(1)}, u32[]{:S(2)}, u32[]{:S(2)}) collective-permute-start(bf16[2048,128]{1,0:T(8,128)(2,1)S(1)} %bitcast.218), channel_id=1, source_target_pairs={{0,8},{4,68},{8,0},{12,76},{16,24},{20,84},{24,16},{28,92},{32,40}... | collective-permute-start | bytes 1572872 | tf_op jit(solution)/shard_map/ppermute | solution.py:30
  96.2 5.8 %collective-permute-start.8 = (f32[8192]{0:T(1024)S(1)}, f32[8192]{0:T(1024)S(1)}, u32[]{:S(2)}, u32[]{:S(2)}) collective-permute-start(f32[8192]{0:T(1024)S(1)} %add.212), channel_id=1, source_target_pairs={{0,8},{4,12},{8,0},{12,4},{16,24},{20,28},{24,16},{28,20},{32,40},... | collective-permute-start | bytes 98312 | tf_op jit(solution)/shard_map/ppermute | solution.py:17
  102.0 7.0 %collective-permute-start.9 = (f32[8192]{0:T(1024)S(1)}, f32[8192]{0:T(1024)S(1)}, u32[]{:S(2)}, u32[]{:S(2)}) collective-permute-start(f32[8192]{0:T(1024)S(1)} %add.213), channel_id=1, source_target_pairs={{0,16},{4,20},{8,24},{12,28},{16,0},{20,4},{24,8},{28,12},{32,48},... | collective-permute-start | bytes 98312 | tf_op jit(solution)/shard_map/ppermute | solution.py:17
  109.0 10.0 %collective-permute-start.10 = (f32[8192]{0:T(1024)S(1)}, f32[8192]{0:T(1024)S(1)}, u32[]{:S(2)}, u32[]{:S(2)}) collective-permute-start(f32[8192]{0:T(1024)S(1)} %add.214), channel_id=1, source_target_pairs={{0,32},{4,36},{8,40},{12,44},{16,48},{20,52},{24,56},{28,60},{32,0... | collective-permute-start | bytes 98312 | tf_op jit(solution)/shard_map/ppermute | solution.py:17
  119.0 5.9 %collective-permute-start.11 = (f32[8192]{0:T(1024)S(1)}, f32[8192]{0:T(1024)S(1)}, u32[]{:S(2)}, u32[]{:S(2)}) collective-permute-start(f32[8192]{0:T(1024)S(1)} %add.215), channel_id=1, source_target_pairs={{0,64},{4,68},{8,72},{12,76},{16,80},{20,84},{24,88},{28,92},{32,9... | collective-permute-start | bytes 98312 | tf_op jit(solution)/shard_map/ppermute | solution.py:17
  124.9 6.9 %collective-permute-start.12 = (f32[8192]{0:T(1024)S(1)}, f32[8192]{0:T(1024)S(1)}, u32[]{:S(2)}, u32[]{:S(2)}) collective-permute-start(f32[8192]{0:T(1024)S(1)} %add.216), channel_id=1, source_target_pairs={{0,128},{4,132},{8,136},{12,140},{16,144},{20,148},{24,152},{28,15... | collective-permute-start | bytes 98312 | tf_op jit(solution)/shard_map/ppermute | solution.py:17
  131.8 10.0 %collective-permute-start.13 = (f32[8192]{0:T(1024)S(1)}, f32[8192]{0:T(1024)S(1)}, u32[]{:S(2)}, u32[]{:S(2)}) collective-permute-start(f32[8192]{0:T(1024)S(1)} %add.217), channel_id=1, source_target_pairs={{0,256},{4,260},{8,264},{12,268},{16,272},{20,276},{24,280},{28,28... | collective-permute-start | bytes 98312 | tf_op jit(solution)/shard_map/ppermute | solution.py:17
  161.2 5.8 %collective-permute-start.15 = (f32[8192]{0:T(1024)S(1)}, f32[8192]{0:T(1024)S(1)}, u32[]{:S(2)}, u32[]{:S(2)}) collective-permute-start(f32[8192]{0:T(1024)S(1)} %add.219), channel_id=1, source_target_pairs={{0,8},{4,12},{8,0},{12,4},{16,24},{20,28},{24,16},{28,20},{32,40},... | collective-permute-start | bytes 98312 | tf_op jit(solution)/shard_map/ppermute | solution.py:17
  167.0 6.9 %collective-permute-start.16 = (f32[8192]{0:T(1024)S(1)}, f32[8192]{0:T(1024)S(1)}, u32[]{:S(2)}, u32[]{:S(2)}) collective-permute-start(f32[8192]{0:T(1024)S(1)} %add.220), channel_id=1, source_target_pairs={{0,16},{4,20},{8,24},{12,28},{16,0},{20,4},{24,8},{28,12},{32,48},... | collective-permute-start | bytes 98312 | tf_op jit(solution)/shard_map/ppermute | solution.py:17
  174.0 9.7 %collective-permute-start.17 = (f32[8192]{0:T(1024)S(1)}, f32[8192]{0:T(1024)S(1)}, u32[]{:S(2)}, u32[]{:S(2)}) collective-permute-start(f32[8192]{0:T(1024)S(1)} %add.221), channel_id=1, source_target_pairs={{0,32},{4,36},{8,40},{12,44},{16,48},{20,52},{24,56},{28,60},{32,0... | collective-permute-start | bytes 98312 | tf_op jit(solution)/shard_map/ppermute | solution.py:17
  183.7 5.8 %collective-permute-start.18 = (f32[8192]{0:T(1024)S(1)}, f32[8192]{0:T(1024)S(1)}, u32[]{:S(2)}, u32[]{:S(2)}) collective-permute-start(f32[8192]{0:T(1024)S(1)} %add.222), channel_id=1, source_target_pairs={{0,64},{4,68},{8,72},{12,76},{16,80},{20,84},{24,88},{28,92},{32,9... | collective-permute-start | bytes 98312 | tf_op jit(solution)/shard_map/ppermute | solution.py:17
  189.5 6.7 %collective-permute-start.19 = (f32[8192]{0:T(1024)S(1)}, f32[8192]{0:T(1024)S(1)}, u32[]{:S(2)}, u32[]{:S(2)}) collective-permute-start(f32[8192]{0:T(1024)S(1)} %add.223), channel_id=1, source_target_pairs={{0,128},{4,132},{8,136},{12,140},{16,144},{20,148},{24,152},{28,15... | collective-permute-start | bytes 98312 | tf_op jit(solution)/shard_map/ppermute | solution.py:17
  196.2 9.9 %collective-permute-start.20 = (f32[8192]{0:T(1024)S(1)}, f32[8192]{0:T(1024)S(1)}, u32[]{:S(2)}, u32[]{:S(2)}) collective-permute-start(f32[8192]{0:T(1024)S(1)} %add.224), channel_id=1, source_target_pairs={{0,256},{4,260},{8,264},{12,268},{16,272},{20,276},{24,280},{28,28... | collective-permute-start | bytes 98312 | tf_op jit(solution)/shard_map/ppermute | solution.py:17
  228.0 5.8 %collective-permute-start.22 = (f32[8192]{0:T(1024)S(1)}, f32[8192]{0:T(1024)S(1)}, u32[]{:S(2)}, u32[]{:S(2)}) collective-permute-start(f32[8192]{0:T(1024)S(1)} %add.226), channel_id=1, source_target_pairs={{0,8},{4,12},{8,0},{12,4},{16,24},{20,28},{24,16},{28,20},{32,40},... | collective-permute-start | bytes 98312 | tf_op jit(solution)/shard_map/ppermute | solution.py:17
  233.8 6.7 %collective-permute-start.23 = (f32[8192]{0:T(1024)S(1)}, f32[8192]{0:T(1024)S(1)}, u32[]{:S(2)}, u32[]{:S(2)}) collective-permute-start(f32[8192]{0:T(1024)S(1)} %add.227), channel_id=1, source_target_pairs={{0,16},{4,20},{8,24},{12,28},{16,0},{20,4},{24,8},{28,12},{32,48},... | collective-permute-start | bytes 98312 | tf_op jit(solution)/shard_map/ppermute | solution.py:17
  240.5 9.7 %collective-permute-start.24 = (f32[8192]{0:T(1024)S(1)}, f32[8192]{0:T(1024)S(1)}, u32[]{:S(2)}, u32[]{:S(2)}) collective-permute-start(f32[8192]{0:T(1024)S(1)} %add.228), channel_id=1, source_target_pairs={{0,32},{4,36},{8,40},{12,44},{16,48},{20,52},{24,56},{28,60},{32,0... | collective-permute-start | bytes 98312 | tf_op jit(solution)/shard_map/ppermute | solution.py:17
  256.0 6.7 %collective-permute-start.26 = (f32[8192]{0:T(1024)S(1)}, f32[8192]{0:T(1024)S(1)}, u32[]{:S(2)}, u32[]{:S(2)}) collective-permute-start(f32[8192]{0:T(1024)S(1)} %add.230), channel_id=1, source_target_pairs={{0,128},{4,132},{8,136},{12,140},{16,144},{20,148},{24,152},{28,15... | collective-permute-start | bytes 98312 | tf_op jit(solution)/shard_map/ppermute | solution.py:17
  262.7 9.9 %collective-permute-start.27 = (f32[8192]{0:T(1024)S(1)}, f32[8192]{0:T(1024)S(1)}, u32[]{:S(2)}, u32[]{:S(2)}) collective-permute-start(f32[8192]{0:T(1024)S(1)} %add.231), channel_id=1, source_target_pairs={{0,256},{4,260},{8,264},{12,268},{16,272},{20,276},{24,280},{28,28... | collective-permute-start | bytes 98312 | tf_op jit(solution)/shard_map/ppermute | solution.py:17
  299.9 6.1 %collective-permute-start.28 = (f32[4096,128]{1,0:T(8,128)S(1)}, f32[4096,128]{1,0:T(8,128)S(1)}, u32[]{:S(2)}, u32[]{:S(2)}) collective-permute-start(f32[4096,128]{1,0:T(8,128)S(1)} %get-tuple-element.169), channel_id=1, source_target_pairs={{0,4},{4,0},{8,12},{12,8},{16,20},{20,16},{24,28},{28,24},{32,36},... | collective-permute-start | bytes 6291464 | tf_op jit(solution)/shard_map/ppermute | solution.py:30
  306.5 16.7 %collective-permute-start.29 = (f32[2048,128]{1,0:T(8,128)S(1)}, f32[2048,128]{1,0:T(8,128)S(1)}, u32[]{:S(2)}, u32[]{:S(2)}) collective-permute-start(f32[2048,128]{1,0:T(8,128)S(1)} %dynamic-slice_bitcast_fusion.1), channel_id=1, source_target_pairs={{0,8},{4,68},{8,0},{12,76},{16,24},{20,84},{24,16},{28,92},{32,40}... | collective-permute-start | bytes 3145736 | tf_op jit(solution)/shard_map/ppermute | solution.py:30
  323.4 11.1 %collective-permute-start.30 = (f32[1024,128]{1,0:T(8,128)S(1)}, f32[1024,128]{1,0:T(8,128)S(1)}, u32[]{:S(2)}, u32[]{:S(2)}) collective-permute-start(f32[1024,128]{1,0:T(8,128)S(1)} %dynamic-slice_bitcast_fusion.2), channel_id=1, source_target_pairs={{0,64},{4,12},{8,72},{12,4},{16,80},{20,28},{24,88},{28,20},{32,96... | collective-permute-start | bytes 1572872 | tf_op jit(solution)/shard_map/ppermute | solution.py:30
  334.6 11.6 %collective-permute-start.31 = (f32[512,128]{1,0:T(8,128)S(1)}, f32[512,128]{1,0:T(8,128)S(1)}, u32[]{:S(2)}, u32[]{:S(2)}) collective-permute-start(f32[512,128]{1,0:T(8,128)S(1)} %dynamic-slice_bitcast_fusion.3), channel_id=1, source_target_pairs={{0,16},{4,132},{8,24},{12,140},{16,0},{20,148},{24,8},{28,156},{32... | collective-permute-start | bytes 786440 | tf_op jit(solution)/shard_map/ppermute | solution.py:30
  346.3 9.2 %collective-permute-start.32 = (f32[256,128]{1,0:T(8,128)S(1)}, f32[256,128]{1,0:T(8,128)S(1)}, u32[]{:S(2)}, u32[]{:S(2)}) collective-permute-start(f32[256,128]{1,0:T(8,128)S(1)} %dynamic-slice_bitcast_fusion.4), channel_id=1, source_target_pairs={{0,128},{4,20},{8,136},{12,28},{16,144},{20,4},{24,152},{28,12},{3... | collective-permute-start | bytes 393224 | tf_op jit(solution)/shard_map/ppermute | solution.py:30
  350.9 11.3 %collective-permute-start.35 = (f32[256,128]{1,0:T(8,128)S(1)}, f32[256,128]{1,0:T(8,128)S(1)}, u32[]{:S(2)}, u32[]{:S(2)}) collective-permute-start(f32[256,128]{1,0:T(8,128)S(1)} %bitcast.238), channel_id=1, source_target_pairs={{0,1},{1,0},{2,3},{3,2},{4,5},{5,4},{6,7},{7,6},{8,9},{9,8},{10,11... | collective-permute-start | bytes 393224 | tf_op jit(solution)/shard_map/ppermute | solution.py:17
  355.5 11.3 %collective-permute-start.33 = (f32[128,128]{1,0:T(8,128)S(1)}, f32[128,128]{1,0:T(8,128)S(1)}, u32[]{:S(2)}, u32[]{:S(2)}) collective-permute-start(f32[128,128]{1,0:T(8,128)S(1)} %dynamic-slice_bitcast_fusion.5), channel_id=1, source_target_pairs={{0,32},{4,260},{8,40},{12,268},{16,48},{20,276},{24,56},{28,284},{... | collective-permute-start | bytes 196616 | tf_op jit(solution)/shard_map/ppermute | solution.py:30
  362.2 12.6 %collective-permute-start.36 = (f32[256,128]{1,0:T(8,128)S(1)}, f32[256,128]{1,0:T(8,128)S(1)}, u32[]{:S(2)}, u32[]{:S(2)}) collective-permute-start(f32[256,128]{1,0:T(8,128)S(1)} %bitcast_add_fusion.7), channel_id=1, source_target_pairs={{0,2},{1,3},{2,0},{3,1},{4,6},{5,7},{6,4},{7,5},{8,10},{9,11},{10,... | collective-permute-start | bytes 393224 | tf_op jit(solution)/shard_map/ppermute | solution.py:17
  366.8 9.9 %collective-permute-start.34 = (f32[64,128]{1,0:T(8,128)S(1)}, f32[64,128]{1,0:T(8,128)S(1)}, u32[]{:S(2)}, u32[]{:S(2)}) collective-permute-start(f32[64,128]{1,0:T(8,128)S(1)} %dynamic-slice_bitcast_fusion.6), channel_id=1, source_target_pairs={{0,256},{4,36},{8,264},{12,44},{16,272},{20,52},{24,280},{28,60},{... | collective-permute-start | bytes 98312 | tf_op jit(solution)/shard_map/ppermute | solution.py:30
  (7 other events, 30.9 us)

commit v7 on v6

--- a/solution.py
+++ b/solution.py
@@ -105,7 +105,7 @@
     copies = gather_blocks(prototypes.astype(jnp.bfloat16), "dp")
     rows_here = teacher_emb.shape[0]
     width = teacher_emb.shape[1]
-    block = math.gcd(rows_here, 128)
+    block = rows_here
     count_blocks = rows_here // block
 
     def teacher_block(emb):

time: 380 us -> 367 us (0.966)
  matrix products: 18.2 us -> 5.64 us
    dot_general x6 -> x2, matrix products: 13.2 us -> 3.07 us  [contract_rows(): lax.dot_general(left, right, (((1,), (1,)), ((), ())), preferred_element_...]
    convert_element_type x0 -> x1, other arithmetic: none -> 7.82 us  [gradient_block(): grads = (probs - targets).astype(jnp.bfloat16)]
    dynamic_update_slice x2 -> x0, other arithmetic: 5.18 us -> none  [per_device(): lax.map(teacher_block, teacher_emb.reshape(count_blocks, block, width))]
  transfers between devices with their start and end apart: 37 -> 37, of which waited for: 34 -> 33; matrix products, arithmetic and copies ran while one was open for 0% -> 1% of each run, Pallas kernels for 0% -> 0%
where the time goes in v7:
time: 367 us; the launch traced here: 366 us
  starting transfers between devices  165 us (45%)
  waiting for transfers between devices  115 us (31%)
  blocking collectives  37.2 us (10%)
  other arithmetic  36.7 us (10%)
  matrix products  5.64 us (2%)
  local copies, waits for them, and re-layouts  3.9 us (1%)
    ppermute x23, starting transfers between devices, swap(): return lax.ppermute(x, axis, [(i, i ^ 1 << k) for i in range(n)])  101 us
    ppermute x14, starting transfers between devices, core_swap(): return lax.ppermute(x, axis, pairs)  64.7 us
    ppermute x14, waiting for transfers between devices, core_swap(): return lax.ppermute(x, axis, pairs)  63.4 us
    ppermute x23, waiting for transfers between devices, swap(): return lax.ppermute(x, axis, [(i, i ^ 1 << k) for i in range(n)])  51.9 us
    psum x3, blocking collectives, per_device(): row_scale = 1.0 / lax.psum(partial_rows, 'proto')  25.2 us
    reduce_sum x3, other arithmetic, per_device(): partial_rows = shift * jnp.sum(base_local * col_scale[None, :], axis=1)  13 us
    reduce_sum x3, other arithmetic, per_device(): partial_cols = jnp.sum((row_scale * shift)[:, None] * base_local, axis=0)  12 us
    all_gather x1, blocking collectives, per_device(): lax.all_gather(jnp.stack([teacher_local, student_local, total_local]), 'p...  11.9 us
  transfers between devices with their start and end apart: 37, of which 33 were waited for; matrix products, arithmetic and copies ran while one was open for 1% of the time, Pallas kernels for 0%

profile of v7, /device:TPU:6, one launch (start us, length us, event | category | flops | bytes accessed | tf_op | source)
XLA Modules:
  0.0 365.6 jit_solution(181701491798096131)
XLA Ops:
  1.5 10.9 %collective-permute-start = (bf16[64,128]{1,0:T(8,128)(2,1)S(1)}, bf16[64,128]{1,0:T(8,128)(2,1)S(1)}, u32[]{:S(2)}, u32[]{:S(2)}) collective-permute-start(bf16[64,128]{1,0:T(8,128)(2,1)S(1)} %get-tuple-element.43), channel_id=1, source_target_pairs={{0,256},{4,36},{8,264},{12,44},{16,272},{20,52},{24,280},{28,60},{... | collective-permute-start | bytes 49160 | tf_op jit(solution)/shard_map/ppermute | solution.py:30
  14.1 7.7 %collective-permute-start.1 = (bf16[128,128]{1,0:T(8,128)(2,1)S(1)}, bf16[128,128]{1,0:T(8,128)(2,1)S(1)}, u32[]{:S(2)}, u32[]{:S(2)}) collective-permute-start(bf16[128,128]{1,0:T(8,128)(2,1)S(1)} %bitcast.142), channel_id=1, source_target_pairs={{0,32},{4,260},{8,40},{12,268},{16,48},{20,276},{24,56},{28,284},{... | collective-permute-start | bytes 98312 | tf_op jit(solution)/shard_map/ppermute | solution.py:30
  23.9 4.4 %collective-permute-start.2 = (bf16[256,128]{1,0:T(8,128)(2,1)S(1)}, bf16[256,128]{1,0:T(8,128)(2,1)S(1)}, u32[]{:S(2)}, u32[]{:S(2)}) collective-permute-start(bf16[256,128]{1,0:T(8,128)(2,1)S(1)} %bitcast.140), channel_id=1, source_target_pairs={{0,128},{4,20},{8,136},{12,28},{16,144},{20,4},{24,152},{28,12},{3... | collective-permute-start | bytes 196616 | tf_op jit(solution)/shard_map/ppermute | solution.py:30
  30.9 4.6 %collective-permute-start.3 = (bf16[512,128]{1,0:T(8,128)(2,1)S(1)}, bf16[512,128]{1,0:T(8,128)(2,1)S(1)}, u32[]{:S(2)}, u32[]{:S(2)}) collective-permute-start(bf16[512,128]{1,0:T(8,128)(2,1)S(1)} %bitcast.133), channel_id=1, source_target_pairs={{0,16},{4,132},{8,24},{12,140},{16,0},{20,148},{24,8},{28,156},{32... | collective-permute-start | bytes 393224 | tf_op jit(solution)/shard_map/ppermute | solution.py:30
  35.6 4.4 %collective-permute-done.3 = bf16[512,128]{1,0:T(8,128)(2,1)S(1)} collective-permute-done((bf16[512,128]{1,0:T(8,128)(2,1)S(1)}, bf16[512,128]{1,0:T(8,128)(2,1)S(1)}, u32[]{:S(2)}, u32[]{:S(2)}) %collective-permute-start.3) | collective-permute-done | bytes 131104 | tf_op jit(solution)/shard_map/ppermute | solution.py:30
  43.7 5.3 %collective-permute-done.4 = bf16[1024,128]{1,0:T(8,128)(2,1)S(1)} collective-permute-done((bf16[1024,128]{1,0:T(8,128)(2,1)S(1)}, bf16[1024,128]{1,0:T(8,128)(2,1)S(1)}, u32[]{:S(2)}, u32[]{:S(2)}) %collective-permute-start.4) | collective-permute-done | bytes 262176 | tf_op jit(solution)/shard_map/ppermute | solution.py:30
  51.3 8.8 %collective-permute-done.5 = bf16[2048,128]{1,0:T(8,128)(2,1)S(1)} collective-permute-done((bf16[2048,128]{1,0:T(8,128)(2,1)S(1)}, bf16[2048,128]{1,0:T(8,128)(2,1)S(1)}, u32[]{:S(2)}, u32[]{:S(2)}) %collective-permute-start.5) | collective-permute-done | bytes 524320 | tf_op jit(solution)/shard_map/ppermute | solution.py:30
  70.7 11.9 %all-gather.1 = f32[4,3,256]{2,1,0:T(4,128)S(1)} all-gather(f32[1,3,256]{2,1,0:T(4,128)S(1)} %maximum_bitcast_fusion), channel_id=2, replica_groups=mesh['dp'=128,'proto'=4] {'proto'}, dimensions={0}, use_global_device_ids=true | all-gather | bytes 15360 | tf_op jit(solution)/shard_map/all_gather | solution.py:132
  100.6 7.3 %collective-permute-start.10 = (f32[8192]{0:T(1024)S(1)}, f32[8192]{0:T(1024)S(1)}, u32[]{:S(2)}, u32[]{:S(2)}) collective-permute-start(f32[8192]{0:T(1024)S(1)} %add.208), channel_id=1, source_target_pairs={{0,32},{4,36},{8,40},{12,44},{16,48},{20,52},{24,56},{28,60},{32,0... | collective-permute-start | bytes 98312 | tf_op jit(solution)/shard_map/ppermute | solution.py:17
  116.5 5.0 %collective-permute-start.12 = (f32[8192]{0:T(1024)S(1)}, f32[8192]{0:T(1024)S(1)}, u32[]{:S(2)}, u32[]{:S(2)}) collective-permute-start(f32[8192]{0:T(1024)S(1)} %add.210), channel_id=1, source_target_pairs={{0,128},{4,132},{8,136},{12,140},{16,144},{20,148},{24,152},{28,15... | collective-permute-start | bytes 98312 | tf_op jit(solution)/shard_map/ppermute | solution.py:17
  123.4 8.1 %collective-permute-start.13 = (f32[8192]{0:T(1024)S(1)}, f32[8192]{0:T(1024)S(1)}, u32[]{:S(2)}, u32[]{:S(2)}) collective-permute-start(f32[8192]{0:T(1024)S(1)} %add.211), channel_id=1, source_target_pairs={{0,256},{4,260},{8,264},{12,268},{16,272},{20,276},{24,280},{28,28... | collective-permute-start | bytes 98312 | tf_op jit(solution)/shard_map/ppermute | solution.py:17
  133.4 4.3 %multiply_reduce_fusion.4 = f32[256]{0:T(256)S(1)} fusion(f32[8192]{0:T(1024)S(1)} %add_divide_fusion.2, f32[8192,256]{1,0:T(8,128)} %copy-done.1, f32[256]{0:T(256)S(1)} %get-tuple-element.65), kind=kLoop, calls=%fused_computation.7 | loop fusion | flops 8388352 | bytes 8423424 | tf_op jit(solution)/shard_map/reduce_sum | solution.py:145
  137.8 7.5 %psum.21 = f32[256]{0:T(256)S(1)} all-reduce(f32[256]{0:T(256)S(1)} %mul.145), channel_id=1, replica_groups=mesh['dp'=128,'proto'=4] {'proto'}, use_global_device_ids=true, to_apply=%region_5.6 | all-reduce | flops 256 | bytes 2048 | tf_op jit(solution)/shard_map/psum | solution.py:146
  145.3 5.1 %multiply_reduce_fusion.3 = f32[8192]{0:T(1024)S(1)} fusion(f32[256]{0:T(256)S(1)} %divide_multiply_fusion.2, f32[8192,256]{1,0:T(8,128)} %copy-done.1, f32[256]{0:T(256)S(1)} %get-tuple-element.65), kind=kLoop, calls=%fused_computation.6 | loop fusion | flops 8380416 | bytes 8423424 | tf_op jit(solution)/shard_map/reduce_sum | solution.py:143
  166.5 6.7 %collective-permute-start.17 = (f32[8192]{0:T(1024)S(1)}, f32[8192]{0:T(1024)S(1)}, u32[]{:S(2)}, u32[]{:S(2)}) collective-permute-start(f32[8192]{0:T(1024)S(1)} %add.215), channel_id=1, source_target_pairs={{0,32},{4,36},{8,40},{12,44},{16,48},{20,52},{24,56},{28,60},{32,0... | collective-permute-start | bytes 98312 | tf_op jit(solution)/shard_map/ppermute | solution.py:17
  182.0 4.7 %collective-permute-start.19 = (f32[8192]{0:T(1024)S(1)}, f32[8192]{0:T(1024)S(1)}, u32[]{:S(2)}, u32[]{:S(2)}) collective-permute-start(f32[8192]{0:T(1024)S(1)} %add.217), channel_id=1, source_target_pairs={{0,128},{4,132},{8,136},{12,140},{16,144},{20,148},{24,152},{28,15... | collective-permute-start | bytes 98312 | tf_op jit(solution)/shard_map/ppermute | solution.py:17
  188.7 8.0 %collective-permute-start.20 = (f32[8192]{0:T(1024)S(1)}, f32[8192]{0:T(1024)S(1)}, u32[]{:S(2)}, u32[]{:S(2)}) collective-permute-start(f32[8192]{0:T(1024)S(1)} %add.218), channel_id=1, source_target_pairs={{0,256},{4,260},{8,264},{12,268},{16,272},{20,276},{24,280},{28,28... | collective-permute-start | bytes 98312 | tf_op jit(solution)/shard_map/ppermute | solution.py:17
  198.6 4.3 %multiply_reduce_fusion.2 = f32[256]{0:T(256)S(1)} fusion(f32[8192]{0:T(1024)S(1)} %add_divide_fusion.1, f32[8192,256]{1,0:T(8,128)} %copy-done.1, f32[256]{0:T(256)S(1)} %get-tuple-element.65), kind=kLoop, calls=%fused_computation.5 | loop fusion | flops 8388352 | bytes 8423424 | tf_op jit(solution)/shard_map/reduce_sum | solution.py:145
  202.9 10.0 %psum.22 = f32[256]{0:T(256)S(1)} all-reduce(f32[256]{0:T(256)S(1)} %mul.151), channel_id=1, replica_groups=mesh['dp'=128,'proto'=4] {'proto'}, use_global_device_ids=true, to_apply=%region_8.9 | all-reduce | flops 256 | bytes 2048 | tf_op jit(solution)/shard_map/psum | solution.py:146
  212.9 5.1 %multiply_reduce_fusion.1 = f32[8192]{0:T(1024)S(1)} fusion(f32[256]{0:T(256)S(1)} %divide_multiply_fusion.1, f32[8192,256]{1,0:T(8,128)} %copy-done.1, f32[256]{0:T(256)S(1)} %get-tuple-element.65), kind=kLoop, calls=%fused_computation.4 | loop fusion | flops 8380416 | bytes 8423424 | tf_op jit(solution)/shard_map/reduce_sum | solution.py:143
  233.9 6.8 %collective-permute-start.24 = (f32[8192]{0:T(1024)S(1)}, f32[8192]{0:T(1024)S(1)}, u32[]{:S(2)}, u32[]{:S(2)}) collective-permute-start(f32[8192]{0:T(1024)S(1)} %add.222), channel_id=1, source_target_pairs={{0,32},{4,36},{8,40},{12,44},{16,48},{20,52},{24,56},{28,60},{32,0... | collective-permute-start | bytes 98312 | tf_op jit(solution)/shard_map/ppermute | solution.py:17
  249.4 4.6 %collective-permute-start.26 = (f32[8192]{0:T(1024)S(1)}, f32[8192]{0:T(1024)S(1)}, u32[]{:S(2)}, u32[]{:S(2)}) collective-permute-start(f32[8192]{0:T(1024)S(1)} %add.224), channel_id=1, source_target_pairs={{0,128},{4,132},{8,136},{12,140},{16,144},{20,148},{24,152},{28,15... | collective-permute-start | bytes 98312 | tf_op jit(solution)/shard_map/ppermute | solution.py:17
  256.1 8.0 %collective-permute-start.27 = (f32[8192]{0:T(1024)S(1)}, f32[8192]{0:T(1024)S(1)}, u32[]{:S(2)}, u32[]{:S(2)}) collective-permute-start(f32[8192]{0:T(1024)S(1)} %add.225), channel_id=1, source_target_pairs={{0,256},{4,260},{8,264},{12,268},{16,272},{20,276},{24,280},{28,28... | collective-permute-start | bytes 98312 | tf_op jit(solution)/shard_map/ppermute | solution.py:17
  270.4 7.7 %psum.23 = f32[256]{0:T(256)S(1)} all-reduce(f32[256]{0:T(256)S(1)} %mul.157), channel_id=1, replica_groups=mesh['dp'=128,'proto'=4] {'proto'}, use_global_device_ids=true, to_apply=%region_11.12 | all-reduce | flops 256 | bytes 2048 | tf_op jit(solution)/shard_map/psum | solution.py:146
  278.1 7.8 %subtract_convert_fusion = bf16[8192,256]{1,0:T(8,128)(2,1)S(1)} fusion(f32[8192,256]{1,0:T(8,128)} %copy-done.2, f32[256]{0:T(256)S(1)} %divide_multiply_fusion, f32[8192]{0:T(1024)S(1)} %add_divide_fusion, f32[256]{0:T(256)S(1)} %add_divide_fusion.3, f32[256]{0:T(256)S(1)} %get-tuple-element.67, f32[8192,256]{1,0:T(8,128)} %copy-done.1, ...), kind=kLoop, calls=%fused_computation.2 | loop fusion | flops 16777216 | bytes 21008384 | tf_op jit(solution)/shard_map/while/body/eval_jaxpr/convert_element_type | solution.py:155
  296.2 14.6 %collective-permute-done.29 = f32[2048,128]{1,0:T(8,128)S(1)} collective-permute-done((f32[2048,128]{1,0:T(8,128)S(1)}, f32[2048,128]{1,0:T(8,128)S(1)}, u32[]{:S(2)}, u32[]{:S(2)}) %collective-permute-start.29) | collective-permute-done | bytes 1048608 | tf_op jit(solution)/shard_map/ppermute | solution.py:30
  314.3 7.7 %collective-permute-done.30 = f32[1024,128]{1,0:T(8,128)S(1)} collective-permute-done((f32[1024,128]{1,0:T(8,128)S(1)}, f32[1024,128]{1,0:T(8,128)S(1)}, u32[]{:S(2)}, u32[]{:S(2)}) %collective-permute-start.30) | collective-permute-done | bytes 524320 | tf_op jit(solution)/shard_map/ppermute | solution.py:30
  325.1 8.7 %collective-permute-done.31 = f32[512,128]{1,0:T(8,128)S(1)} collective-permute-done((f32[512,128]{1,0:T(8,128)S(1)}, f32[512,128]{1,0:T(8,128)S(1)}, u32[]{:S(2)}, u32[]{:S(2)}) %collective-permute-start.31) | collective-permute-done | bytes 262176 | tf_op jit(solution)/shard_map/ppermute | solution.py:30
  333.8 4.6 %collective-permute-start.32 = (f32[256,128]{1,0:T(8,128)S(1)}, f32[256,128]{1,0:T(8,128)S(1)}, u32[]{:S(2)}, u32[]{:S(2)}) collective-permute-start(f32[256,128]{1,0:T(8,128)S(1)} %dynamic-slice_bitcast_fusion.4), channel_id=1, source_target_pairs={{0,128},{4,20},{8,136},{12,28},{16,144},{20,4},{24,152},{28,12},{3... | collective-permute-start | bytes 393224 | tf_op jit(solution)/shard_map/ppermute | solution.py:30
  343.1 6.7 %collective-permute-start.33 = (f32[128,128]{1,0:T(8,128)S(1)}, f32[128,128]{1,0:T(8,128)S(1)}, u32[]{:S(2)}, u32[]{:S(2)}) collective-permute-start(f32[128,128]{1,0:T(8,128)S(1)} %dynamic-slice_bitcast_fusion.5), channel_id=1, source_target_pairs={{0,32},{4,260},{8,40},{12,268},{16,48},{20,276},{24,56},{28,284},{... | collective-permute-start | bytes 196616 | tf_op jit(solution)/shard_map/ppermute | solution.py:30
  349.9 5.2 %collective-permute-start.36 = (f32[256,128]{1,0:T(8,128)S(1)}, f32[256,128]{1,0:T(8,128)S(1)}, u32[]{:S(2)}, u32[]{:S(2)}) collective-permute-start(f32[256,128]{1,0:T(8,128)S(1)} %add.234), channel_id=1, source_target_pairs={{0,2},{1,3},{2,0},{3,1},{4,6},{5,7},{6,4},{7,5},{8,10},{9,11},{10,... | collective-permute-start | bytes 393224 | tf_op jit(solution)/shard_map/ppermute | solution.py:17
  355.1 8.0 %collective-permute-start.34 = (f32[64,128]{1,0:T(8,128)S(1)}, f32[64,128]{1,0:T(8,128)S(1)}, u32[]{:S(2)}, u32[]{:S(2)}) collective-permute-start(f32[64,128]{1,0:T(8,128)S(1)} %dynamic-slice_bitcast_fusion.6), channel_id=1, source_target_pairs={{0,256},{4,36},{8,264},{12,44},{16,272},{20,52},{24,280},{28,60},{... | collective-permute-start | bytes 98312 | tf_op jit(solution)/shard_map/ppermute | solution.py:30
  (145 shorter events, 139.3 us)
Async XLA Ops:
  1.5 12.6 %collective-permute-start = (bf16[64,128]{1,0:T(8,128)(2,1)S(1)}, bf16[64,128]{1,0:T(8,128)(2,1)S(1)}, u32[]{:S(2)}, u32[]{:S(2)}) collective-permute-start(bf16[64,128]{1,0:T(8,128)(2,1)S(1)} %get-tuple-element.43), channel_id=1, source_target_pairs={{0,256},{4,36},{8,264},{12,44},{16,272},{20,52},{24,280},{28,60},{... | collective-permute-start | bytes 49160 | tf_op jit(solution)/shard_map/ppermute | solution.py:30
  14.1 9.7 %collective-permute-start.1 = (bf16[128,128]{1,0:T(8,128)(2,1)S(1)}, bf16[128,128]{1,0:T(8,128)(2,1)S(1)}, u32[]{:S(2)}, u32[]{:S(2)}) collective-permute-start(bf16[128,128]{1,0:T(8,128)(2,1)S(1)} %bitcast.142), channel_id=1, source_target_pairs={{0,32},{4,260},{8,40},{12,268},{16,48},{20,276},{24,56},{28,284},{... | collective-permute-start | bytes 98312 | tf_op jit(solution)/shard_map/ppermute | solution.py:30
  23.9 7.0 %collective-permute-start.2 = (bf16[256,128]{1,0:T(8,128)(2,1)S(1)}, bf16[256,128]{1,0:T(8,128)(2,1)S(1)}, u32[]{:S(2)}, u32[]{:S(2)}) collective-permute-start(bf16[256,128]{1,0:T(8,128)(2,1)S(1)} %bitcast.140), channel_id=1, source_target_pairs={{0,128},{4,20},{8,136},{12,28},{16,144},{20,4},{24,152},{28,12},{3... | collective-permute-start | bytes 196616 | tf_op jit(solution)/shard_map/ppermute | solution.py:30
  30.9 9.2 %collective-permute-start.3 = (bf16[512,128]{1,0:T(8,128)(2,1)S(1)}, bf16[512,128]{1,0:T(8,128)(2,1)S(1)}, u32[]{:S(2)}, u32[]{:S(2)}) collective-permute-start(bf16[512,128]{1,0:T(8,128)(2,1)S(1)} %bitcast.133), channel_id=1, source_target_pairs={{0,16},{4,132},{8,24},{12,140},{16,0},{20,148},{24,8},{28,156},{32... | collective-permute-start | bytes 393224 | tf_op jit(solution)/shard_map/ppermute | solution.py:30
  40.1 9.0 %collective-permute-start.4 = (bf16[1024,128]{1,0:T(8,128)(2,1)S(1)}, bf16[1024,128]{1,0:T(8,128)(2,1)S(1)}, u32[]{:S(2)}, u32[]{:S(2)}) collective-permute-start(bf16[1024,128]{1,0:T(8,128)(2,1)S(1)} %bitcast.127), channel_id=1, source_target_pairs={{0,64},{4,12},{8,72},{12,4},{16,80},{20,28},{24,88},{28,20},{32,96... | collective-permute-start | bytes 786440 | tf_op jit(solution)/shard_map/ppermute | solution.py:30
  49.1 11.1 %collective-permute-start.5 = (bf16[2048,128]{1,0:T(8,128)(2,1)S(1)}, bf16[2048,128]{1,0:T(8,128)(2,1)S(1)}, u32[]{:S(2)}, u32[]{:S(2)}) collective-permute-start(bf16[2048,128]{1,0:T(8,128)(2,1)S(1)} %bitcast.125), channel_id=1, source_target_pairs={{0,8},{4,68},{8,0},{12,76},{16,24},{20,84},{24,16},{28,92},{32,40}... | collective-permute-start | bytes 1572872 | tf_op jit(solution)/shard_map/ppermute | solution.py:30
  87.8 5.8 %collective-permute-start.8 = (f32[8192]{0:T(1024)S(1)}, f32[8192]{0:T(1024)S(1)}, u32[]{:S(2)}, u32[]{:S(2)}) collective-permute-start(f32[8192]{0:T(1024)S(1)} %add.206), channel_id=1, source_target_pairs={{0,8},{4,12},{8,0},{12,4},{16,24},{20,28},{24,16},{28,20},{32,40},... | collective-permute-start | bytes 98312 | tf_op jit(solution)/shard_map/ppermute | solution.py:17
  93.6 7.0 %collective-permute-start.9 = (f32[8192]{0:T(1024)S(1)}, f32[8192]{0:T(1024)S(1)}, u32[]{:S(2)}, u32[]{:S(2)}) collective-permute-start(f32[8192]{0:T(1024)S(1)} %add.207), channel_id=1, source_target_pairs={{0,16},{4,20},{8,24},{12,28},{16,0},{20,4},{24,8},{28,12},{32,48},... | collective-permute-start | bytes 98312 | tf_op jit(solution)/shard_map/ppermute | solution.py:17
  100.6 10.0 %collective-permute-start.10 = (f32[8192]{0:T(1024)S(1)}, f32[8192]{0:T(1024)S(1)}, u32[]{:S(2)}, u32[]{:S(2)}) collective-permute-start(f32[8192]{0:T(1024)S(1)} %add.208), channel_id=1, source_target_pairs={{0,32},{4,36},{8,40},{12,44},{16,48},{20,52},{24,56},{28,60},{32,0... | collective-permute-start | bytes 98312 | tf_op jit(solution)/shard_map/ppermute | solution.py:17
  110.6 5.9 %collective-permute-start.11 = (f32[8192]{0:T(1024)S(1)}, f32[8192]{0:T(1024)S(1)}, u32[]{:S(2)}, u32[]{:S(2)}) collective-permute-start(f32[8192]{0:T(1024)S(1)} %add.209), channel_id=1, source_target_pairs={{0,64},{4,68},{8,72},{12,76},{16,80},{20,84},{24,88},{28,92},{32,9... | collective-permute-start | bytes 98312 | tf_op jit(solution)/shard_map/ppermute | solution.py:17
  116.5 6.9 %collective-permute-start.12 = (f32[8192]{0:T(1024)S(1)}, f32[8192]{0:T(1024)S(1)}, u32[]{:S(2)}, u32[]{:S(2)}) collective-permute-start(f32[8192]{0:T(1024)S(1)} %add.210), channel_id=1, source_target_pairs={{0,128},{4,132},{8,136},{12,140},{16,144},{20,148},{24,152},{28,15... | collective-permute-start | bytes 98312 | tf_op jit(solution)/shard_map/ppermute | solution.py:17
  123.4 10.0 %collective-permute-start.13 = (f32[8192]{0:T(1024)S(1)}, f32[8192]{0:T(1024)S(1)}, u32[]{:S(2)}, u32[]{:S(2)}) collective-permute-start(f32[8192]{0:T(1024)S(1)} %add.211), channel_id=1, source_target_pairs={{0,256},{4,260},{8,264},{12,268},{16,272},{20,276},{24,280},{28,28... | collective-permute-start | bytes 98312 | tf_op jit(solution)/shard_map/ppermute | solution.py:17
  153.7 5.8 %collective-permute-start.15 = (f32[8192]{0:T(1024)S(1)}, f32[8192]{0:T(1024)S(1)}, u32[]{:S(2)}, u32[]{:S(2)}) collective-permute-start(f32[8192]{0:T(1024)S(1)} %add.213), channel_id=1, source_target_pairs={{0,8},{4,12},{8,0},{12,4},{16,24},{20,28},{24,16},{28,20},{32,40},... | collective-permute-start | bytes 98312 | tf_op jit(solution)/shard_map/ppermute | solution.py:17
  159.6 6.9 %collective-permute-start.16 = (f32[8192]{0:T(1024)S(1)}, f32[8192]{0:T(1024)S(1)}, u32[]{:S(2)}, u32[]{:S(2)}) collective-permute-start(f32[8192]{0:T(1024)S(1)} %add.214), channel_id=1, source_target_pairs={{0,16},{4,20},{8,24},{12,28},{16,0},{20,4},{24,8},{28,12},{32,48},... | collective-permute-start | bytes 98312 | tf_op jit(solution)/shard_map/ppermute | solution.py:17
  166.5 9.7 %collective-permute-start.17 = (f32[8192]{0:T(1024)S(1)}, f32[8192]{0:T(1024)S(1)}, u32[]{:S(2)}, u32[]{:S(2)}) collective-permute-start(f32[8192]{0:T(1024)S(1)} %add.215), channel_id=1, source_target_pairs={{0,32},{4,36},{8,40},{12,44},{16,48},{20,52},{24,56},{28,60},{32,0... | collective-permute-start | bytes 98312 | tf_op jit(solution)/shard_map/ppermute | solution.py:17
  176.2 5.8 %collective-permute-start.18 = (f32[8192]{0:T(1024)S(1)}, f32[8192]{0:T(1024)S(1)}, u32[]{:S(2)}, u32[]{:S(2)}) collective-permute-start(f32[8192]{0:T(1024)S(1)} %add.216), channel_id=1, source_target_pairs={{0,64},{4,68},{8,72},{12,76},{16,80},{20,84},{24,88},{28,92},{32,9... | collective-permute-start | bytes 98312 | tf_op jit(solution)/shard_map/ppermute | solution.py:17
  182.0 6.7 %collective-permute-start.19 = (f32[8192]{0:T(1024)S(1)}, f32[8192]{0:T(1024)S(1)}, u32[]{:S(2)}, u32[]{:S(2)}) collective-permute-start(f32[8192]{0:T(1024)S(1)} %add.217), channel_id=1, source_target_pairs={{0,128},{4,132},{8,136},{12,140},{16,144},{20,148},{24,152},{28,15... | collective-permute-start | bytes 98312 | tf_op jit(solution)/shard_map/ppermute | solution.py:17
  188.7 9.8 %collective-permute-start.20 = (f32[8192]{0:T(1024)S(1)}, f32[8192]{0:T(1024)S(1)}, u32[]{:S(2)}, u32[]{:S(2)}) collective-permute-start(f32[8192]{0:T(1024)S(1)} %add.218), channel_id=1, source_target_pairs={{0,256},{4,260},{8,264},{12,268},{16,272},{20,276},{24,280},{28,28... | collective-permute-start | bytes 98312 | tf_op jit(solution)/shard_map/ppermute | solution.py:17
  221.4 5.8 %collective-permute-start.22 = (f32[8192]{0:T(1024)S(1)}, f32[8192]{0:T(1024)S(1)}, u32[]{:S(2)}, u32[]{:S(2)}) collective-permute-start(f32[8192]{0:T(1024)S(1)} %add.220), channel_id=1, source_target_pairs={{0,8},{4,12},{8,0},{12,4},{16,24},{20,28},{24,16},{28,20},{32,40},... | collective-permute-start | bytes 98312 | tf_op jit(solution)/shard_map/ppermute | solution.py:17
  227.2 6.7 %collective-permute-start.23 = (f32[8192]{0:T(1024)S(1)}, f32[8192]{0:T(1024)S(1)}, u32[]{:S(2)}, u32[]{:S(2)}) collective-permute-start(f32[8192]{0:T(1024)S(1)} %add.221), channel_id=1, source_target_pairs={{0,16},{4,20},{8,24},{12,28},{16,0},{20,4},{24,8},{28,12},{32,48},... | collective-permute-start | bytes 98312 | tf_op jit(solution)/shard_map/ppermute | solution.py:17
  233.9 9.7 %collective-permute-start.24 = (f32[8192]{0:T(1024)S(1)}, f32[8192]{0:T(1024)S(1)}, u32[]{:S(2)}, u32[]{:S(2)}) collective-permute-start(f32[8192]{0:T(1024)S(1)} %add.222), channel_id=1, source_target_pairs={{0,32},{4,36},{8,40},{12,44},{16,48},{20,52},{24,56},{28,60},{32,0... | collective-permute-start | bytes 98312 | tf_op jit(solution)/shard_map/ppermute | solution.py:17
  249.4 6.7 %collective-permute-start.26 = (f32[8192]{0:T(1024)S(1)}, f32[8192]{0:T(1024)S(1)}, u32[]{:S(2)}, u32[]{:S(2)}) collective-permute-start(f32[8192]{0:T(1024)S(1)} %add.224), channel_id=1, source_target_pairs={{0,128},{4,132},{8,136},{12,140},{16,144},{20,148},{24,152},{28,15... | collective-permute-start | bytes 98312 | tf_op jit(solution)/shard_map/ppermute | solution.py:17
  256.1 9.9 %collective-permute-start.27 = (f32[8192]{0:T(1024)S(1)}, f32[8192]{0:T(1024)S(1)}, u32[]{:S(2)}, u32[]{:S(2)}) collective-permute-start(f32[8192]{0:T(1024)S(1)} %add.225), channel_id=1, source_target_pairs={{0,256},{4,260},{8,264},{12,268},{16,272},{20,276},{24,280},{28,28... | collective-permute-start | bytes 98312 | tf_op jit(solution)/shard_map/ppermute | solution.py:17
  287.5 6.1 %collective-permute-start.28 = (f32[4096,128]{1,0:T(8,128)S(1)}, f32[4096,128]{1,0:T(8,128)S(1)}, u32[]{:S(2)}, u32[]{:S(2)}) collective-permute-start(f32[4096,128]{1,0:T(8,128)S(1)} %get-tuple-element.44), channel_id=1, source_target_pairs={{0,4},{4,0},{8,12},{12,8},{16,20},{20,16},{24,28},{28,24},{32,36},... | collective-permute-start | bytes 6291464 | tf_op jit(solution)/shard_map/ppermute | solution.py:30
  294.1 16.7 %collective-permute-start.29 = (f32[2048,128]{1,0:T(8,128)S(1)}, f32[2048,128]{1,0:T(8,128)S(1)}, u32[]{:S(2)}, u32[]{:S(2)}) collective-permute-start(f32[2048,128]{1,0:T(8,128)S(1)} %dynamic-slice_bitcast_fusion.1), channel_id=1, source_target_pairs={{0,8},{4,68},{8,0},{12,76},{16,24},{20,84},{24,16},{28,92},{32,40}... | collective-permute-start | bytes 3145736 | tf_op jit(solution)/shard_map/ppermute | solution.py:30
  310.9 11.1 %collective-permute-start.30 = (f32[1024,128]{1,0:T(8,128)S(1)}, f32[1024,128]{1,0:T(8,128)S(1)}, u32[]{:S(2)}, u32[]{:S(2)}) collective-permute-start(f32[1024,128]{1,0:T(8,128)S(1)} %dynamic-slice_bitcast_fusion.2), channel_id=1, source_target_pairs={{0,64},{4,12},{8,72},{12,4},{16,80},{20,28},{24,88},{28,20},{32,96... | collective-permute-start | bytes 1572872 | tf_op jit(solution)/shard_map/ppermute | solution.py:30
  322.1 11.6 %collective-permute-start.31 = (f32[512,128]{1,0:T(8,128)S(1)}, f32[512,128]{1,0:T(8,128)S(1)}, u32[]{:S(2)}, u32[]{:S(2)}) collective-permute-start(f32[512,128]{1,0:T(8,128)S(1)} %dynamic-slice_bitcast_fusion.3), channel_id=1, source_target_pairs={{0,16},{4,132},{8,24},{12,140},{16,0},{20,148},{24,8},{28,156},{32... | collective-permute-start | bytes 786440 | tf_op jit(solution)/shard_map/ppermute | solution.py:30
  333.8 9.3 %collective-permute-start.32 = (f32[256,128]{1,0:T(8,128)S(1)}, f32[256,128]{1,0:T(8,128)S(1)}, u32[]{:S(2)}, u32[]{:S(2)}) collective-permute-start(f32[256,128]{1,0:T(8,128)S(1)} %dynamic-slice_bitcast_fusion.4), channel_id=1, source_target_pairs={{0,128},{4,20},{8,136},{12,28},{16,144},{20,4},{24,152},{28,12},{3... | collective-permute-start | bytes 393224 | tf_op jit(solution)/shard_map/ppermute | solution.py:30
  339.8 10.1 %collective-permute-start.35 = (f32[256,128]{1,0:T(8,128)S(1)}, f32[256,128]{1,0:T(8,128)S(1)}, u32[]{:S(2)}, u32[]{:S(2)}) collective-permute-start(f32[256,128]{1,0:T(8,128)S(1)} %convolution_multiply_fusion.2), channel_id=1, source_target_pairs={{0,1},{1,0},{2,3},{3,2},{4,5},{5,4},{6,7},{7,6},{8,9},{9,8},{10,11... | collective-permute-start | bytes 393224 | tf_op jit(solution)/shard_map/ppermute | solution.py:17
  343.1 12.0 %collective-permute-start.33 = (f32[128,128]{1,0:T(8,128)S(1)}, f32[128,128]{1,0:T(8,128)S(1)}, u32[]{:S(2)}, u32[]{:S(2)}) collective-permute-start(f32[128,128]{1,0:T(8,128)S(1)} %dynamic-slice_bitcast_fusion.5), channel_id=1, source_target_pairs={{0,32},{4,260},{8,40},{12,268},{16,48},{20,276},{24,56},{28,284},{... | collective-permute-start | bytes 196616 | tf_op jit(solution)/shard_map/ppermute | solution.py:30
  349.9 13.2 %collective-permute-start.36 = (f32[256,128]{1,0:T(8,128)S(1)}, f32[256,128]{1,0:T(8,128)S(1)}, u32[]{:S(2)}, u32[]{:S(2)}) collective-permute-start(f32[256,128]{1,0:T(8,128)S(1)} %add.234), channel_id=1, source_target_pairs={{0,2},{1,3},{2,0},{3,1},{4,6},{5,7},{6,4},{7,5},{8,10},{9,11},{10,... | collective-permute-start | bytes 393224 | tf_op jit(solution)/shard_map/ppermute | solution.py:17
  355.1 9.8 %collective-permute-start.34 = (f32[64,128]{1,0:T(8,128)S(1)}, f32[64,128]{1,0:T(8,128)S(1)}, u32[]{:S(2)}, u32[]{:S(2)}) collective-permute-start(f32[64,128]{1,0:T(8,128)S(1)} %dynamic-slice_bitcast_fusion.6), channel_id=1, source_target_pairs={{0,256},{4,36},{8,264},{12,44},{16,272},{20,52},{24,280},{28,60},{... | collective-permute-start | bytes 98312 | tf_op jit(solution)/shard_map/ppermute | solution.py:30
  (9 other events, 182.5 us)

commit v8 on v7

--- a/solution.py
+++ b/solution.py
@@ -129,13 +129,15 @@
     )
     student_local = student_local.reshape(rows_here)
     total_local = total_local.reshape(rows_here)
-    every = lax.all_gather(
-        jnp.stack([teacher_local, student_local, total_local]), "proto", axis=0, tiled=False
-    )
-    stats = every[0]
-    for j in range(1, every.shape[0]):
-        stats = combine_stats(stats, every[j])
-    teacher_top, student_top, total = stats[0], stats[1], stats[2]
+    teacher_top = lax.pmax(teacher_local, "proto")
+    student_pair = jnp.stack([student_local, total_local])
+    for k in range(bits("proto")):
+        other = swap(student_pair, "proto", k)
+        top = jnp.maximum(student_pair[0], other[0])
+        student_pair = jnp.stack(
+            [top, student_pair[1] * jnp.exp(student_pair[0] - top) + other[1] * jnp.exp(other[0] - top)]
+        )
+    student_top, total = student_pair[0], student_pair[1]
     shift = jnp.exp((teacher_local - teacher_top) / teacher_temp)
     row_scale = jnp.ones((rows_here,), jnp.float32)
     col_scale = jnp.ones((base_local.shape[1],), jnp.float32)

time: 367 us -> 376 us (1.025)
  waiting for transfers between devices: 115 us -> 108 us
  other arithmetic: 36.7 us -> 43.5 us
  matrix products: 5.64 us -> 12 us
  starting transfers between devices: 165 us -> 171 us
    all_gather x1 -> x0, blocking collectives: 11.9 us -> none  [per_device(): lax.all_gather(jnp.stack([teacher_local, student_local, total_local]), 'p...]
    pmax x0 -> x1, blocking collectives: none -> 8.6 us  [per_device(): teacher_top = lax.pmax(teacher_local, 'proto')]
    ppermute x23 -> x25, waiting for transfers between devices: 51.9 us -> 44 us  [swap(): return lax.ppermute(x, axis, [(i, i ^ 1 << k) for i in range(n)])]
    ppermute x23 -> x25, starting transfers between devices: 101 us -> 107 us  [swap(): return lax.ppermute(x, axis, [(i, i ^ 1 << k) for i in range(n)])]
    dot_general x2, matrix products: 3.07 us -> 9.43 us  [contract_rows(): lax.dot_general(left, right, (((1,), (1,)), ((), ())), preferred_element_...]
  transfers between devices with their start and end apart: 37 -> 39, of which waited for: 33 -> 29; matrix products, arithmetic and copies ran while one was open for 1% -> 3% of each run, Pallas kernels for 0% -> 0%
where the time goes in v8:
time: 376 us; the launch traced here: 374 us
  starting transfers between devices  171 us (45%)
  waiting for transfers between devices  108 us (29%)
  other arithmetic  43.5 us (12%)
  blocking collectives  34 us (9%)
  matrix products  12 us (3%)
  local copies, waits for them, and re-layouts  3.9 us (1%)
    ppermute x25, starting transfers between devices, swap(): return lax.ppermute(x, axis, [(i, i ^ 1 << k) for i in range(n)])  107 us
    ppermute x14, waiting for transfers between devices, core_swap(): return lax.ppermute(x, axis, pairs)  64.1 us
    ppermute x14, starting transfers between devices, core_swap(): return lax.ppermute(x, axis, pairs)  63.9 us
    ppermute x25, waiting for transfers between devices, swap(): return lax.ppermute(x, axis, [(i, i ^ 1 << k) for i in range(n)])  44 us
    psum x3, blocking collectives, per_device(): row_scale = 1.0 / lax.psum(partial_rows, 'proto')  25.4 us
    reduce_sum x3, other arithmetic, per_device(): partial_cols = jnp.sum((row_scale * shift)[:, None] * base_local, axis=0)  15.4 us
    reduce_sum x3, other arithmetic, per_device(): partial_rows = shift * jnp.sum(base_local * col_scale[None, :], axis=1)  13 us
    dot_general x2, matrix products, contract_rows(): lax.dot_general(left, right, (((1,), (1,)), ((), ())), preferred_element_...  9.43 us
  transfers between devices with their start and end apart: 39, of which 29 were waited for; matrix products, arithmetic and copies ran while one was open for 3% of the time, Pallas kernels for 0%

profile of v8, /device:TPU:6, one launch (start us, length us, event | category | flops | bytes accessed | tf_op | source)
XLA Modules:
  0.0 374.0 jit_solution(15862956461233249524)
XLA Ops:
  1.5 10.9 %collective-permute-start = (bf16[64,128]{1,0:T(8,128)(2,1)S(1)}, bf16[64,128]{1,0:T(8,128)(2,1)S(1)}, u32[]{:S(2)}, u32[]{:S(2)}) collective-permute-start(bf16[64,128]{1,0:T(8,128)(2,1)S(1)} %get-tuple-element.43), channel_id=1, source_target_pairs={{0,256},{4,36},{8,264},{12,44},{16,272},{20,52},{24,280},{28,60},{... | collective-permute-start | bytes 49160 | tf_op jit(solution)/shard_map/ppermute | solution.py:30
  14.1 7.7 %collective-permute-start.1 = (bf16[128,128]{1,0:T(8,128)(2,1)S(1)}, bf16[128,128]{1,0:T(8,128)(2,1)S(1)}, u32[]{:S(2)}, u32[]{:S(2)}) collective-permute-start(bf16[128,128]{1,0:T(8,128)(2,1)S(1)} %bitcast.134), channel_id=1, source_target_pairs={{0,32},{4,260},{8,40},{12,268},{16,48},{20,276},{24,56},{28,284},{... | collective-permute-start | bytes 98312 | tf_op jit(solution)/shard_map/ppermute | solution.py:30
  30.9 4.6 %collective-permute-start.3 = (bf16[512,128]{1,0:T(8,128)(2,1)S(1)}, bf16[512,128]{1,0:T(8,128)(2,1)S(1)}, u32[]{:S(2)}, u32[]{:S(2)}) collective-permute-start(bf16[512,128]{1,0:T(8,128)(2,1)S(1)} %bitcast.125), channel_id=1, source_target_pairs={{0,16},{4,132},{8,24},{12,140},{16,0},{20,148},{24,8},{28,156},{32... | collective-permute-start | bytes 393224 | tf_op jit(solution)/shard_map/ppermute | solution.py:30
  43.7 5.3 %collective-permute-done.4 = bf16[1024,128]{1,0:T(8,128)(2,1)S(1)} collective-permute-done((bf16[1024,128]{1,0:T(8,128)(2,1)S(1)}, bf16[1024,128]{1,0:T(8,128)(2,1)S(1)}, u32[]{:S(2)}, u32[]{:S(2)}) %collective-permute-start.4) | collective-permute-done | bytes 262176 | tf_op jit(solution)/shard_map/ppermute | solution.py:30
  51.3 8.8 %collective-permute-done.5 = bf16[2048,128]{1,0:T(8,128)(2,1)S(1)} collective-permute-done((bf16[2048,128]{1,0:T(8,128)(2,1)S(1)}, bf16[2048,128]{1,0:T(8,128)(2,1)S(1)}, u32[]{:S(2)}, u32[]{:S(2)}) %collective-permute-start.5) | collective-permute-done | bytes 524320 | tf_op jit(solution)/shard_map/ppermute | solution.py:30
  66.4 4.7 %fusion.8 = (f32[256]{0:T(256)S(1)}, f32[8192,256]{1,0:T(8,128)}) fusion(bf16[8192,128]{1,0:T(8,128)(2,1)S(1)} %bitcast.104, bf16[256,128]{1,0:T(8,128)(2,1)S(1)} %copy-done.1), kind=kOutput, calls=%fused_computation.64 | convolution fusion | flops 538967808 | bytes 10552320 | tf_op jit(solution)/shard_map/while/body/eval_jaxpr/dot_general | solution.py:90
  71.1 8.6 %pmax.7 = f32[256]{0:T(256)S(1)} all-reduce(f32[256]{0:T(256)S(1)} %get-tuple-element.62), channel_id=1, replica_groups=mesh['dp'=128,'proto'=4] {'proto'}, use_global_device_ids=true, to_apply=%region_3.4 | all-reduce | flops 256 | bytes 2048 | tf_op jit(solution)/shard_map/pmax | solution.py:132
  79.7 5.1 %multiply_reduce_fusion.5 = f32[8192]{0:T(1024)S(1)} fusion(f32[256]{0:T(256)S(1)} %multiply_exponential_fusion.1, f32[8192,256]{1,0:T(8,128)} %get-tuple-element.63, f32[256]{0:T(256)S(1)} %get-tuple-element.62), kind=kLoop, calls=%fused_computation.8 | loop fusion | flops 8380416 | bytes 8423424 | tf_op jit(solution)/shard_map/reduce_sum | solution.py:145
  100.7 6.5 %collective-permute-start.12 = (f32[8192]{0:T(1024)S(1)}, f32[8192]{0:T(1024)S(1)}, u32[]{:S(2)}, u32[]{:S(2)}) collective-permute-start(f32[8192]{0:T(1024)S(1)} %add.208), channel_id=1, source_target_pairs={{0,32},{4,36},{8,40},{12,44},{16,48},{20,52},{24,56},{28,60},{32,0... | collective-permute-start | bytes 98312 | tf_op jit(solution)/shard_map/ppermute | solution.py:17
  122.9 7.9 %collective-permute-start.15 = (f32[8192]{0:T(1024)S(1)}, f32[8192]{0:T(1024)S(1)}, u32[]{:S(2)}, u32[]{:S(2)}) collective-permute-start(f32[8192]{0:T(1024)S(1)} %add.211), channel_id=1, source_target_pairs={{0,256},{4,260},{8,264},{12,268},{16,272},{20,276},{24,280},{28,28... | collective-permute-start | bytes 98312 | tf_op jit(solution)/shard_map/ppermute | solution.py:17
  137.1 10.0 %psum.21 = f32[256]{0:T(256)S(1)} all-reduce(f32[256]{0:T(256)S(1)} %mul.145), channel_id=1, replica_groups=mesh['dp'=128,'proto'=4] {'proto'}, use_global_device_ids=true, to_apply=%region_6.7 | all-reduce | flops 256 | bytes 2048 | tf_op jit(solution)/shard_map/psum | solution.py:148
  147.1 5.1 %multiply_reduce_fusion.3 = f32[8192]{0:T(1024)S(1)} fusion(f32[256]{0:T(256)S(1)} %divide_multiply_fusion.2, f32[8192,256]{1,0:T(8,128)} %get-tuple-element.63, f32[256]{0:T(256)S(1)} %get-tuple-element.62), kind=kLoop, calls=%fused_computation.6 | loop fusion | flops 8380416 | bytes 8423424 | tf_op jit(solution)/shard_map/reduce_sum | solution.py:145
  168.3 6.7 %collective-permute-start.19 = (f32[8192]{0:T(1024)S(1)}, f32[8192]{0:T(1024)S(1)}, u32[]{:S(2)}, u32[]{:S(2)}) collective-permute-start(f32[8192]{0:T(1024)S(1)} %add.215), channel_id=1, source_target_pairs={{0,32},{4,36},{8,40},{12,44},{16,48},{20,52},{24,56},{28,60},{32,0... | collective-permute-start | bytes 98312 | tf_op jit(solution)/shard_map/ppermute | solution.py:17
  183.8 4.7 %collective-permute-start.21 = (f32[8192]{0:T(1024)S(1)}, f32[8192]{0:T(1024)S(1)}, u32[]{:S(2)}, u32[]{:S(2)}) collective-permute-start(f32[8192]{0:T(1024)S(1)} %add.217), channel_id=1, source_target_pairs={{0,128},{4,132},{8,136},{12,140},{16,144},{20,148},{24,152},{28,15... | collective-permute-start | bytes 98312 | tf_op jit(solution)/shard_map/ppermute | solution.py:17
  190.5 8.0 %collective-permute-start.22 = (f32[8192]{0:T(1024)S(1)}, f32[8192]{0:T(1024)S(1)}, u32[]{:S(2)}, u32[]{:S(2)}) collective-permute-start(f32[8192]{0:T(1024)S(1)} %add.218), channel_id=1, source_target_pairs={{0,256},{4,260},{8,264},{12,268},{16,272},{20,276},{24,280},{28,28... | collective-permute-start | bytes 98312 | tf_op jit(solution)/shard_map/ppermute | solution.py:17
  204.7 7.9 %psum.22 = f32[256]{0:T(256)S(1)} all-reduce(f32[256]{0:T(256)S(1)} %mul.151), channel_id=1, replica_groups=mesh['dp'=128,'proto'=4] {'proto'}, use_global_device_ids=true, to_apply=%region_9.10 | all-reduce | flops 256 | bytes 2048 | tf_op jit(solution)/shard_map/psum | solution.py:148
  212.6 5.1 %multiply_reduce_fusion.1 = f32[8192]{0:T(1024)S(1)} fusion(f32[256]{0:T(256)S(1)} %divide_multiply_fusion.1, f32[8192,256]{1,0:T(8,128)} %get-tuple-element.63, f32[256]{0:T(256)S(1)} %get-tuple-element.62), kind=kLoop, calls=%fused_computation.4 | loop fusion | flops 8380416 | bytes 8423424 | tf_op jit(solution)/shard_map/reduce_sum | solution.py:145
  219.7 4.7 %fusion.9 = (f32[256]{0:T(256)S(1)}, f32[8192,256]{1,0:T(8,128)}) fusion(bf16[8192,128]{1,0:T(8,128)(2,1)S(1)} %bitcast.105, bf16[256,128]{1,0:T(8,128)(2,1)S(1)} %copy-done), kind=kOutput, calls=%fused_computation.65 | convolution fusion | flops 541064960 | bytes 10552320 | tf_op jit(solution)/shard_map/while/body/eval_jaxpr/dot_general | solution.py:90
  231.4 4.7 %collective-permute-start.25 = (f32[8192]{0:T(1024)S(1)}, f32[8192]{0:T(1024)S(1)}, u32[]{:S(2)}, u32[]{:S(2)}) collective-permute-start(f32[8192]{0:T(1024)S(1)} %add.221), channel_id=1, source_target_pairs={{0,16},{4,20},{8,24},{12,28},{16,0},{20,4},{24,8},{28,12},{32,48},... | collective-permute-start | bytes 98312 | tf_op jit(solution)/shard_map/ppermute | solution.py:17
  239.4 6.0 %collective-permute-start.26 = (f32[8192]{0:T(1024)S(1)}, f32[8192]{0:T(1024)S(1)}, u32[]{:S(2)}, u32[]{:S(2)}) collective-permute-start(f32[8192]{0:T(1024)S(1)} %add.222), channel_id=1, source_target_pairs={{0,32},{4,36},{8,40},{12,44},{16,48},{20,52},{24,56},{28,60},{32,0... | collective-permute-start | bytes 98312 | tf_op jit(solution)/shard_map/ppermute | solution.py:17
  252.7 5.2 %collective-permute-start.8 = (f32[2,256]{1,0:T(2,128)S(1)}, f32[2,256]{1,0:T(2,128)S(1)}, u32[]{:S(2)}, u32[]{:S(2)}) collective-permute-start(f32[2,256]{1,0:T(2,128)S(1)} %pad_maximum_fusion.1), channel_id=1, source_target_pairs={{0,2},{1,3},{2,0},{3,1},{4,6},{5,7},{6,4},{7,5},{8,10},{9,11},{10,... | collective-permute-start | bytes 6152 | tf_op jit(solution)/shard_map/ppermute | solution.py:17
  257.9 4.8 %collective-permute-start.28 = (f32[8192]{0:T(1024)S(1)}, f32[8192]{0:T(1024)S(1)}, u32[]{:S(2)}, u32[]{:S(2)}) collective-permute-start(f32[8192]{0:T(1024)S(1)} %add.224), channel_id=1, source_target_pairs={{0,128},{4,132},{8,136},{12,140},{16,144},{20,148},{24,152},{28,15... | collective-permute-start | bytes 98312 | tf_op jit(solution)/shard_map/ppermute | solution.py:17
  264.8 8.0 %collective-permute-start.29 = (f32[8192]{0:T(1024)S(1)}, f32[8192]{0:T(1024)S(1)}, u32[]{:S(2)}, u32[]{:S(2)}) collective-permute-start(f32[8192]{0:T(1024)S(1)} %add.225), channel_id=1, source_target_pairs={{0,256},{4,260},{8,264},{12,268},{16,272},{20,276},{24,280},{28,28... | collective-permute-start | bytes 98312 | tf_op jit(solution)/shard_map/ppermute | solution.py:17
  279.1 7.5 %psum.23 = f32[256]{0:T(256)S(1)} all-reduce(f32[256]{0:T(256)S(1)} %mul.157), channel_id=1, replica_groups=mesh['dp'=128,'proto'=4] {'proto'}, use_global_device_ids=true, to_apply=%region_12.13 | all-reduce | flops 256 | bytes 2048 | tf_op jit(solution)/shard_map/psum | solution.py:148
  286.6 7.8 %subtract_convert_fusion = bf16[8192,256]{1,0:T(8,128)(2,1)S(1)} fusion(f32[8192,256]{1,0:T(8,128)} %get-tuple-element.65, f32[256]{0:T(256)S(1)} %divide_multiply_fusion, f32[8192]{0:T(1024)S(1)} %add_divide_fusion, f32[256]{0:T(256)S(1)} %add_divide_fusion.3, f32[256]{0:T(256)S(1)} %get-tuple-element.64, f32[8192,256]{1,0:T(8,128)} %get-tuple-element.63, ...), kind=kLoop, calls=%fused_computation.2 | loop fusion | flops 16777216 | bytes 21008384 | tf_op jit(solution)/shard_map/while/body/eval_jaxpr/convert_element_type | solution.py:157
  304.9 14.3 %collective-permute-done.31 = f32[2048,128]{1,0:T(8,128)S(1)} collective-permute-done((f32[2048,128]{1,0:T(8,128)S(1)}, f32[2048,128]{1,0:T(8,128)S(1)}, u32[]{:S(2)}, u32[]{:S(2)}) %collective-permute-start.31) | collective-permute-done | bytes 1048608 | tf_op jit(solution)/shard_map/ppermute | solution.py:30
  321.5 8.9 %collective-permute-done.32 = f32[1024,128]{1,0:T(8,128)S(1)} collective-permute-done((f32[1024,128]{1,0:T(8,128)S(1)}, f32[1024,128]{1,0:T(8,128)S(1)}, u32[]{:S(2)}, u32[]{:S(2)}) %collective-permute-start.32) | collective-permute-done | bytes 524320 | tf_op jit(solution)/shard_map/ppermute | solution.py:30
  334.1 8.4 %collective-permute-done.33 = f32[512,128]{1,0:T(8,128)S(1)} collective-permute-done((f32[512,128]{1,0:T(8,128)S(1)}, f32[512,128]{1,0:T(8,128)S(1)}, u32[]{:S(2)}, u32[]{:S(2)}) %collective-permute-start.33) | collective-permute-done | bytes 262176 | tf_op jit(solution)/shard_map/ppermute | solution.py:30
  342.5 4.7 %collective-permute-start.34 = (f32[256,128]{1,0:T(8,128)S(1)}, f32[256,128]{1,0:T(8,128)S(1)}, u32[]{:S(2)}, u32[]{:S(2)}) collective-permute-start(f32[256,128]{1,0:T(8,128)S(1)} %dynamic-slice_bitcast_fusion.4), channel_id=1, source_target_pairs={{0,128},{4,20},{8,136},{12,28},{16,144},{20,4},{24,152},{28,12},{3... | collective-permute-start | bytes 393224 | tf_op jit(solution)/shard_map/ppermute | solution.py:30
  352.1 6.2 %collective-permute-start.35 = (f32[128,128]{1,0:T(8,128)S(1)}, f32[128,128]{1,0:T(8,128)S(1)}, u32[]{:S(2)}, u32[]{:S(2)}) collective-permute-start(f32[128,128]{1,0:T(8,128)S(1)} %dynamic-slice_bitcast_fusion.5), channel_id=1, source_target_pairs={{0,32},{4,260},{8,40},{12,268},{16,48},{20,276},{24,56},{28,284},{... | collective-permute-start | bytes 196616 | tf_op jit(solution)/shard_map/ppermute | solution.py:30
  358.3 5.2 %collective-permute-start.38 = (f32[256,128]{1,0:T(8,128)S(1)}, f32[256,128]{1,0:T(8,128)S(1)}, u32[]{:S(2)}, u32[]{:S(2)}) collective-permute-start(f32[256,128]{1,0:T(8,128)S(1)} %add.234), channel_id=1, source_target_pairs={{0,2},{1,3},{2,0},{3,1},{4,6},{5,7},{6,4},{7,5},{8,10},{9,11},{10,... | collective-permute-start | bytes 393224 | tf_op jit(solution)/shard_map/ppermute | solution.py:17
  363.6 8.0 %collective-permute-start.36 = (f32[64,128]{1,0:T(8,128)S(1)}, f32[64,128]{1,0:T(8,128)S(1)}, u32[]{:S(2)}, u32[]{:S(2)}) collective-permute-start(f32[64,128]{1,0:T(8,128)S(1)} %dynamic-slice_bitcast_fusion.6), channel_id=1, source_target_pairs={{0,256},{4,36},{8,264},{12,44},{16,272},{20,52},{24,280},{28,60},{... | collective-permute-start | bytes 98312 | tf_op jit(solution)/shard_map/ppermute | solution.py:30
  (147 shorter events, 150.4 us)
Async XLA Ops:
  1.5 12.6 %collective-permute-start = (bf16[64,128]{1,0:T(8,128)(2,1)S(1)}, bf16[64,128]{1,0:T(8,128)(2,1)S(1)}, u32[]{:S(2)}, u32[]{:S(2)}) collective-permute-start(bf16[64,128]{1,0:T(8,128)(2,1)S(1)} %get-tuple-element.43), channel_id=1, source_target_pairs={{0,256},{4,36},{8,264},{12,44},{16,272},{20,52},{24,280},{28,60},{... | collective-permute-start | bytes 49160 | tf_op jit(solution)/shard_map/ppermute | solution.py:30
  14.1 9.7 %collective-permute-start.1 = (bf16[128,128]{1,0:T(8,128)(2,1)S(1)}, bf16[128,128]{1,0:T(8,128)(2,1)S(1)}, u32[]{:S(2)}, u32[]{:S(2)}) collective-permute-start(bf16[128,128]{1,0:T(8,128)(2,1)S(1)} %bitcast.134), channel_id=1, source_target_pairs={{0,32},{4,260},{8,40},{12,268},{16,48},{20,276},{24,56},{28,284},{... | collective-permute-start | bytes 98312 | tf_op jit(solution)/shard_map/ppermute | solution.py:30
  23.9 7.0 %collective-permute-start.2 = (bf16[256,128]{1,0:T(8,128)(2,1)S(1)}, bf16[256,128]{1,0:T(8,128)(2,1)S(1)}, u32[]{:S(2)}, u32[]{:S(2)}) collective-permute-start(bf16[256,128]{1,0:T(8,128)(2,1)S(1)} %bitcast.132), channel_id=1, source_target_pairs={{0,128},{4,20},{8,136},{12,28},{16,144},{20,4},{24,152},{28,12},{3... | collective-permute-start | bytes 196616 | tf_op jit(solution)/shard_map/ppermute | solution.py:30
  30.9 9.2 %collective-permute-start.3 = (bf16[512,128]{1,0:T(8,128)(2,1)S(1)}, bf16[512,128]{1,0:T(8,128)(2,1)S(1)}, u32[]{:S(2)}, u32[]{:S(2)}) collective-permute-start(bf16[512,128]{1,0:T(8,128)(2,1)S(1)} %bitcast.125), channel_id=1, source_target_pairs={{0,16},{4,132},{8,24},{12,140},{16,0},{20,148},{24,8},{28,156},{32... | collective-permute-start | bytes 393224 | tf_op jit(solution)/shard_map/ppermute | solution.py:30
  40.1 9.0 %collective-permute-start.4 = (bf16[1024,128]{1,0:T(8,128)(2,1)S(1)}, bf16[1024,128]{1,0:T(8,128)(2,1)S(1)}, u32[]{:S(2)}, u32[]{:S(2)}) collective-permute-start(bf16[1024,128]{1,0:T(8,128)(2,1)S(1)} %bitcast.119), channel_id=1, source_target_pairs={{0,64},{4,12},{8,72},{12,4},{16,80},{20,28},{24,88},{28,20},{32,96... | collective-permute-start | bytes 786440 | tf_op jit(solution)/shard_map/ppermute | solution.py:30
  49.1 11.1 %collective-permute-start.5 = (bf16[2048,128]{1,0:T(8,128)(2,1)S(1)}, bf16[2048,128]{1,0:T(8,128)(2,1)S(1)}, u32[]{:S(2)}, u32[]{:S(2)}) collective-permute-start(bf16[2048,128]{1,0:T(8,128)(2,1)S(1)} %bitcast.117), channel_id=1, source_target_pairs={{0,8},{4,68},{8,0},{12,76},{16,24},{20,84},{24,16},{28,92},{32,40}... | collective-permute-start | bytes 1572872 | tf_op jit(solution)/shard_map/ppermute | solution.py:30
  94.0 6.7 %collective-permute-start.11 = (f32[8192]{0:T(1024)S(1)}, f32[8192]{0:T(1024)S(1)}, u32[]{:S(2)}, u32[]{:S(2)}) collective-permute-start(f32[8192]{0:T(1024)S(1)} %add.207), channel_id=1, source_target_pairs={{0,16},{4,20},{8,24},{12,28},{16,0},{20,4},{24,8},{28,12},{32,48},... | collective-permute-start | bytes 98312 | tf_op jit(solution)/shard_map/ppermute | solution.py:17
  100.7 9.7 %collective-permute-start.12 = (f32[8192]{0:T(1024)S(1)}, f32[8192]{0:T(1024)S(1)}, u32[]{:S(2)}, u32[]{:S(2)}) collective-permute-start(f32[8192]{0:T(1024)S(1)} %add.208), channel_id=1, source_target_pairs={{0,32},{4,36},{8,40},{12,44},{16,48},{20,52},{24,56},{28,60},{32,0... | collective-permute-start | bytes 98312 | tf_op jit(solution)/shard_map/ppermute | solution.py:17
  116.2 6.7 %collective-permute-start.14 = (f32[8192]{0:T(1024)S(1)}, f32[8192]{0:T(1024)S(1)}, u32[]{:S(2)}, u32[]{:S(2)}) collective-permute-start(f32[8192]{0:T(1024)S(1)} %add.210), channel_id=1, source_target_pairs={{0,128},{4,132},{8,136},{12,140},{16,144},{20,148},{24,152},{28,15... | collective-permute-start | bytes 98312 | tf_op jit(solution)/shard_map/ppermute | solution.py:17
  122.9 9.8 %collective-permute-start.15 = (f32[8192]{0:T(1024)S(1)}, f32[8192]{0:T(1024)S(1)}, u32[]{:S(2)}, u32[]{:S(2)}) collective-permute-start(f32[8192]{0:T(1024)S(1)} %add.211), channel_id=1, source_target_pairs={{0,256},{4,260},{8,264},{12,268},{16,272},{20,276},{24,280},{28,28... | collective-permute-start | bytes 98312 | tf_op jit(solution)/shard_map/ppermute | solution.py:17
  161.4 6.9 %collective-permute-start.18 = (f32[8192]{0:T(1024)S(1)}, f32[8192]{0:T(1024)S(1)}, u32[]{:S(2)}, u32[]{:S(2)}) collective-permute-start(f32[8192]{0:T(1024)S(1)} %add.214), channel_id=1, source_target_pairs={{0,16},{4,20},{8,24},{12,28},{16,0},{20,4},{24,8},{28,12},{32,48},... | collective-permute-start | bytes 98312 | tf_op jit(solution)/shard_map/ppermute | solution.py:17
  168.3 9.7 %collective-permute-start.19 = (f32[8192]{0:T(1024)S(1)}, f32[8192]{0:T(1024)S(1)}, u32[]{:S(2)}, u32[]{:S(2)}) collective-permute-start(f32[8192]{0:T(1024)S(1)} %add.215), channel_id=1, source_target_pairs={{0,32},{4,36},{8,40},{12,44},{16,48},{20,52},{24,56},{28,60},{32,0... | collective-permute-start | bytes 98312 | tf_op jit(solution)/shard_map/ppermute | solution.py:17
  183.8 6.7 %collective-permute-start.21 = (f32[8192]{0:T(1024)S(1)}, f32[8192]{0:T(1024)S(1)}, u32[]{:S(2)}, u32[]{:S(2)}) collective-permute-start(f32[8192]{0:T(1024)S(1)} %add.217), channel_id=1, source_target_pairs={{0,128},{4,132},{8,136},{12,140},{16,144},{20,148},{24,152},{28,15... | collective-permute-start | bytes 98312 | tf_op jit(solution)/shard_map/ppermute | solution.py:17
  190.5 9.8 %collective-permute-start.22 = (f32[8192]{0:T(1024)S(1)}, f32[8192]{0:T(1024)S(1)}, u32[]{:S(2)}, u32[]{:S(2)}) collective-permute-start(f32[8192]{0:T(1024)S(1)} %add.218), channel_id=1, source_target_pairs={{0,256},{4,260},{8,264},{12,268},{16,272},{20,276},{24,280},{28,28... | collective-permute-start | bytes 98312 | tf_op jit(solution)/shard_map/ppermute | solution.py:17
  217.8 6.7 %collective-permute-start.23 = (f32[8192]{0:T(1024)S(1)}, f32[8192]{0:T(1024)S(1)}, u32[]{:S(2)}, u32[]{:S(2)}) collective-permute-start(f32[8192]{0:T(1024)S(1)} %multiply_reduce_fusion.1), channel_id=1, source_target_pairs={{0,4},{4,0},{8,12},{12,8},{16,20},{20,16},{24,28},{28,24},{32,36},... | collective-permute-start | bytes 98312 | tf_op jit(solution)/shard_map/ppermute | solution.py:17
  224.7 6.7 %collective-permute-start.24 = (f32[8192]{0:T(1024)S(1)}, f32[8192]{0:T(1024)S(1)}, u32[]{:S(2)}, u32[]{:S(2)}) collective-permute-start(f32[8192]{0:T(1024)S(1)} %add.220), channel_id=1, source_target_pairs={{0,8},{4,12},{8,0},{12,4},{16,24},{20,28},{24,16},{28,20},{32,40},... | collective-permute-start | bytes 98312 | tf_op jit(solution)/shard_map/ppermute | solution.py:17
  231.4 8.0 %collective-permute-start.25 = (f32[8192]{0:T(1024)S(1)}, f32[8192]{0:T(1024)S(1)}, u32[]{:S(2)}, u32[]{:S(2)}) collective-permute-start(f32[8192]{0:T(1024)S(1)} %add.221), channel_id=1, source_target_pairs={{0,16},{4,20},{8,24},{12,28},{16,0},{20,4},{24,8},{28,12},{32,48},... | collective-permute-start | bytes 98312 | tf_op jit(solution)/shard_map/ppermute | solution.py:17
  236.1 9.4 %collective-permute-start.7 = (f32[2,256]{1,0:T(2,128)S(1)}, f32[2,256]{1,0:T(2,128)S(1)}, u32[]{:S(2)}, u32[]{:S(2)}) collective-permute-start(f32[2,256]{1,0:T(2,128)S(1)} %pad_maximum_fusion), channel_id=1, source_target_pairs={{0,1},{1,0},{2,3},{3,2},{4,5},{5,4},{6,7},{7,6},{8,9},{9,8},{10,11... | collective-permute-start | bytes 6152 | tf_op jit(solution)/shard_map/ppermute | solution.py:17
  239.4 9.7 %collective-permute-start.26 = (f32[8192]{0:T(1024)S(1)}, f32[8192]{0:T(1024)S(1)}, u32[]{:S(2)}, u32[]{:S(2)}) collective-permute-start(f32[8192]{0:T(1024)S(1)} %add.222), channel_id=1, source_target_pairs={{0,32},{4,36},{8,40},{12,44},{16,48},{20,52},{24,56},{28,60},{32,0... | collective-permute-start | bytes 98312 | tf_op jit(solution)/shard_map/ppermute | solution.py:17
  249.2 8.7 %collective-permute-start.27 = (f32[8192]{0:T(1024)S(1)}, f32[8192]{0:T(1024)S(1)}, u32[]{:S(2)}, u32[]{:S(2)}) collective-permute-start(f32[8192]{0:T(1024)S(1)} %add.223), channel_id=1, source_target_pairs={{0,64},{4,68},{8,72},{12,76},{16,80},{20,84},{24,88},{28,92},{32,9... | collective-permute-start | bytes 98312 | tf_op jit(solution)/shard_map/ppermute | solution.py:17
  252.7 10.1 %collective-permute-start.8 = (f32[2,256]{1,0:T(2,128)S(1)}, f32[2,256]{1,0:T(2,128)S(1)}, u32[]{:S(2)}, u32[]{:S(2)}) collective-permute-start(f32[2,256]{1,0:T(2,128)S(1)} %pad_maximum_fusion.1), channel_id=1, source_target_pairs={{0,2},{1,3},{2,0},{3,1},{4,6},{5,7},{6,4},{7,5},{8,10},{9,11},{10,... | collective-permute-start | bytes 6152 | tf_op jit(solution)/shard_map/ppermute | solution.py:17
  257.9 6.9 %collective-permute-start.28 = (f32[8192]{0:T(1024)S(1)}, f32[8192]{0:T(1024)S(1)}, u32[]{:S(2)}, u32[]{:S(2)}) collective-permute-start(f32[8192]{0:T(1024)S(1)} %add.224), channel_id=1, source_target_pairs={{0,128},{4,132},{8,136},{12,140},{16,144},{20,148},{24,152},{28,15... | collective-permute-start | bytes 98312 | tf_op jit(solution)/shard_map/ppermute | solution.py:17
  264.8 9.9 %collective-permute-start.29 = (f32[8192]{0:T(1024)S(1)}, f32[8192]{0:T(1024)S(1)}, u32[]{:S(2)}, u32[]{:S(2)}) collective-permute-start(f32[8192]{0:T(1024)S(1)} %add.225), channel_id=1, source_target_pairs={{0,256},{4,260},{8,264},{12,268},{16,272},{20,276},{24,280},{28,28... | collective-permute-start | bytes 98312 | tf_op jit(solution)/shard_map/ppermute | solution.py:17
  295.9 6.1 %collective-permute-start.30 = (f32[4096,128]{1,0:T(8,128)S(1)}, f32[4096,128]{1,0:T(8,128)S(1)}, u32[]{:S(2)}, u32[]{:S(2)}) collective-permute-start(f32[4096,128]{1,0:T(8,128)S(1)} %get-tuple-element.44), channel_id=1, source_target_pairs={{0,4},{4,0},{8,12},{12,8},{16,20},{20,16},{24,28},{28,24},{32,36},... | collective-permute-start | bytes 6291464 | tf_op jit(solution)/shard_map/ppermute | solution.py:30
  302.5 16.7 %collective-permute-start.31 = (f32[2048,128]{1,0:T(8,128)S(1)}, f32[2048,128]{1,0:T(8,128)S(1)}, u32[]{:S(2)}, u32[]{:S(2)}) collective-permute-start(f32[2048,128]{1,0:T(8,128)S(1)} %dynamic-slice_bitcast_fusion.1), channel_id=1, source_target_pairs={{0,8},{4,68},{8,0},{12,76},{16,24},{20,84},{24,16},{28,92},{32,40}... | collective-permute-start | bytes 3145736 | tf_op jit(solution)/shard_map/ppermute | solution.py:30
  319.4 11.1 %collective-permute-start.32 = (f32[1024,128]{1,0:T(8,128)S(1)}, f32[1024,128]{1,0:T(8,128)S(1)}, u32[]{:S(2)}, u32[]{:S(2)}) collective-permute-start(f32[1024,128]{1,0:T(8,128)S(1)} %dynamic-slice_bitcast_fusion.2), channel_id=1, source_target_pairs={{0,64},{4,12},{8,72},{12,4},{16,80},{20,28},{24,88},{28,20},{32,96... | collective-permute-start | bytes 1572872 | tf_op jit(solution)/shard_map/ppermute | solution.py:30
  330.6 11.9 %collective-permute-start.33 = (f32[512,128]{1,0:T(8,128)S(1)}, f32[512,128]{1,0:T(8,128)S(1)}, u32[]{:S(2)}, u32[]{:S(2)}) collective-permute-start(f32[512,128]{1,0:T(8,128)S(1)} %dynamic-slice_bitcast_fusion.3), channel_id=1, source_target_pairs={{0,16},{4,132},{8,24},{12,140},{16,0},{20,148},{24,8},{28,156},{32... | collective-permute-start | bytes 786440 | tf_op jit(solution)/shard_map/ppermute | solution.py:30
  342.5 9.5 %collective-permute-start.34 = (f32[256,128]{1,0:T(8,128)S(1)}, f32[256,128]{1,0:T(8,128)S(1)}, u32[]{:S(2)}, u32[]{:S(2)}) collective-permute-start(f32[256,128]{1,0:T(8,128)S(1)} %dynamic-slice_bitcast_fusion.4), channel_id=1, source_target_pairs={{0,128},{4,20},{8,136},{12,28},{16,144},{20,4},{24,152},{28,12},{3... | collective-permute-start | bytes 393224 | tf_op jit(solution)/shard_map/ppermute | solution.py:30
  348.5 9.8 %collective-permute-start.37 = (f32[256,128]{1,0:T(8,128)S(1)}, f32[256,128]{1,0:T(8,128)S(1)}, u32[]{:S(2)}, u32[]{:S(2)}) collective-permute-start(f32[256,128]{1,0:T(8,128)S(1)} %convolution_multiply_fusion.2), channel_id=1, source_target_pairs={{0,1},{1,0},{2,3},{3,2},{4,5},{5,4},{6,7},{7,6},{8,9},{9,8},{10,11... | collective-permute-start | bytes 393224 | tf_op jit(solution)/shard_map/ppermute | solution.py:17
  352.1 11.4 %collective-permute-start.35 = (f32[128,128]{1,0:T(8,128)S(1)}, f32[128,128]{1,0:T(8,128)S(1)}, u32[]{:S(2)}, u32[]{:S(2)}) collective-permute-start(f32[128,128]{1,0:T(8,128)S(1)} %dynamic-slice_bitcast_fusion.5), channel_id=1, source_target_pairs={{0,32},{4,260},{8,40},{12,268},{16,48},{20,276},{24,56},{28,284},{... | collective-permute-start | bytes 196616 | tf_op jit(solution)/shard_map/ppermute | solution.py:30
  358.3 13.2 %collective-permute-start.38 = (f32[256,128]{1,0:T(8,128)S(1)}, f32[256,128]{1,0:T(8,128)S(1)}, u32[]{:S(2)}, u32[]{:S(2)}) collective-permute-start(f32[256,128]{1,0:T(8,128)S(1)} %add.234), channel_id=1, source_target_pairs={{0,2},{1,3},{2,0},{3,1},{4,6},{5,7},{6,4},{7,5},{8,10},{9,11},{10,... | collective-permute-start | bytes 393224 | tf_op jit(solution)/shard_map/ppermute | solution.py:17
  363.6 9.8 %collective-permute-start.36 = (f32[64,128]{1,0:T(8,128)S(1)}, f32[64,128]{1,0:T(8,128)S(1)}, u32[]{:S(2)}, u32[]{:S(2)}) collective-permute-start(f32[64,128]{1,0:T(8,128)S(1)} %dynamic-slice_bitcast_fusion.6), channel_id=1, source_target_pairs={{0,256},{4,36},{8,264},{12,44},{16,272},{20,52},{24,280},{28,60},{... | collective-permute-start | bytes 98312 | tf_op jit(solution)/shard_map/ppermute | solution.py:30
  (9 other events, 318.9 us)

commit v9 on v7

--- a/solution.py
+++ b/solution.py
@@ -122,9 +122,10 @@
     def student_stats(emb):
         logits = contract_rows(emb, copies) / student_temp
         top = jnp.max(logits, axis=1)
-        return (top, jnp.sum(jnp.exp(logits - top[:, None]), axis=1))
+        expo = jnp.exp(logits - top[:, None])
+        return (top, jnp.sum(expo, axis=1), expo)
 
-    student_local, total_local = lax.map(
+    student_local, total_local, student_expo = lax.map(
         student_stats, student_emb.reshape(count_blocks, block, width)
     )
     student_local = student_local.reshape(rows_here)
@@ -148,9 +149,8 @@
     student_factor = jnp.exp(student_local - student_top) / total
 
     def gradient_block(items):
-        emb, plan, factor, local_top, soft_factor = items
-        logits = contract_rows(emb, copies) / student_temp
-        probs = jnp.exp(logits - local_top[:, None]) * soft_factor[:, None]
+        expo, plan, factor, soft_factor = items
+        probs = expo * soft_factor[:, None]
         targets = factor[:, None] * plan * col_scale[None, :]
         grads = (probs - targets).astype(jnp.bfloat16)
         return (grads, jnp.dot(grads, copies, preferred_element_type=jnp.float32) / student_temp)
@@ -158,10 +158,9 @@
     grad_logits, student_terms = lax.map(
         gradient_block,
         (
-            student_emb.reshape(count_blocks, block, width),
+            student_expo.reshape(count_blocks, block, -1),
             base_local.reshape(count_blocks, block, -1),
             row_factor.reshape(count_blocks, block),
-            student_local.reshape(count_blocks, block),
             student_factor.reshape(count_blocks, block),
         ),
     )

time: 367 us -> 367 us (level)
  no operation moved by 1% of the time
where the time goes in v9:
time: 367 us; the launch traced here: 366 us
  starting transfers between devices  165 us (45%)
  waiting for transfers between devices  115 us (31%)
  blocking collectives  37.2 us (10%)
  other arithmetic  36.7 us (10%)
  matrix products  5.64 us (2%)
  local copies, waits for them, and re-layouts  3.9 us (1%)
    ppermute x23, starting transfers between devices, swap(): return lax.ppermute(x, axis, [(i, i ^ 1 << k) for i in range(n)])  101 us
    ppermute x14, starting transfers between devices, core_swap(): return lax.ppermute(x, axis, pairs)  64.7 us
    ppermute x14, waiting for transfers between devices, core_swap(): return lax.ppermute(x, axis, pairs)  63.4 us
    ppermute x23, waiting for transfers between devices, swap(): return lax.ppermute(x, axis, [(i, i ^ 1 << k) for i in range(n)])  51.9 us
    psum x3, blocking collectives, per_device(): row_scale = 1.0 / lax.psum(partial_rows, 'proto')  25.2 us
    reduce_sum x3, other arithmetic, per_device(): partial_rows = shift * jnp.sum(base_local * col_scale[None, :], axis=1)  13 us
    reduce_sum x3, other arithmetic, per_device(): partial_cols = jnp.sum((row_scale * shift)[:, None] * base_local, axis=0)  12 us
    all_gather x1, blocking collectives, per_device(): lax.all_gather(jnp.stack([teacher_local, student_local, total_local]), 'p...  11.9 us
  transfers between devices with their start and end apart: 37, of which 33 were waited for; matrix products, arithmetic and copies ran while one was open for 1% of the time, Pallas kernels for 0%

profile of v9, /device:TPU:6, one launch (start us, length us, event | category | flops | bytes accessed | tf_op | source)
XLA Modules:
  0.0 365.6 jit_solution(181701491798096131)
XLA Ops:
  1.5 10.9 %collective-permute-start = (bf16[64,128]{1,0:T(8,128)(2,1)S(1)}, bf16[64,128]{1,0:T(8,128)(2,1)S(1)}, u32[]{:S(2)}, u32[]{:S(2)}) collective-permute-start(bf16[64,128]{1,0:T(8,128)(2,1)S(1)} %get-tuple-element.45), channel_id=1, source_target_pairs={{0,256},{4,36},{8,264},{12,44},{16,272},{20,52},{24,280},{28,60},{... | collective-permute-start | bytes 49160 | tf_op jit(solution)/shard_map/ppermute | solution.py:30
  14.1 7.7 %collective-permute-start.1 = (bf16[128,128]{1,0:T(8,128)(2,1)S(1)}, bf16[128,128]{1,0:T(8,128)(2,1)S(1)}, u32[]{:S(2)}, u32[]{:S(2)}) collective-permute-start(bf16[128,128]{1,0:T(8,128)(2,1)S(1)} %bitcast.142), channel_id=1, source_target_pairs={{0,32},{4,260},{8,40},{12,268},{16,48},{20,276},{24,56},{28,284},{... | collective-permute-start | bytes 98312 | tf_op jit(solution)/shard_map/ppermute | solution.py:30
  23.9 4.4 %collective-permute-start.2 = (bf16[256,128]{1,0:T(8,128)(2,1)S(1)}, bf16[256,128]{1,0:T(8,128)(2,1)S(1)}, u32[]{:S(2)}, u32[]{:S(2)}) collective-permute-start(bf16[256,128]{1,0:T(8,128)(2,1)S(1)} %bitcast.140), channel_id=1, source_target_pairs={{0,128},{4,20},{8,136},{12,28},{16,144},{20,4},{24,152},{28,12},{3... | collective-permute-start | bytes 196616 | tf_op jit(solution)/shard_map/ppermute | solution.py:30
  30.9 4.6 %collective-permute-start.3 = (bf16[512,128]{1,0:T(8,128)(2,1)S(1)}, bf16[512,128]{1,0:T(8,128)(2,1)S(1)}, u32[]{:S(2)}, u32[]{:S(2)}) collective-permute-start(bf16[512,128]{1,0:T(8,128)(2,1)S(1)} %bitcast.133), channel_id=1, source_target_pairs={{0,16},{4,132},{8,24},{12,140},{16,0},{20,148},{24,8},{28,156},{32... | collective-permute-start | bytes 393224 | tf_op jit(solution)/shard_map/ppermute | solution.py:30
  35.6 4.4 %collective-permute-done.3 = bf16[512,128]{1,0:T(8,128)(2,1)S(1)} collective-permute-done((bf16[512,128]{1,0:T(8,128)(2,1)S(1)}, bf16[512,128]{1,0:T(8,128)(2,1)S(1)}, u32[]{:S(2)}, u32[]{:S(2)}) %collective-permute-start.3) | collective-permute-done | bytes 131104 | tf_op jit(solution)/shard_map/ppermute | solution.py:30
  43.7 5.3 %collective-permute-done.4 = bf16[1024,128]{1,0:T(8,128)(2,1)S(1)} collective-permute-done((bf16[1024,128]{1,0:T(8,128)(2,1)S(1)}, bf16[1024,128]{1,0:T(8,128)(2,1)S(1)}, u32[]{:S(2)}, u32[]{:S(2)}) %collective-permute-start.4) | collective-permute-done | bytes 262176 | tf_op jit(solution)/shard_map/ppermute | solution.py:30
  51.3 8.8 %collective-permute-done.5 = bf16[2048,128]{1,0:T(8,128)(2,1)S(1)} collective-permute-done((bf16[2048,128]{1,0:T(8,128)(2,1)S(1)}, bf16[2048,128]{1,0:T(8,128)(2,1)S(1)}, u32[]{:S(2)}, u32[]{:S(2)}) %collective-permute-start.5) | collective-permute-done | bytes 524320 | tf_op jit(solution)/shard_map/ppermute | solution.py:30
  70.7 11.9 %all-gather.1 = f32[4,3,256]{2,1,0:T(4,128)S(1)} all-gather(f32[1,3,256]{2,1,0:T(4,128)S(1)} %maximum_bitcast_fusion), channel_id=2, replica_groups=mesh['dp'=128,'proto'=4] {'proto'}, dimensions={0}, use_global_device_ids=true | all-gather | bytes 15360 | tf_op jit(solution)/shard_map/all_gather | solution.py:133
  100.6 7.3 %collective-permute-start.10 = (f32[8192]{0:T(1024)S(1)}, f32[8192]{0:T(1024)S(1)}, u32[]{:S(2)}, u32[]{:S(2)}) collective-permute-start(f32[8192]{0:T(1024)S(1)} %add.208), channel_id=1, source_target_pairs={{0,32},{4,36},{8,40},{12,44},{16,48},{20,52},{24,56},{28,60},{32,0... | collective-permute-start | bytes 98312 | tf_op jit(solution)/shard_map/ppermute | solution.py:17
  116.5 5.0 %collective-permute-start.12 = (f32[8192]{0:T(1024)S(1)}, f32[8192]{0:T(1024)S(1)}, u32[]{:S(2)}, u32[]{:S(2)}) collective-permute-start(f32[8192]{0:T(1024)S(1)} %add.210), channel_id=1, source_target_pairs={{0,128},{4,132},{8,136},{12,140},{16,144},{20,148},{24,152},{28,15... | collective-permute-start | bytes 98312 | tf_op jit(solution)/shard_map/ppermute | solution.py:17
  123.4 8.1 %collective-permute-start.13 = (f32[8192]{0:T(1024)S(1)}, f32[8192]{0:T(1024)S(1)}, u32[]{:S(2)}, u32[]{:S(2)}) collective-permute-start(f32[8192]{0:T(1024)S(1)} %add.211), channel_id=1, source_target_pairs={{0,256},{4,260},{8,264},{12,268},{16,272},{20,276},{24,280},{28,28... | collective-permute-start | bytes 98312 | tf_op jit(solution)/shard_map/ppermute | solution.py:17
  133.4 4.3 %multiply_reduce_fusion.4 = f32[256]{0:T(256)S(1)} fusion(f32[8192]{0:T(1024)S(1)} %add_divide_fusion.2, f32[8192,256]{1,0:T(8,128)} %copy-done.1, f32[256]{0:T(256)S(1)} %get-tuple-element.66), kind=kLoop, calls=%fused_computation.7 | loop fusion | flops 8388352 | bytes 8423424 | tf_op jit(solution)/shard_map/reduce_sum | solution.py:146
  137.8 7.5 %psum.21 = f32[256]{0:T(256)S(1)} all-reduce(f32[256]{0:T(256)S(1)} %mul.151), channel_id=1, replica_groups=mesh['dp'=128,'proto'=4] {'proto'}, use_global_device_ids=true, to_apply=%region_5.6 | all-reduce | flops 256 | bytes 2048 | tf_op jit(solution)/shard_map/psum | solution.py:147
  145.3 5.1 %multiply_reduce_fusion.3 = f32[8192]{0:T(1024)S(1)} fusion(f32[256]{0:T(256)S(1)} %divide_multiply_fusion.2, f32[8192,256]{1,0:T(8,128)} %copy-done.1, f32[256]{0:T(256)S(1)} %get-tuple-element.66), kind=kLoop, calls=%fused_computation.6 | loop fusion | flops 8380416 | bytes 8423424 | tf_op jit(solution)/shard_map/reduce_sum | solution.py:144
  166.5 6.7 %collective-permute-start.17 = (f32[8192]{0:T(1024)S(1)}, f32[8192]{0:T(1024)S(1)}, u32[]{:S(2)}, u32[]{:S(2)}) collective-permute-start(f32[8192]{0:T(1024)S(1)} %add.215), channel_id=1, source_target_pairs={{0,32},{4,36},{8,40},{12,44},{16,48},{20,52},{24,56},{28,60},{32,0... | collective-permute-start | bytes 98312 | tf_op jit(solution)/shard_map/ppermute | solution.py:17
  182.0 4.7 %collective-permute-start.19 = (f32[8192]{0:T(1024)S(1)}, f32[8192]{0:T(1024)S(1)}, u32[]{:S(2)}, u32[]{:S(2)}) collective-permute-start(f32[8192]{0:T(1024)S(1)} %add.217), channel_id=1, source_target_pairs={{0,128},{4,132},{8,136},{12,140},{16,144},{20,148},{24,152},{28,15... | collective-permute-start | bytes 98312 | tf_op jit(solution)/shard_map/ppermute | solution.py:17
  188.7 8.0 %collective-permute-start.20 = (f32[8192]{0:T(1024)S(1)}, f32[8192]{0:T(1024)S(1)}, u32[]{:S(2)}, u32[]{:S(2)}) collective-permute-start(f32[8192]{0:T(1024)S(1)} %add.218), channel_id=1, source_target_pairs={{0,256},{4,260},{8,264},{12,268},{16,272},{20,276},{24,280},{28,28... | collective-permute-start | bytes 98312 | tf_op jit(solution)/shard_map/ppermute | solution.py:17
  198.6 4.3 %multiply_reduce_fusion.2 = f32[256]{0:T(256)S(1)} fusion(f32[8192]{0:T(1024)S(1)} %add_divide_fusion.1, f32[8192,256]{1,0:T(8,128)} %copy-done.1, f32[256]{0:T(256)S(1)} %get-tuple-element.66), kind=kLoop, calls=%fused_computation.5 | loop fusion | flops 8388352 | bytes 8423424 | tf_op jit(solution)/shard_map/reduce_sum | solution.py:146
  202.9 10.0 %psum.22 = f32[256]{0:T(256)S(1)} all-reduce(f32[256]{0:T(256)S(1)} %mul.157), channel_id=1, replica_groups=mesh['dp'=128,'proto'=4] {'proto'}, use_global_device_ids=true, to_apply=%region_8.9 | all-reduce | flops 256 | bytes 2048 | tf_op jit(solution)/shard_map/psum | solution.py:147
  212.9 5.1 %multiply_reduce_fusion.1 = f32[8192]{0:T(1024)S(1)} fusion(f32[256]{0:T(256)S(1)} %divide_multiply_fusion.1, f32[8192,256]{1,0:T(8,128)} %copy-done.1, f32[256]{0:T(256)S(1)} %get-tuple-element.66), kind=kLoop, calls=%fused_computation.4 | loop fusion | flops 8380416 | bytes 8423424 | tf_op jit(solution)/shard_map/reduce_sum | solution.py:144
  233.9 6.8 %collective-permute-start.24 = (f32[8192]{0:T(1024)S(1)}, f32[8192]{0:T(1024)S(1)}, u32[]{:S(2)}, u32[]{:S(2)}) collective-permute-start(f32[8192]{0:T(1024)S(1)} %add.222), channel_id=1, source_target_pairs={{0,32},{4,36},{8,40},{12,44},{16,48},{20,52},{24,56},{28,60},{32,0... | collective-permute-start | bytes 98312 | tf_op jit(solution)/shard_map/ppermute | solution.py:17
  249.4 4.6 %collective-permute-start.26 = (f32[8192]{0:T(1024)S(1)}, f32[8192]{0:T(1024)S(1)}, u32[]{:S(2)}, u32[]{:S(2)}) collective-permute-start(f32[8192]{0:T(1024)S(1)} %add.224), channel_id=1, source_target_pairs={{0,128},{4,132},{8,136},{12,140},{16,144},{20,148},{24,152},{28,15... | collective-permute-start | bytes 98312 | tf_op jit(solution)/shard_map/ppermute | solution.py:17
  256.1 8.0 %collective-permute-start.27 = (f32[8192]{0:T(1024)S(1)}, f32[8192]{0:T(1024)S(1)}, u32[]{:S(2)}, u32[]{:S(2)}) collective-permute-start(f32[8192]{0:T(1024)S(1)} %add.225), channel_id=1, source_target_pairs={{0,256},{4,260},{8,264},{12,268},{16,272},{20,276},{24,280},{28,28... | collective-permute-start | bytes 98312 | tf_op jit(solution)/shard_map/ppermute | solution.py:17
  270.4 7.7 %psum.23 = f32[256]{0:T(256)S(1)} all-reduce(f32[256]{0:T(256)S(1)} %mul.163), channel_id=1, replica_groups=mesh['dp'=128,'proto'=4] {'proto'}, use_global_device_ids=true, to_apply=%region_11.12 | all-reduce | flops 256 | bytes 2048 | tf_op jit(solution)/shard_map/psum | solution.py:147
  278.1 7.8 %subtract_convert_fusion = bf16[8192,256]{1,0:T(8,128)(2,1)S(1)} fusion(f32[8192,256]{1,0:T(8,128)} %copy-done.2, f32[256]{0:T(256)S(1)} %divide_multiply_fusion, f32[8192]{0:T(1024)S(1)} %add_divide_fusion, f32[256]{0:T(256)S(1)} %add_divide_fusion.3, f32[256]{0:T(256)S(1)} %get-tuple-element.68, f32[8192,256]{1,0:T(8,128)} %copy-done.1, ...), kind=kLoop, calls=%fused_computation.2 | loop fusion | flops 16777216 | bytes 21008384 | tf_op jit(solution)/shard_map/while/body/eval_jaxpr/convert_element_type | solution.py:155
  296.2 14.6 %collective-permute-done.29 = f32[2048,128]{1,0:T(8,128)S(1)} collective-permute-done((f32[2048,128]{1,0:T(8,128)S(1)}, f32[2048,128]{1,0:T(8,128)S(1)}, u32[]{:S(2)}, u32[]{:S(2)}) %collective-permute-start.29) | collective-permute-done | bytes 1048608 | tf_op jit(solution)/shard_map/ppermute | solution.py:30
  314.3 7.7 %collective-permute-done.30 = f32[1024,128]{1,0:T(8,128)S(1)} collective-permute-done((f32[1024,128]{1,0:T(8,128)S(1)}, f32[1024,128]{1,0:T(8,128)S(1)}, u32[]{:S(2)}, u32[]{:S(2)}) %collective-permute-start.30) | collective-permute-done | bytes 524320 | tf_op jit(solution)/shard_map/ppermute | solution.py:30
  325.1 8.7 %collective-permute-done.31 = f32[512,128]{1,0:T(8,128)S(1)} collective-permute-done((f32[512,128]{1,0:T(8,128)S(1)}, f32[512,128]{1,0:T(8,128)S(1)}, u32[]{:S(2)}, u32[]{:S(2)}) %collective-permute-start.31) | collective-permute-done | bytes 262176 | tf_op jit(solution)/shard_map/ppermute | solution.py:30
  333.8 4.6 %collective-permute-start.32 = (f32[256,128]{1,0:T(8,128)S(1)}, f32[256,128]{1,0:T(8,128)S(1)}, u32[]{:S(2)}, u32[]{:S(2)}) collective-permute-start(f32[256,128]{1,0:T(8,128)S(1)} %dynamic-slice_bitcast_fusion.4), channel_id=1, source_target_pairs={{0,128},{4,20},{8,136},{12,28},{16,144},{20,4},{24,152},{28,12},{3... | collective-permute-start | bytes 393224 | tf_op jit(solution)/shard_map/ppermute | solution.py:30
  343.1 6.7 %collective-permute-start.33 = (f32[128,128]{1,0:T(8,128)S(1)}, f32[128,128]{1,0:T(8,128)S(1)}, u32[]{:S(2)}, u32[]{:S(2)}) collective-permute-start(f32[128,128]{1,0:T(8,128)S(1)} %dynamic-slice_bitcast_fusion.5), channel_id=1, source_target_pairs={{0,32},{4,260},{8,40},{12,268},{16,48},{20,276},{24,56},{28,284},{... | collective-permute-start | bytes 196616 | tf_op jit(solution)/shard_map/ppermute | solution.py:30
  349.9 5.2 %collective-permute-start.36 = (f32[256,128]{1,0:T(8,128)S(1)}, f32[256,128]{1,0:T(8,128)S(1)}, u32[]{:S(2)}, u32[]{:S(2)}) collective-permute-start(f32[256,128]{1,0:T(8,128)S(1)} %add.234), channel_id=1, source_target_pairs={{0,2},{1,3},{2,0},{3,1},{4,6},{5,7},{6,4},{7,5},{8,10},{9,11},{10,... | collective-permute-start | bytes 393224 | tf_op jit(solution)/shard_map/ppermute | solution.py:17
  355.1 8.0 %collective-permute-start.34 = (f32[64,128]{1,0:T(8,128)S(1)}, f32[64,128]{1,0:T(8,128)S(1)}, u32[]{:S(2)}, u32[]{:S(2)}) collective-permute-start(f32[64,128]{1,0:T(8,128)S(1)} %dynamic-slice_bitcast_fusion.6), channel_id=1, source_target_pairs={{0,256},{4,36},{8,264},{12,44},{16,272},{20,52},{24,280},{28,60},{... | collective-permute-start | bytes 98312 | tf_op jit(solution)/shard_map/ppermute | solution.py:30
  (145 shorter events, 139.3 us)
Async XLA Ops:
  1.5 12.6 %collective-permute-start = (bf16[64,128]{1,0:T(8,128)(2,1)S(1)}, bf16[64,128]{1,0:T(8,128)(2,1)S(1)}, u32[]{:S(2)}, u32[]{:S(2)}) collective-permute-start(bf16[64,128]{1,0:T(8,128)(2,1)S(1)} %get-tuple-element.45), channel_id=1, source_target_pairs={{0,256},{4,36},{8,264},{12,44},{16,272},{20,52},{24,280},{28,60},{... | collective-permute-start | bytes 49160 | tf_op jit(solution)/shard_map/ppermute | solution.py:30
  14.1 9.7 %collective-permute-start.1 = (bf16[128,128]{1,0:T(8,128)(2,1)S(1)}, bf16[128,128]{1,0:T(8,128)(2,1)S(1)}, u32[]{:S(2)}, u32[]{:S(2)}) collective-permute-start(bf16[128,128]{1,0:T(8,128)(2,1)S(1)} %bitcast.142), channel_id=1, source_target_pairs={{0,32},{4,260},{8,40},{12,268},{16,48},{20,276},{24,56},{28,284},{... | collective-permute-start | bytes 98312 | tf_op jit(solution)/shard_map/ppermute | solution.py:30
  23.9 7.0 %collective-permute-start.2 = (bf16[256,128]{1,0:T(8,128)(2,1)S(1)}, bf16[256,128]{1,0:T(8,128)(2,1)S(1)}, u32[]{:S(2)}, u32[]{:S(2)}) collective-permute-start(bf16[256,128]{1,0:T(8,128)(2,1)S(1)} %bitcast.140), channel_id=1, source_target_pairs={{0,128},{4,20},{8,136},{12,28},{16,144},{20,4},{24,152},{28,12},{3... | collective-permute-start | bytes 196616 | tf_op jit(solution)/shard_map/ppermute | solution.py:30
  30.9 9.2 %collective-permute-start.3 = (bf16[512,128]{1,0:T(8,128)(2,1)S(1)}, bf16[512,128]{1,0:T(8,128)(2,1)S(1)}, u32[]{:S(2)}, u32[]{:S(2)}) collective-permute-start(bf16[512,128]{1,0:T(8,128)(2,1)S(1)} %bitcast.133), channel_id=1, source_target_pairs={{0,16},{4,132},{8,24},{12,140},{16,0},{20,148},{24,8},{28,156},{32... | collective-permute-start | bytes 393224 | tf_op jit(solution)/shard_map/ppermute | solution.py:30
  40.1 9.0 %collective-permute-start.4 = (bf16[1024,128]{1,0:T(8,128)(2,1)S(1)}, bf16[1024,128]{1,0:T(8,128)(2,1)S(1)}, u32[]{:S(2)}, u32[]{:S(2)}) collective-permute-start(bf16[1024,128]{1,0:T(8,128)(2,1)S(1)} %bitcast.127), channel_id=1, source_target_pairs={{0,64},{4,12},{8,72},{12,4},{16,80},{20,28},{24,88},{28,20},{32,96... | collective-permute-start | bytes 786440 | tf_op jit(solution)/shard_map/ppermute | solution.py:30
  49.1 11.1 %collective-permute-start.5 = (bf16[2048,128]{1,0:T(8,128)(2,1)S(1)}, bf16[2048,128]{1,0:T(8,128)(2,1)S(1)}, u32[]{:S(2)}, u32[]{:S(2)}) collective-permute-start(bf16[2048,128]{1,0:T(8,128)(2,1)S(1)} %bitcast.125), channel_id=1, source_target_pairs={{0,8},{4,68},{8,0},{12,76},{16,24},{20,84},{24,16},{28,92},{32,40}... | collective-permute-start | bytes 1572872 | tf_op jit(solution)/shard_map/ppermute | solution.py:30
  87.8 5.8 %collective-permute-start.8 = (f32[8192]{0:T(1024)S(1)}, f32[8192]{0:T(1024)S(1)}, u32[]{:S(2)}, u32[]{:S(2)}) collective-permute-start(f32[8192]{0:T(1024)S(1)} %add.206), channel_id=1, source_target_pairs={{0,8},{4,12},{8,0},{12,4},{16,24},{20,28},{24,16},{28,20},{32,40},... | collective-permute-start | bytes 98312 | tf_op jit(solution)/shard_map/ppermute | solution.py:17
  93.6 7.0 %collective-permute-start.9 = (f32[8192]{0:T(1024)S(1)}, f32[8192]{0:T(1024)S(1)}, u32[]{:S(2)}, u32[]{:S(2)}) collective-permute-start(f32[8192]{0:T(1024)S(1)} %add.207), channel_id=1, source_target_pairs={{0,16},{4,20},{8,24},{12,28},{16,0},{20,4},{24,8},{28,12},{32,48},... | collective-permute-start | bytes 98312 | tf_op jit(solution)/shard_map/ppermute | solution.py:17
  100.6 10.0 %collective-permute-start.10 = (f32[8192]{0:T(1024)S(1)}, f32[8192]{0:T(1024)S(1)}, u32[]{:S(2)}, u32[]{:S(2)}) collective-permute-start(f32[8192]{0:T(1024)S(1)} %add.208), channel_id=1, source_target_pairs={{0,32},{4,36},{8,40},{12,44},{16,48},{20,52},{24,56},{28,60},{32,0... | collective-permute-start | bytes 98312 | tf_op jit(solution)/shard_map/ppermute | solution.py:17
  110.6 5.9 %collective-permute-start.11 = (f32[8192]{0:T(1024)S(1)}, f32[8192]{0:T(1024)S(1)}, u32[]{:S(2)}, u32[]{:S(2)}) collective-permute-start(f32[8192]{0:T(1024)S(1)} %add.209), channel_id=1, source_target_pairs={{0,64},{4,68},{8,72},{12,76},{16,80},{20,84},{24,88},{28,92},{32,9... | collective-permute-start | bytes 98312 | tf_op jit(solution)/shard_map/ppermute | solution.py:17
  116.5 6.9 %collective-permute-start.12 = (f32[8192]{0:T(1024)S(1)}, f32[8192]{0:T(1024)S(1)}, u32[]{:S(2)}, u32[]{:S(2)}) collective-permute-start(f32[8192]{0:T(1024)S(1)} %add.210), channel_id=1, source_target_pairs={{0,128},{4,132},{8,136},{12,140},{16,144},{20,148},{24,152},{28,15... | collective-permute-start | bytes 98312 | tf_op jit(solution)/shard_map/ppermute | solution.py:17
  123.4 10.0 %collective-permute-start.13 = (f32[8192]{0:T(1024)S(1)}, f32[8192]{0:T(1024)S(1)}, u32[]{:S(2)}, u32[]{:S(2)}) collective-permute-start(f32[8192]{0:T(1024)S(1)} %add.211), channel_id=1, source_target_pairs={{0,256},{4,260},{8,264},{12,268},{16,272},{20,276},{24,280},{28,28... | collective-permute-start | bytes 98312 | tf_op jit(solution)/shard_map/ppermute | solution.py:17
  153.7 5.8 %collective-permute-start.15 = (f32[8192]{0:T(1024)S(1)}, f32[8192]{0:T(1024)S(1)}, u32[]{:S(2)}, u32[]{:S(2)}) collective-permute-start(f32[8192]{0:T(1024)S(1)} %add.213), channel_id=1, source_target_pairs={{0,8},{4,12},{8,0},{12,4},{16,24},{20,28},{24,16},{28,20},{32,40},... | collective-permute-start | bytes 98312 | tf_op jit(solution)/shard_map/ppermute | solution.py:17
  159.6 6.9 %collective-permute-start.16 = (f32[8192]{0:T(1024)S(1)}, f32[8192]{0:T(1024)S(1)}, u32[]{:S(2)}, u32[]{:S(2)}) collective-permute-start(f32[8192]{0:T(1024)S(1)} %add.214), channel_id=1, source_target_pairs={{0,16},{4,20},{8,24},{12,28},{16,0},{20,4},{24,8},{28,12},{32,48},... | collective-permute-start | bytes 98312 | tf_op jit(solution)/shard_map/ppermute | solution.py:17
  166.5 9.7 %collective-permute-start.17 = (f32[8192]{0:T(1024)S(1)}, f32[8192]{0:T(1024)S(1)}, u32[]{:S(2)}, u32[]{:S(2)}) collective-permute-start(f32[8192]{0:T(1024)S(1)} %add.215), channel_id=1, source_target_pairs={{0,32},{4,36},{8,40},{12,44},{16,48},{20,52},{24,56},{28,60},{32,0... | collective-permute-start | bytes 98312 | tf_op jit(solution)/shard_map/ppermute | solution.py:17
  176.2 5.8 %collective-permute-start.18 = (f32[8192]{0:T(1024)S(1)}, f32[8192]{0:T(1024)S(1)}, u32[]{:S(2)}, u32[]{:S(2)}) collective-permute-start(f32[8192]{0:T(1024)S(1)} %add.216), channel_id=1, source_target_pairs={{0,64},{4,68},{8,72},{12,76},{16,80},{20,84},{24,88},{28,92},{32,9... | collective-permute-start | bytes 98312 | tf_op jit(solution)/shard_map/ppermute | solution.py:17
  182.0 6.7 %collective-permute-start.19 = (f32[8192]{0:T(1024)S(1)}, f32[8192]{0:T(1024)S(1)}, u32[]{:S(2)}, u32[]{:S(2)}) collective-permute-start(f32[8192]{0:T(1024)S(1)} %add.217), channel_id=1, source_target_pairs={{0,128},{4,132},{8,136},{12,140},{16,144},{20,148},{24,152},{28,15... | collective-permute-start | bytes 98312 | tf_op jit(solution)/shard_map/ppermute | solution.py:17
  188.7 9.8 %collective-permute-start.20 = (f32[8192]{0:T(1024)S(1)}, f32[8192]{0:T(1024)S(1)}, u32[]{:S(2)}, u32[]{:S(2)}) collective-permute-start(f32[8192]{0:T(1024)S(1)} %add.218), channel_id=1, source_target_pairs={{0,256},{4,260},{8,264},{12,268},{16,272},{20,276},{24,280},{28,28... | collective-permute-start | bytes 98312 | tf_op jit(solution)/shard_map/ppermute | solution.py:17
  221.4 5.8 %collective-permute-start.22 = (f32[8192]{0:T(1024)S(1)}, f32[8192]{0:T(1024)S(1)}, u32[]{:S(2)}, u32[]{:S(2)}) collective-permute-start(f32[8192]{0:T(1024)S(1)} %add.220), channel_id=1, source_target_pairs={{0,8},{4,12},{8,0},{12,4},{16,24},{20,28},{24,16},{28,20},{32,40},... | collective-permute-start | bytes 98312 | tf_op jit(solution)/shard_map/ppermute | solution.py:17
  227.2 6.7 %collective-permute-start.23 = (f32[8192]{0:T(1024)S(1)}, f32[8192]{0:T(1024)S(1)}, u32[]{:S(2)}, u32[]{:S(2)}) collective-permute-start(f32[8192]{0:T(1024)S(1)} %add.221), channel_id=1, source_target_pairs={{0,16},{4,20},{8,24},{12,28},{16,0},{20,4},{24,8},{28,12},{32,48},... | collective-permute-start | bytes 98312 | tf_op jit(solution)/shard_map/ppermute | solution.py:17
  233.9 9.7 %collective-permute-start.24 = (f32[8192]{0:T(1024)S(1)}, f32[8192]{0:T(1024)S(1)}, u32[]{:S(2)}, u32[]{:S(2)}) collective-permute-start(f32[8192]{0:T(1024)S(1)} %add.222), channel_id=1, source_target_pairs={{0,32},{4,36},{8,40},{12,44},{16,48},{20,52},{24,56},{28,60},{32,0... | collective-permute-start | bytes 98312 | tf_op jit(solution)/shard_map/ppermute | solution.py:17
  249.4 6.7 %collective-permute-start.26 = (f32[8192]{0:T(1024)S(1)}, f32[8192]{0:T(1024)S(1)}, u32[]{:S(2)}, u32[]{:S(2)}) collective-permute-start(f32[8192]{0:T(1024)S(1)} %add.224), channel_id=1, source_target_pairs={{0,128},{4,132},{8,136},{12,140},{16,144},{20,148},{24,152},{28,15... | collective-permute-start | bytes 98312 | tf_op jit(solution)/shard_map/ppermute | solution.py:17
  256.1 9.9 %collective-permute-start.27 = (f32[8192]{0:T(1024)S(1)}, f32[8192]{0:T(1024)S(1)}, u32[]{:S(2)}, u32[]{:S(2)}) collective-permute-start(f32[8192]{0:T(1024)S(1)} %add.225), channel_id=1, source_target_pairs={{0,256},{4,260},{8,264},{12,268},{16,272},{20,276},{24,280},{28,28... | collective-permute-start | bytes 98312 | tf_op jit(solution)/shard_map/ppermute | solution.py:17
  287.5 6.1 %collective-permute-start.28 = (f32[4096,128]{1,0:T(8,128)S(1)}, f32[4096,128]{1,0:T(8,128)S(1)}, u32[]{:S(2)}, u32[]{:S(2)}) collective-permute-start(f32[4096,128]{1,0:T(8,128)S(1)} %get-tuple-element.46), channel_id=1, source_target_pairs={{0,4},{4,0},{8,12},{12,8},{16,20},{20,16},{24,28},{28,24},{32,36},... | collective-permute-start | bytes 6291464 | tf_op jit(solution)/shard_map/ppermute | solution.py:30
  294.1 16.7 %collective-permute-start.29 = (f32[2048,128]{1,0:T(8,128)S(1)}, f32[2048,128]{1,0:T(8,128)S(1)}, u32[]{:S(2)}, u32[]{:S(2)}) collective-permute-start(f32[2048,128]{1,0:T(8,128)S(1)} %dynamic-slice_bitcast_fusion.1), channel_id=1, source_target_pairs={{0,8},{4,68},{8,0},{12,76},{16,24},{20,84},{24,16},{28,92},{32,40}... | collective-permute-start | bytes 3145736 | tf_op jit(solution)/shard_map/ppermute | solution.py:30
  310.9 11.1 %collective-permute-start.30 = (f32[1024,128]{1,0:T(8,128)S(1)}, f32[1024,128]{1,0:T(8,128)S(1)}, u32[]{:S(2)}, u32[]{:S(2)}) collective-permute-start(f32[1024,128]{1,0:T(8,128)S(1)} %dynamic-slice_bitcast_fusion.2), channel_id=1, source_target_pairs={{0,64},{4,12},{8,72},{12,4},{16,80},{20,28},{24,88},{28,20},{32,96... | collective-permute-start | bytes 1572872 | tf_op jit(solution)/shard_map/ppermute | solution.py:30
  322.1 11.6 %collective-permute-start.31 = (f32[512,128]{1,0:T(8,128)S(1)}, f32[512,128]{1,0:T(8,128)S(1)}, u32[]{:S(2)}, u32[]{:S(2)}) collective-permute-start(f32[512,128]{1,0:T(8,128)S(1)} %dynamic-slice_bitcast_fusion.3), channel_id=1, source_target_pairs={{0,16},{4,132},{8,24},{12,140},{16,0},{20,148},{24,8},{28,156},{32... | collective-permute-start | bytes 786440 | tf_op jit(solution)/shard_map/ppermute | solution.py:30
  333.8 9.3 %collective-permute-start.32 = (f32[256,128]{1,0:T(8,128)S(1)}, f32[256,128]{1,0:T(8,128)S(1)}, u32[]{:S(2)}, u32[]{:S(2)}) collective-permute-start(f32[256,128]{1,0:T(8,128)S(1)} %dynamic-slice_bitcast_fusion.4), channel_id=1, source_target_pairs={{0,128},{4,20},{8,136},{12,28},{16,144},{20,4},{24,152},{28,12},{3... | collective-permute-start | bytes 393224 | tf_op jit(solution)/shard_map/ppermute | solution.py:30
  339.8 10.1 %collective-permute-start.35 = (f32[256,128]{1,0:T(8,128)S(1)}, f32[256,128]{1,0:T(8,128)S(1)}, u32[]{:S(2)}, u32[]{:S(2)}) collective-permute-start(f32[256,128]{1,0:T(8,128)S(1)} %convolution_multiply_fusion.2), channel_id=1, source_target_pairs={{0,1},{1,0},{2,3},{3,2},{4,5},{5,4},{6,7},{7,6},{8,9},{9,8},{10,11... | collective-permute-start | bytes 393224 | tf_op jit(solution)/shard_map/ppermute | solution.py:17
  343.1 12.0 %collective-permute-start.33 = (f32[128,128]{1,0:T(8,128)S(1)}, f32[128,128]{1,0:T(8,128)S(1)}, u32[]{:S(2)}, u32[]{:S(2)}) collective-permute-start(f32[128,128]{1,0:T(8,128)S(1)} %dynamic-slice_bitcast_fusion.5), channel_id=1, source_target_pairs={{0,32},{4,260},{8,40},{12,268},{16,48},{20,276},{24,56},{28,284},{... | collective-permute-start | bytes 196616 | tf_op jit(solution)/shard_map/ppermute | solution.py:30
  349.9 13.2 %collective-permute-start.36 = (f32[256,128]{1,0:T(8,128)S(1)}, f32[256,128]{1,0:T(8,128)S(1)}, u32[]{:S(2)}, u32[]{:S(2)}) collective-permute-start(f32[256,128]{1,0:T(8,128)S(1)} %add.234), channel_id=1, source_target_pairs={{0,2},{1,3},{2,0},{3,1},{4,6},{5,7},{6,4},{7,5},{8,10},{9,11},{10,... | collective-permute-start | bytes 393224 | tf_op jit(solution)/shard_map/ppermute | solution.py:17
  355.1 9.8 %collective-permute-start.34 = (f32[64,128]{1,0:T(8,128)S(1)}, f32[64,128]{1,0:T(8,128)S(1)}, u32[]{:S(2)}, u32[]{:S(2)}) collective-permute-start(f32[64,128]{1,0:T(8,128)S(1)} %dynamic-slice_bitcast_fusion.6), channel_id=1, source_target_pairs={{0,256},{4,36},{8,264},{12,44},{16,272},{20,52},{24,280},{28,60},{... | collective-permute-start | bytes 98312 | tf_op jit(solution)/shard_map/ppermute | solution.py:30
  (9 other events, 182.5 us)
